TPU v7x, 256 devices: a whole 4x4x8 slice. The times are simulated.
256 devices in a mesh: ctx: 16 (over x, y), tp: 16 (over z, core).
Axes of the slice: x: 4, y: 4, z: 8, core: 2. Of those that a mesh axis runs over, the one named last changes fastest.
Arguments:
- tokens: bfloat16 [16384, 2560], P(('ctx', 'tp')), may hold values from -8 to 8
- norm1_gain: float32 [2560], replicated, may hold values from 0.1 to 1.9
- w_z: bfloat16 [2560, 5120], P(None, 'tp'), may hold values from -0.125 to 0.125
- w_x: bfloat16 [2560, 5120], P(None, 'tp'), may hold values from -0.125 to 0.125
- w_bc: bfloat16 [2560, 256], replicated, may hold values from -0.125 to 0.125
- w_dt: bfloat16 [2560, 80], P(None, 'tp'), may hold values from -1 to 1
- dt_bias: float32 [80], P('tp'), may hold values from -5.5 to -4
- a_log: float32 [80], P('tp'), may hold values from -12 to 1.4
- conv_x: float32 [4, 5120], P(None, 'tp'), may hold values from -3 to 3
- conv_bc: float32 [4, 256], replicated, may hold values from -3 to 3
- d_skip: float32 [80], P('tp'), may hold values from 0.1 to 1.9
- ssm_gain: float32 [5120], P('tp'), may hold values from 0.1 to 1.9
- w_out: bfloat16 [5120, 2560], P('tp'), may hold values from -0.078125 to 0.078125
- norm2_gain: float32 [2560], replicated, may hold values from 0.1 to 1.9
- w_gate: bfloat16 [2560, 5120], P(None, 'tp'), may hold values from -0.125 to 0.125
- w_up: bfloat16 [2560, 5120], P(None, 'tp'), may hold values from -0.125 to 0.125
- w_down: bfloat16 [5120, 2560], P('tp'), may hold values from -0.078125 to 0.078125
Outputs:
- layer_out: bfloat16 [16384, 2560], P(('ctx', 'tp'))
All inputs are finite; a program needn't handle non-finite values.
Results may differ from a plain program's by a relative error of at most 0.017.
Values may be sent and summed in bfloat16 or wider, within the bound.
No kernel may reach another device: no remote copies, remote signals or barrier semaphores. Data moves between devices by JAX's collectives and lax.ppermute only.
A program may use at most 128 MiB of HBM per device.

v0:
```python
import jax
import jax.numpy as jnp
from jax import lax
from jax.sharding import PartitionSpec as P

HEADS = 80
HEAD_DIM = 64
STATE_DIM = 128
BLOCK_LEN = 256


EPS = 1e-05


def from_behind(value, axis, steps):
    count = lax.axis_size(axis)
    first, last = (max(0, -steps), min(count, count - steps))
    return lax.ppermute(value, axis, [(source, source + steps) for source in range(first, last)])


def carried_in(shard, axis, join, neutral):
    place = lax.axis_index(axis)
    gathered = jax.tree.map(
        lambda a, kind: lax.all_gather(a.astype(kind), axis), shard, (jnp.bfloat16, jnp.bfloat16)
    )
    state = jax.tree.map(lambda a, e: jnp.zeros_like(a) + jnp.asarray(e, a.dtype), shard, neutral)

    def one(step, state):
        return join(
            state,
            jax.tree.map(
                lambda a, own: lax.dynamic_index_in_dim(a, step, 0, False).astype(own.dtype),
                gathered,
                shard,
            ),
        )

    return lax.fori_loop(0, place, one, state)


def rms_rows(values, gain):
    wide = values.astype(jnp.float32)
    return wide * lax.rsqrt(jnp.mean(wide * wide, axis=-1, keepdims=True) + EPS) * gain


def conv_four(rim, current, kernel):
    extended = jnp.concatenate([rim, current], axis=0).astype(jnp.float32)
    length = current.shape[0]
    result = kernel[0] * extended[0:length]
    for offset in range(1, 4):
        result = result + kernel[offset] * extended[offset : offset + length]
    return result


def combine_states(prior_part, next_part):
    return (
        prior_part[0] * next_part[0],
        next_part[1] + next_part[0][:, None, None] * prior_part[1],
    )


def carry_step(state, pieces):
    decay_now, fresh = pieces
    return (decay_now[:, None, None] * state + fresh, state)


def local(
    tokens,
    norm1_gain,
    w_z,
    w_x,
    w_bc,
    w_dt,
    dt_bias,
    a_log,
    conv_x,
    conv_bc,
    d_skip,
    ssm_gain,
    w_out,
    norm2_gain,
    w_gate,
    w_up,
    w_down,
):
    gathered = lax.all_gather(tokens, "tp", axis=0, tiled=True)
    normed = rms_rows(gathered, norm1_gain).astype(jnp.bfloat16)
    bc_rows = jnp.dot(normed, w_bc, preferred_element_type=jnp.float32).astype(jnp.bfloat16)
    group_len = gathered.shape[0]
    head_count = w_dt.shape[1]
    channels = w_x.shape[1]
    gate_z = jnp.dot(normed, w_z, preferred_element_type=jnp.float32)
    inner_rows = jnp.dot(normed, w_x, preferred_element_type=jnp.float32).astype(jnp.bfloat16)
    dt_raw = jnp.dot(normed, w_dt, preferred_element_type=jnp.float32)
    rim_inner, rim_bc = from_behind((inner_rows[-3:], bc_rows[-3:]), "ctx", 1)
    conv_inner = jax.nn.silu(conv_four(rim_inner, inner_rows, conv_x)).astype(jnp.bfloat16)
    conv_bcm = jax.nn.silu(conv_four(rim_bc, bc_rows, conv_bc)).astype(jnp.bfloat16)
    dt_step = jax.nn.softplus(dt_raw + dt_bias)
    log_decay = -dt_step * jnp.exp(a_log)
    block_count = group_len // BLOCK_LEN
    log_blocks = log_decay.reshape(block_count, BLOCK_LEN, head_count)
    step_blocks = dt_step.reshape(block_count, BLOCK_LEN, head_count)
    cum_decay = jnp.cumsum(log_blocks, axis=1)
    b_mat = conv_bcm[:, :STATE_DIM].reshape(block_count, BLOCK_LEN, STATE_DIM)
    c_mat = conv_bcm[:, STATE_DIM:].reshape(block_count, BLOCK_LEN, STATE_DIM)
    scores = jnp.einsum("btn,bsn->bts", c_mat, b_mat, preferred_element_type=jnp.float32)
    causal_mask = jnp.tril(jnp.ones((BLOCK_LEN, BLOCK_LEN), dtype=bool))[None, :, :, None]
    decay_diff = jnp.where(causal_mask, cum_decay[:, :, None, :] - cum_decay[:, None, :, :], 0.0)
    weights = jnp.where(causal_mask, jnp.exp(decay_diff), 0.0)
    inner_wide = conv_inner.astype(jnp.float32).reshape(
        block_count, BLOCK_LEN, head_count, HEAD_DIM
    )
    scaled = inner_wide * step_blocks[..., None]
    mixed_w = scores[..., None] * weights
    y_intra = jnp.einsum("btsh,bshp->bthp", mixed_w, scaled, precision=lax.Precision.HIGHEST)
    block_last = cum_decay[:, -1, :]
    tail_decay = jnp.exp(block_last[:, None, :] - cum_decay)
    b_wide = b_mat.astype(jnp.float32)
    c_wide = c_mat.astype(jnp.float32)
    block_states = jnp.einsum(
        "bsh,bshp,bsn->bhpn", tail_decay, scaled, b_wide, precision=lax.Precision.HIGHEST
    )
    block_decay = jnp.exp(block_last)
    zero_state = jnp.zeros((head_count, HEAD_DIM, STATE_DIM), jnp.float32)
    local_final, local_in = lax.scan(carry_step, zero_state, (block_decay, block_states))
    total_decay = jnp.prod(block_decay, axis=0)
    prior_decay = jnp.exp(jnp.cumsum(block_last, axis=0) - block_last)
    identity = (jnp.ones((head_count,), jnp.float32), zero_state)
    incoming_decay, incoming = carried_in(
        (total_decay, local_final), "ctx", combine_states, identity
    )
    state_in = local_in + prior_decay[:, :, None, None] * incoming[None]
    y_inter = jnp.exp(cum_decay)[..., None] * jnp.einsum(
        "btn,bhpn->bthp", c_wide, state_in, precision=lax.Precision.HIGHEST
    )
    ssm_out = y_intra + y_inter + d_skip[None, None, :, None] * inner_wide
    gated = ssm_out.reshape(group_len, channels) * jax.nn.silu(gate_z)
    squares = lax.psum(jnp.sum(gated * gated, axis=-1), "tp")
    scaled_out = (gated * lax.rsqrt(squares / (HEADS * HEAD_DIM) + EPS)[:, None] * ssm_gain).astype(
        jnp.bfloat16
    )
    piece = scaled_out
    mixer_own = lax.psum_scatter(
        jnp.dot(piece, w_out, preferred_element_type=jnp.float32).astype(jnp.bfloat16),
        "tp",
        scatter_dimension=0,
        tiled=True,
    ).astype(jnp.float32)
    resid = (tokens.astype(jnp.float32) + mixer_own).astype(jnp.bfloat16)
    normed_own = rms_rows(resid, norm2_gain).astype(jnp.bfloat16)
    mlp_in = lax.all_gather(normed_own, "tp", axis=0, tiled=True)
    mlp_gate = jnp.dot(mlp_in, w_gate, preferred_element_type=jnp.float32)
    mlp_up = jnp.dot(mlp_in, w_up, preferred_element_type=jnp.float32)
    hidden = (jax.nn.silu(mlp_gate) * mlp_up).astype(jnp.bfloat16)
    piece = hidden
    mlp_down = lax.psum_scatter(
        jnp.dot(piece, w_down, preferred_element_type=jnp.float32).astype(jnp.bfloat16),
        "tp",
        scatter_dimension=0,
        tiled=True,
    ).astype(jnp.float32)
    return (resid.astype(jnp.float32) + mlp_down).astype(jnp.bfloat16)


def solution(mesh):
    return jax.shard_map(
        local,
        mesh=mesh,
        in_specs=(
            P(("ctx", "tp"), None),
            P(),
            P(None, "tp"),
            P(None, "tp"),
            P(),
            P(None, "tp"),
            P("tp"),
            P("tp"),
            P(None, "tp"),
            P(),
            P("tp"),
            P("tp"),
            P("tp", None),
            P(),
            P(None, "tp"),
            P(None, "tp"),
            P("tp", None),
        ),
        out_specs=P(("ctx", "tp"), None),
        check_vma=False,
    )
```

profile of v0, /device:TPU:2, one launch (start us, length us, event | category | flops | bytes accessed | tf_op | source)
XLA Modules:
  0.0 395.9 jit_solution(1112012405852655867)
XLA Ops:
  9.7 45.6 %all-gather.6.cloned.1.call-done = bf16[1024,2560]{1,0:T(8,128)(2,1)} async-done(((bf16[64,2560]{1,0:T(8,128)(2,1)}), bf16[1024,2560]{1,0:T(8,128)(2,1)}) %all-gather.6.cloned.1.call-update) | async-done | bytes 5242896 | tf_op jit(solution)/shard_map/all_gather | solution.py:86
  55.3 3.7 fusion.1
  59.4 1.3 fusion.3
  60.7 1.5 negate_multiply_fusion
  63.0 6.0 %reduce-window.6 = f32[4,5,2,128]{3,2,1,0:T(2,128)S(1)} reduce-window(f32[4,5,2,128]{3,2,1,0:T(2,128)S(1)} %copy.46, f32[]{:T(128)} %constant.61.clone.1), window={size=1x1x1x128 pad=0_0x0_0x0_0x127_0}, to_apply=%region_1.2 | reduce-window | flops 650240 | bytes 40964 | tf_op jit(solution)/shard_map/reduce-window
  70.0 4.5 %convolution_convert_fusion.3 = bf16[1024,256]{1,0:T(8,128)(2,1)S(1)} fusion(bf16[1024,2560]{1,0:T(8,128)(2,1)} %copy-done.1, bf16[2560,256]{1,0:T(8,128)(2,1)} %param.25), kind=kOutput, calls=%fused_computation.44 | convolution fusion | flops 1342439424 | bytes 7077888 | tf_op jit(solution)/shard_map/dot_general | solution.py:88
  74.6 3.4 collective-permute-start.1
  78.0 1.9 convolution_convert_fusion.2
  80.0 3.4 collective-permute-start
  84.3 4.2 %collective-permute-done = bf16[3,320]{0,1:T(8,128)(2,1)S(1)} collective-permute-done((bf16[3,320]{0,1:T(8,128)(2,1)S(1)}, bf16[3,320]{0,1:T(8,128)(2,1)S(1)}, u32[]{:S(2)}, u32[]{:S(2)}) %collective-permute-start) | collective-permute-done | bytes 1952 | tf_op jit(solution)/shard_map/ppermute | solution.py:18
  88.8 2.4 fusion.40
  91.2 2.8 reshape.107
  94.0 2.2 fusion.24
  96.2 3.2 while.26
  101.7 31.4 %all-reduce = bf16[80]{0:T(256)(128)(2,1)S(1)} all-reduce(bf16[80]{0:T(256)(128)(2,1)S(1)} %dynamic-update-slice), channel_id=3, replica_groups=mesh['ctx'=16,'tp'=16] {'ctx'}, use_global_device_ids=true, to_apply=%add | all-reduce | flops 80 | bytes 320
  133.5 8.5 %fusion.17 = f32[4,256,5,64]{1,3,2,0:T(8,128)} fusion(f32[4,256,5]{1,2,0:T(8,128)S(1)} %copy.50, f32[4,256,256]{2,1,0:T(8,128)S(1)} %fusion.50, pred[256,256]{1,0:T(8,128)(4,1)S(1)} %iota_compare_fusion, f32[4,256,5,64]{1,0,3,2:T(4,128)} %reshape.107, f32[4,256,5]{1,2,0:T(8,128)S(1)} %bitcast.98), kind=kOutput, calls=%fused_computation.28 | convolution fusion | flops 1012203520 | bytes 3776512 | tf_op jit(solution)/shard_map/btsh,bshp->bthp/dot_general | solution.py:115
  142.0 2.3 all-gather.10.cloned.1.call-done
  144.3 4.2 %while.25 = (s32[]{:T(128)}, f32[5,64,128]{2,1,0:T(8,128)S(1)}, s32[]{:T(128)}, bf16[16,5,64,128]{3,2,1,0:T(8,128)(2,1)}, bf16[16,5]{1,0:T(8,128)(2,1)S(1)}, /*index=5*/s32[]{:T(128)}, s32[]{:T(128)}, s32[]{:T(128)}) while((s32[]{:T(128)}, f32[5,64,128]{2,1,0:T(8,128)S(1)}, s32[]{:T(128)}, bf16[16,5,64,128]{3,2,1,0:T(8,128)(2,1)}, ...), condition=%wide.region_8.9_spmd, body=%wide.region_7.8_spmd.sunk | while | flops 122890 | bytes 409785 | solution.py:38
  144.4 1.1 convert_add_fusion.3
  148.5 3.0 fusion.16
  152.7 1.6 copy-done.12
  154.3 3.1 multiply_reduce_fusion
  157.4 24.7 %psum.7 = f32[1024]{0:T(1024)S(1)} all-reduce(f32[1024]{0:T(1024)S(1)} %get-tuple-element.135), channel_id=1, replica_groups=mesh['ctx'=16,'tp'=16] {'tp'}, use_global_device_ids=true, to_apply=%region_10.11 | all-reduce | flops 1024 | bytes 8192 | tf_op jit(solution)/shard_map/psum | solution.py:138
  182.1 6.8 %convolution_convert_fusion.1 = bf16[1024,2560]{1,0:T(8,128)(2,1)} fusion(bf16[320,2560]{1,0:T(8,128)(2,1)S(1)} %copy-done, f32[320]{0:T(512)S(1)} %copy-done.13, f32[1024]{0:T(1024)S(1)} %add_rsqrt_fusion, f32[1024,320]{0,1:T(8,128)} %bitcast.94, f32[1024,320]{0,1:T(8,128)} %get-tuple-element.136), kind=kOutput, calls=%fused_computation.12 | convolution fusion | flops 1682964480 | bytes 9508096 | tf_op jit(solution)/shard_map/dot_general | solution.py:144
  189.1 74.3 %reduce-scatter.3.cloned.1.call-done = bf16[64,2560]{1,0:T(8,128)(2,1)} async-done(((bf16[1024,2560]{1,0:T(8,128)(2,1)}), bf16[64,2560]{1,0:T(8,128)(2,1)}) %reduce-scatter.3.cloned.1.call-update) | async-done | bytes 327696 | tf_op jit(solution)/shard_map/reduce_scatter | solution.py:143
  263.4 1.2 fusion.29
  264.6 1.8 fusion.31
  266.7 41.6 %all-gather.8.cloned.1.call-done = bf16[1024,2560]{1,0:T(8,128)(2,1)} async-done(((bf16[64,2560]{1,0:T(8,128)(2,1)}), bf16[1024,2560]{1,0:T(8,128)(2,1)}) %all-gather.8.cloned.1.call-update) | async-done | bytes 5242896 | tf_op jit(solution)/shard_map/all_gather | solution.py:151
  308.3 4.9 %fusion.51 = f32[1024,320]{0,1:T(8,128)S(1)} fusion(bf16[1024,2560]{1,0:T(8,128)(2,1)} %all-gather.8.cloned.1.call-done, bf16[2560,320]{0,1:T(8,128)(2,1)} %param.35), kind=kOutput, calls=%fused_computation.98 | convolution fusion | flops 1677721600 | bytes 8192000 | tf_op jit(solution)/shard_map/dot_general | solution.py:152
  313.2 10.4 %convolution_convert_fusion = bf16[1024,2560]{1,0:T(8,128)(2,1)} fusion(bf16[320,2560]{1,0:T(8,128)(2,1)} %param.37, bf16[1024,2560]{1,0:T(8,128)(2,1)} %all-gather.8.cloned.1.call-done, bf16[2560,320]{0,1:T(8,128)(2,1)} %param.36, f32[1024,320]{0,1:T(8,128)S(1)} %fusion.51), kind=kOutput, calls=%fused_computation.11 | convolution fusion | flops 3360030720 | bytes 15073280 | tf_op jit(solution)/shard_map/dot_general | solution.py:157
  323.7 63.9 %reduce-scatter.5.cloned.1.call-done = bf16[64,2560]{1,0:T(8,128)(2,1)} async-done(((bf16[1024,2560]{1,0:T(8,128)(2,1)}), bf16[64,2560]{1,0:T(8,128)(2,1)}) %reduce-scatter.5.cloned.1.call-update) | async-done | bytes 327696 | tf_op jit(solution)/shard_map/reduce_scatter | solution.py:156
  387.6 1.8 fusion.32
  (113 shorter events, 16.0 us)
Async XLA Ops:
  6.5 175.6 %copy-start = (bf16[320,2560]{1,0:T(8,128)(2,1)S(1)}, bf16[320,2560]{1,0:T(8,128)(2,1)}, u32[]{:S(2)}) copy-start(bf16[320,2560]{1,0:T(8,128)(2,1)} %param.33) | copy-start | bytes 4915204
  6.5 48.8 %all-gather.6.cloned.1.call-start = ((), (), s32[]{:S(2)}) async-start(), calls=%async_computation.2 | async-start | bytes 5570560 | tf_op jit(solution)/shard_map/all_gather | solution.py:86
  7.3 137.0 %all-gather.10.cloned.1.call-start = ((), (), s32[]{:S(2)}) async-start(), calls=%async_computation.6 | async-start | bytes 1392640 | tf_op jit(solution)/shard_map/all_gather | solution.py:24
  9.7 49.4 %copy-start.7 = (f32[2560]{0:T(1024)S(1)}, f32[2560]{0:T(1024)}, u32[]{:S(2)}) copy-start(f32[2560]{0:T(1024)} %param.22) | copy-start | bytes 30724
  55.3 4.0 %copy-start.2 = (bf16[1024,2560]{1,0:T(8,128)(2,1)S(1)}, bf16[1024,2560]{1,0:T(8,128)(2,1)}, u32[]{:S(2)}) copy-start(bf16[1024,2560]{1,0:T(8,128)(2,1)} %all-gather.6.cloned.1.call-done) | copy-start | bytes 15728644
  59.4 1.3 copy-start.6
  59.4 1.3 copy-start.9
  60.7 2.3 copy-start.1
  69.6 8.4 %slice-start = ((s8[5242880]{0:T(1024)(128)(4,1)}), s8[1048576]{0:T(1024)(128)(4,1)S(1)}, s32[]{:S(2)}) async-start(s8[5242880]{0:T(1024)(128)(4,1)} %bitcast.84), calls=%async_computation.7 | async-start | bytes 2097152
  70.0 8.0 %slice-start.1 = ((s8[5242880]{0:T(1024)(128)(4,1)}), s8[4194304]{0:T(1024)(128)(4,1)S(1)}, s32[]{:S(2)}) async-start(s8[5242880]{0:T(1024)(128)(4,1)} %bitcast.84), calls=%async_computation.8 | async-start | bytes 8388608
  70.0 8.0 %copy-start.11 = (bf16[2560,320]{0,1:T(8,128)(2,1)S(1)}, bf16[2560,320]{0,1:T(8,128)(2,1)}, u32[]{:S(2)}) copy-start(bf16[2560,320]{0,1:T(8,128)(2,1)} %param.24) | copy-start | bytes 4915204
  74.6 8.9 %collective-permute-start.1 = (bf16[3,256]{1,0:T(4,128)(2,1)S(1)}, bf16[3,256]{1,0:T(4,128)(2,1)S(1)}, u32[]{:S(2)}, u32[]{:S(2)}) collective-permute-start(bf16[3,256]{1,0:T(4,128)(2,1)S(1)} %slice.97), channel_id=1, source_target_pairs={{0,16},{16,32},{32,48},{48,64},{64,80},{80,96},{96,112},{112,128},... | collective-permute-start | bytes 4616 | tf_op jit(solution)/shard_map/ppermute | solution.py:18
  80.0 8.4 %collective-permute-start = (bf16[3,320]{0,1:T(8,128)(2,1)S(1)}, bf16[3,320]{0,1:T(8,128)(2,1)S(1)}, u32[]{:S(2)}, u32[]{:S(2)}) collective-permute-start(bf16[3,320]{0,1:T(8,128)(2,1)S(1)} %slice.92), channel_id=1, source_target_pairs={{0,16},{16,32},{32,48},{48,64},{64,80},{80,96},{96,112},{112,128},... | collective-permute-start | bytes 5768 | tf_op jit(solution)/shard_map/ppermute | solution.py:18
  96.2 4.0 %copy-start.14 = (u32[256]{0:T(256)S(1)}, u32[256]{0:T(256)}, u32[]{:S(2)}) copy-start(u32[256]{0:T(256)} %constant.76) | copy-start | bytes 3076
  100.1 163.3 %reduce-scatter.3.cloned.1.call-start = ((), (), s32[]{:S(2)}) async-start(), calls=%async_computation.3 | async-start | bytes 5570560 | tf_op jit(solution)/shard_map/reduce_scatter | solution.py:143
  142.0 6.5 %copy-start.10 = (f32[5]{0:T(128)S(1)}, f32[5]{0:T(128)}, u32[]{:S(2)}) copy-start(f32[5]{0:T(128)} %param.31) | copy-start | bytes 64
  144.3 8.4 %slice-start.2 = ((s8[5242880]{0:T(1024)(128)(4,1)}), s8[1048576]{0:T(1024)(128)(4,1)S(1)}, s32[]{:S(2)}) async-start(s8[5242880]{0:T(1024)(128)(4,1)} %bitcast.86), calls=%async_computation.9 | async-start | bytes 2097152
  148.5 4.2 %slice-start.3 = ((s8[5242880]{0:T(1024)(128)(4,1)}), s8[4194304]{0:T(1024)(128)(4,1)S(1)}, s32[]{:S(2)}) async-start(s8[5242880]{0:T(1024)(128)(4,1)} %bitcast.86), calls=%async_computation.10 | async-start | bytes 8388608
  152.4 1.9 copy-start.12
  152.7 4.7 %copy-start.5 = (f32[40,8,4,256]{3,1,2,0:T(8,128)}, f32[40,8,4,256]{3,1,2,0:T(8,128)S(1)}, u32[]{:S(2)}) copy-start(f32[40,8,4,256]{3,1,2,0:T(8,128)S(1)} %copy.60) | copy-start | bytes 3932164
  154.3 27.8 %copy-start.13 = (f32[320]{0:T(512)S(1)}, f32[320]{0:T(512)}, u32[]{:S(2)}) copy-start(f32[320]{0:T(512)} %param.32) | copy-start | bytes 3844
  189.0 74.4 %copy-start.3 = (bf16[64,2560]{1,0:T(8,128)(2,1)S(1)}, bf16[64,2560]{1,0:T(8,128)(2,1)}, u32[]{:S(2)}) copy-start(bf16[64,2560]{1,0:T(8,128)(2,1)} %param.21) | copy-start | bytes 983044
  189.0 75.6 %copy-start.8 = (f32[2560]{0:T(1024)S(1)}, f32[2560]{0:T(1024)}, u32[]{:S(2)}) copy-start(f32[2560]{0:T(1024)} %param.34) | copy-start | bytes 30724
  189.0 119.3 %all-gather.8.cloned.1.call-start = ((), (), s32[]{:S(2)}) async-start(), calls=%async_computation.4 | async-start | bytes 5570560 | tf_op jit(solution)/shard_map/all_gather | solution.py:151
  266.5 121.1 %reduce-scatter.5.cloned.1.call-start = ((), (), s32[]{:S(2)}) async-start(), calls=%async_computation.5 | async-start | bytes 5570560 | tf_op jit(solution)/shard_map/reduce_scatter | solution.py:156
  323.6 64.0 %copy-start.4 = (bf16[64,2560]{1,0:T(8,128)(2,1)S(1)}, bf16[64,2560]{1,0:T(8,128)(2,1)}, u32[]{:S(2)}) copy-start(bf16[64,2560]{1,0:T(8,128)(2,1)} %reduce-scatter.3.cloned.1.call-done) | copy-start | bytes 983044
Sparse Core Ops, SparseCore 0:
  9.2 46.1 all-gather.5
  100.2 44.0 all-gather.9
  189.1 74.2 reduce-scatter.2
  266.6 41.7 all-gather.7
  323.8 63.7 reduce-scatter.4
where the time goes:
time: 397 us; the launch traced here: 396 us
  waiting for transfers between devices  233 us (59%)
  blocking collectives  56.1 us (14%)
  matrix products  47.1 us (12%)
  other arithmetic  27.4 us (7%)
  between operations  14.2 us (4%)
  local copies, waits for them, and re-layouts  10.9 us (3%)
  starting transfers between devices  7.18 us (2%)
    reduce_scatter x1, waiting for transfers between devices, local(): lax.psum_scatter(jnp.dot(piece, w_out, preferred_element_type=jnp.float32...  74.3 us
    reduce_scatter x1, waiting for transfers between devices, local(): lax.psum_scatter(jnp.dot(piece, w_down, preferred_element_type=jnp.float3...  63.9 us
    all_gather x1, waiting for transfers between devices, local(): gathered = lax.all_gather(tokens, 'tp', axis=0, tiled=True)  45.6 us
    all_gather x1, waiting for transfers between devices, local(): mlp_in = lax.all_gather(normed_own, 'tp', axis=0, tiled=True)  41.6 us
    unnamed x1, blocking collectives  31.4 us
    psum x1, blocking collectives, local(): squares = lax.psum(jnp.sum(gated * gated, axis=-1), 'tp')  24.7 us
    dot_general x1, matrix products, local(): jnp.dot(piece, w_down, preferred_element_type=jnp.float32)  10.4 us
    dot_general x1, matrix products, local(): jnp.einsum('btsh,bshp->bthp', mixed_w, scaled, precision=lax.Precision.HI...  8.52 us
  transfers between devices with their start and end apart: 7, of which 6 were waited for; matrix products, arithmetic and copies ran while one was open for 4% of the time, Pallas kernels for 0%

commit v1 on v0

--- a/solution.py
+++ b/solution.py
@@ -18,24 +18,33 @@
     return lax.ppermute(value, axis, [(source, source + steps) for source in range(first, last)])
 
 
-def carried_in(shard, axis, join, neutral):
-    place = lax.axis_index(axis)
-    gathered = jax.tree.map(
-        lambda a, kind: lax.all_gather(a.astype(kind), axis), shard, (jnp.bfloat16, jnp.bfloat16)
-    )
-    state = jax.tree.map(lambda a, e: jnp.zeros_like(a) + jnp.asarray(e, a.dtype), shard, neutral)
+def shifted(value, axis, steps):
+    count = lax.axis_size(axis)
+    return lax.ppermute(value, axis, [(source, source + steps) for source in range(count - steps)])
 
-    def one(step, state):
-        return join(
-            state,
-            jax.tree.map(
-                lambda a, own: lax.dynamic_index_in_dim(a, step, 0, False).astype(own.dtype),
-                gathered,
-                shard,
-            ),
-        )
 
-    return lax.fori_loop(0, place, one, state)
+def join_packed(prior, later):
+    head_dim = later.shape[1] - 1
+    later_log = later[:, head_dim:, :]
+    total_log = prior[:, head_dim:, :] + later_log
+    state = later[:, :head_dim, :] + jnp.exp(later_log) * prior[:, :head_dim, :]
+    return jnp.concatenate([state, total_log], axis=1)
+
+
+def exclusive_prefix(packed, axis):
+    count = lax.axis_size(axis)
+    before = jnp.zeros_like(packed)
+    upto = packed
+    stride = 1
+    while stride < count:
+        parts = [shifted(upto, axis, k * stride) for k in (3, 2, 1) if k * stride < count]
+        older = parts[0]
+        for part in parts[1:]:
+            older = join_packed(older, part)
+        before = join_packed(older, before)
+        upto = join_packed(older, upto)
+        stride *= 4
+    return before
 
 
 def rms_rows(values, gain):
@@ -50,13 +59,6 @@
     for offset in range(1, 4):
         result = result + kernel[offset] * extended[offset : offset + length]
     return result
-
-
-def combine_states(prior_part, next_part):
-    return (
-        prior_part[0] * next_part[0],
-        next_part[1] + next_part[0][:, None, None] * prior_part[1],
-    )
 
 
 def carry_step(state, pieces):
@@ -92,7 +94,8 @@
     gate_z = jnp.dot(normed, w_z, preferred_element_type=jnp.float32)
     inner_rows = jnp.dot(normed, w_x, preferred_element_type=jnp.float32).astype(jnp.bfloat16)
     dt_raw = jnp.dot(normed, w_dt, preferred_element_type=jnp.float32)
-    rim_inner, rim_bc = from_behind((inner_rows[-3:], bc_rows[-3:]), "ctx", 1)
+    rims = from_behind(jnp.concatenate([inner_rows[-3:], bc_rows[-3:]], axis=1), "ctx", 1)
+    rim_inner, rim_bc = rims[:, :channels], rims[:, channels:]
     conv_inner = jax.nn.silu(conv_four(rim_inner, inner_rows, conv_x)).astype(jnp.bfloat16)
     conv_bcm = jax.nn.silu(conv_four(rim_bc, bc_rows, conv_bc)).astype(jnp.bfloat16)
     dt_step = jax.nn.softplus(dt_raw + dt_bias)
@@ -123,29 +126,32 @@
     block_decay = jnp.exp(block_last)
     zero_state = jnp.zeros((head_count, HEAD_DIM, STATE_DIM), jnp.float32)
     local_final, local_in = lax.scan(carry_step, zero_state, (block_decay, block_states))
-    total_decay = jnp.prod(block_decay, axis=0)
+    total_log = jnp.sum(block_last, axis=0)
     prior_decay = jnp.exp(jnp.cumsum(block_last, axis=0) - block_last)
-    identity = (jnp.ones((head_count,), jnp.float32), zero_state)
-    incoming_decay, incoming = carried_in(
-        (total_decay, local_final), "ctx", combine_states, identity
+    packed = jnp.concatenate(
+        [local_final, jnp.broadcast_to(total_log[:, None, None], (head_count, 1, STATE_DIM))], axis=1
     )
+    incoming = exclusive_prefix(packed, "ctx")[:, :HEAD_DIM, :]
     state_in = local_in + prior_decay[:, :, None, None] * incoming[None]
     y_inter = jnp.exp(cum_decay)[..., None] * jnp.einsum(
         "btn,bhpn->bthp", c_wide, state_in, precision=lax.Precision.HIGHEST
     )
     ssm_out = y_intra + y_inter + d_skip[None, None, :, None] * inner_wide
     gated = ssm_out.reshape(group_len, channels) * jax.nn.silu(gate_z)
-    squares = lax.psum(jnp.sum(gated * gated, axis=-1), "tp")
-    scaled_out = (gated * lax.rsqrt(squares / (HEADS * HEAD_DIM) + EPS)[:, None] * ssm_gain).astype(
-        jnp.bfloat16
+    squares = jnp.sum(gated * gated, axis=-1)
+    squares_hi = squares.astype(jnp.bfloat16)
+    squares_lo = (squares - squares_hi.astype(jnp.float32)).astype(jnp.bfloat16)
+    extra = jnp.zeros((group_len, 128), jnp.bfloat16)
+    extra = extra.at[:, 0].set(squares_hi).at[:, 1].set(squares_lo)
+    piece = (gated * ssm_gain).astype(jnp.bfloat16)
+    product = jnp.dot(piece, w_out, preferred_element_type=jnp.float32).astype(jnp.bfloat16)
+    reduced = lax.psum_scatter(
+        jnp.concatenate([product, extra], axis=1), "tp", scatter_dimension=0, tiled=True
     )
-    piece = scaled_out
-    mixer_own = lax.psum_scatter(
-        jnp.dot(piece, w_out, preferred_element_type=jnp.float32).astype(jnp.bfloat16),
-        "tp",
-        scatter_dimension=0,
-        tiled=True,
-    ).astype(jnp.float32)
+    width = w_out.shape[1]
+    squares_own = reduced[:, width].astype(jnp.float32) + reduced[:, width + 1].astype(jnp.float32)
+    scale = lax.rsqrt(squares_own / (HEADS * HEAD_DIM) + EPS)
+    mixer_own = reduced[:, :width].astype(jnp.float32) * scale[:, None]
     resid = (tokens.astype(jnp.float32) + mixer_own).astype(jnp.bfloat16)
     normed_own = rms_rows(resid, norm2_gain).astype(jnp.bfloat16)
     mlp_in = lax.all_gather(normed_own, "tp", axis=0, tiled=True)

time: 397 us -> 362 us (0.912)
  blocking collectives: 56.1 us -> 0 us
  local copies, waits for them, and re-layouts: 10.9 us -> 23 us
  starting transfers between devices: 7.18 us -> 18.9 us
  other arithmetic: 27.4 us -> 31.8 us
  waiting for transfers between devices: 233 us -> 229 us
    reduce_scatter x2 -> x0, waiting for transfers between devices: 138 us -> none  [the longest x1 74.3 us: local(): lax.psum_scatter(jnp.dot(piece, w_out, preferred_element_type=jnp.float32...]
    unnamed x5 -> x6, waiting for transfers between devices: 0.78 us -> 124 us
    unnamed x1 -> x0, blocking collectives: 31.4 us -> none
    psum x1 -> x0, blocking collectives: 24.7 us -> none  [local(): squares = lax.psum(jnp.sum(gated * gated, axis=-1), 'tp')]
    ppermute x0 -> x6, starting transfers between devices: none -> 15.2 us  [shifted(): lax.ppermute(value, axis, [(source, source + steps) for source in range(c...]
    ppermute x0 -> x6, waiting for transfers between devices: none -> 13.8 us  [shifted(): lax.ppermute(value, axis, [(source, source + steps) for source in range(c...]
    unnamed x42 -> x60, local copies, waits for them, and re-layouts: 3.88 us -> 7.89 us
    another operation x3 -> x6, other arithmetic: 6.14 us -> 9.58 us
  transfers between devices with their start and end apart: 7 -> 11, of which waited for: 6 -> 8; matrix products, arithmetic and copies ran while one was open for 4% -> 4% of each run, Pallas kernels for 0% -> 0%
where the time goes in v1:
time: 362 us; the launch traced here: 361 us
  waiting for transfers between devices  229 us (63%)
  matrix products  44.9 us (12%)
  other arithmetic  31.8 us (9%)
  local copies, waits for them, and re-layouts  23 us (6%)
  starting transfers between devices  18.9 us (5%)
  between operations  13.8 us (4%)
    unnamed x6, waiting for transfers between devices  124 us
    all_gather x1, waiting for transfers between devices, local(): gathered = lax.all_gather(tokens, 'tp', axis=0, tiled=True)  43.6 us
    all_gather x1, waiting for transfers between devices, local(): mlp_in = lax.all_gather(normed_own, 'tp', axis=0, tiled=True)  41.6 us
    ppermute x6, starting transfers between devices, shifted(): lax.ppermute(value, axis, [(source, source + steps) for source in range(c...  15.2 us
    ppermute x6, waiting for transfers between devices, shifted(): lax.ppermute(value, axis, [(source, source + steps) for source in range(c...  13.8 us
    dot_general x1, matrix products, local(): jnp.dot(piece, w_down, preferred_element_type=jnp.float32)  10.8 us
    another operation x6, other arithmetic  9.58 us
    unnamed x60, local copies, waits for them, and re-layouts  7.89 us
  transfers between devices with their start and end apart: 11, of which 8 were waited for; matrix products, arithmetic and copies ran while one was open for 4% of the time, Pallas kernels for 0%

profile of v1, /device:TPU:2, one launch (start us, length us, event | category | flops | bytes accessed | tf_op | source)
XLA Modules:
  0.0 361.1 jit_solution(14010606597867941173)
XLA Ops:
  11.7 43.6 %all-gather.3.cloned.1.call-done = bf16[1024,2560]{1,0:T(8,128)(2,1)} async-done(((bf16[64,2560]{1,0:T(8,128)(2,1)}), bf16[1024,2560]{1,0:T(8,128)(2,1)}) %all-gather.3.cloned.1.call-update) | async-done | bytes 5242896 | tf_op jit(solution)/shard_map/all_gather | solution.py:88
  55.3 3.7 %fusion.1 = f32[1024]{0:T(1024)S(1)} fusion(bf16[1024,2560]{1,0:T(8,128)(2,1)} %all-gather.3.cloned.1.call-done), kind=kLoop, calls=%fused_computation.6 | loop fusion | flops 7863296 | bytes 5246976 | tf_op jit(solution)/shard_map/reduce_sum | solution.py:52
  63.0 6.0 %reduce-window.6 = f32[4,5,2,128]{3,2,1,0:T(2,128)S(1)} reduce-window(f32[4,5,2,128]{3,2,1,0:T(2,128)S(1)} %copy.121, f32[]{:T(128)} %constant.92.clone.1), window={size=1x1x1x128 pad=0_0x0_0x0_0x127_0}, to_apply=%region_1.2 | reduce-window | flops 650240 | bytes 40964 | tf_op jit(solution)/shard_map/reduce-window
  70.1 4.6 %convolution_convert_fusion.3 = bf16[1024,256]{0,1:T(8,128)(2,1)S(1)} fusion(bf16[1024,2560]{1,0:T(8,128)(2,1)} %copy-done.1, bf16[2560,256]{1,0:T(8,128)(2,1)} %param.27), kind=kOutput, calls=%fused_computation.51 | convolution fusion | flops 1342439424 | bytes 7077888 | tf_op jit(solution)/shard_map/dot_general | solution.py:90
  74.9 1.9 convolution_convert_fusion.2
  76.9 3.4 collective-permute-start
  81.0 5.9 %collective-permute-done = bf16[3,576]{0,1:T(8,128)(2,1)S(1)} collective-permute-done((bf16[3,576]{0,1:T(8,128)(2,1)S(1)}, bf16[3,576]{0,1:T(8,128)(2,1)S(1)}, u32[]{:S(2)}, u32[]{:S(2)}) %collective-permute-start) | collective-permute-done | bytes 3488 | tf_op jit(solution)/shard_map/ppermute | solution.py:18
  90.4 2.4 fusion.39
  92.8 2.8 reshape.160
  95.6 2.2 fusion.28
  97.8 3.3 while.15
  101.2 2.5 collective-permute-start.3
  103.7 3.8 %collective-permute-start.2 = (f32[5,65,128]{2,1,0:T(8,128)S(1)}, f32[5,65,128]{2,1,0:T(8,128)S(1)}, u32[]{:S(2)}, u32[]{:S(2)}) collective-permute-start(f32[5,65,128]{2,1,0:T(8,128)S(1)} %pad_maximum_fusion.1), channel_id=1, source_target_pairs={{0,32},{16,48},{32,64},{48,80},{64,96},{80,112},{96,128},{112,144}... | collective-permute-start | bytes 499208 | tf_op jit(solution)/shard_map/ppermute | solution.py:23
  107.5 2.8 collective-permute-start.1
  110.7 3.1 collective-permute-done.2
  113.9 5.2 %collective-permute-done.1 = f32[5,65,128]{2,1,0:T(8,128)S(1)} collective-permute-done((f32[5,65,128]{2,1,0:T(8,128)S(1)}, f32[5,65,128]{2,1,0:T(8,128)S(1)}, u32[]{:S(2)}, u32[]{:S(2)}) %collective-permute-start.1) | collective-permute-done | bytes 166432 | tf_op jit(solution)/shard_map/ppermute | solution.py:23
  120.6 3.3 collective-permute-start.5
  123.9 7.1 %fusion.17 = f32[4,256,5,64]{1,3,2,0:T(8,128)} fusion(f32[4,256,5]{1,2,0:T(8,128)S(1)} %copy.125, f32[4,256,256]{2,1,0:T(8,128)S(1)} %fusion.43, pred[256,256]{1,0:T(8,128)(4,1)S(1)} %copy-done.9, f32[4,256,5,64]{1,0,3,2:T(4,128)S(1)} %copy-done.3, f32[4,256,5]{1,2,0:T(8,128)S(1)} %bitcast.102), kind=kOutput, calls=%fused_computation.30 | convolution fusion | flops 1012203520 | bytes 3776512 | tf_op jit(solution)/shard_map/btsh,bshp->bthp/dot_general | solution.py:118
  132.0 1.9 collective-permute-start.4
  134.7 5.4 %collective-permute-done.4 = f32[5,65,128]{2,1,0:T(8,128)S(1)} collective-permute-done((f32[5,65,128]{2,1,0:T(8,128)}, f32[5,65,128]{2,1,0:T(8,128)S(1)}, u32[]{:S(2)}, u32[]{:S(2)}) %collective-permute-start.4) | collective-permute-done | bytes 166432 | tf_op jit(solution)/shard_map/ppermute | solution.py:23
  141.4 2.7 fusion.16
  146.3 3.1 multiply_reduce_fusion
  149.7 2.1 fusion.42
  151.8 1.8 scatter.9
  153.6 4.8 %convolution_convert_fusion.1 = bf16[1024,2560]{1,0:T(8,128)(2,1)S(1)} fusion(bf16[320,2560]{1,0:T(8,128)(2,1)S(1)} %copy-done, f32[320]{0:T(512)S(1)} %copy-done.20, f32[1024,320]{0,1:T(8,128)S(1)} %bitcast.96, f32[1024,320]{0,1:T(8,128)} %get-tuple-element.118), kind=kOutput, calls=%fused_computation.10 | convolution fusion | flops 1682636800 | bytes 9504000 | tf_op jit(solution)/shard_map/dot_general | solution.py:147
  158.4 2.8 pad_maximum_fusion
  162.5 59.1 %reduce-scatter.7.cloned.1.call-done = bf16[64,2688]{1,0:T(8,128)(2,1)} async-done(((bf16[1024,2688]{1,0:T(8,128)(2,1)}), bf16[64,2688]{1,0:T(8,128)(2,1)}) %reduce-scatter.7.cloned.1.call-update) | async-done | bytes 344080
  227.9 41.6 %all-gather.5.cloned.1.call-done = bf16[1024,2560]{1,0:T(8,128)(2,1)} async-done(((bf16[64,2560]{1,0:T(8,128)(2,1)}), bf16[1024,2560]{1,0:T(8,128)(2,1)}) %all-gather.5.cloned.1.call-update) | async-done | bytes 5242896 | tf_op jit(solution)/shard_map/all_gather | solution.py:157
  269.5 5.9 %fusion.69 = f32[1024,320]{0,1:T(8,128)} fusion(bf16[1024,2560]{1,0:T(8,128)(2,1)} %all-gather.5.cloned.1.call-done, bf16[2560,320]{0,1:T(8,128)(2,1)} %param.37), kind=kOutput, calls=%fused_computation.136 | convolution fusion | flops 1677721600 | bytes 8192000 | tf_op jit(solution)/shard_map/dot_general | solution.py:158
  275.4 10.8 %convolution_convert_fusion = bf16[1024,2560]{1,0:T(8,128)(2,1)} fusion(bf16[320,2560]{1,0:T(8,128)(2,1)} %param.39, bf16[1024,2560]{1,0:T(8,128)(2,1)} %all-gather.5.cloned.1.call-done, bf16[2560,320]{0,1:T(8,128)(2,1)} %param.38, f32[1024,320]{0,1:T(8,128)} %fusion.69), kind=kOutput, calls=%fused_computation.9 | convolution fusion | flops 3360030720 | bytes 15073280 | tf_op jit(solution)/shard_map/dot_general | solution.py:163
  286.3 64.0 %reduce-scatter.9.cloned.1.call-done = bf16[64,2560]{1,0:T(8,128)(2,1)} async-done(((bf16[1024,2560]{1,0:T(8,128)(2,1)}), bf16[64,2560]{1,0:T(8,128)(2,1)}) %reduce-scatter.9.cloned.1.call-update) | async-done | bytes 327696
  352.5 2.0 copy.140
  (151 shorter events, 34.8 us)
Async XLA Ops:
  6.5 147.1 %copy-start = (bf16[320,2560]{1,0:T(8,128)(2,1)S(1)}, bf16[320,2560]{1,0:T(8,128)(2,1)}, u32[]{:S(2)}) copy-start(bf16[320,2560]{1,0:T(8,128)(2,1)} %param.35) | copy-start | bytes 4915204
  6.5 48.8 %all-gather.3.cloned.1.call-start = ((), (), s32[]{:S(2)}) async-start(), calls=%async_computation.2 | async-start | bytes 5570560 | tf_op jit(solution)/shard_map/all_gather | solution.py:88
  7.3 214.3 %reduce-scatter.7.cloned.1.call-start = ((), (), s32[]{:S(2)}) async-start(), calls=%async_computation.4 | async-start | bytes 5849088
  11.7 47.4 %copy-start.11 = (f32[2560]{0:T(1024)S(1)}, f32[2560]{0:T(1024)}, u32[]{:S(2)}) copy-start(f32[2560]{0:T(1024)} %param.24) | copy-start | bytes 30724
  55.3 4.0 %copy-start.2 = (bf16[1024,2560]{1,0:T(8,128)(2,1)S(1)}, bf16[1024,2560]{1,0:T(8,128)(2,1)}, u32[]{:S(2)}) copy-start(bf16[1024,2560]{1,0:T(8,128)(2,1)} %all-gather.3.cloned.1.call-done) | copy-start | bytes 15728644
  59.4 1.3 copy-start.16
  60.7 2.3 copy-start.1
  69.5 5.3 %slice-start = ((s8[5242880]{0:T(1024)(128)(4,1)}), s8[1048576]{0:T(1024)(128)(4,1)S(1)}, s32[]{:S(2)}) async-start(s8[5242880]{0:T(1024)(128)(4,1)} %bitcast.88), calls=%async_computation.6 | async-start | bytes 2097152
  69.8 11.2 %copy-start.14 = (f32[5]{0:T(128)}, f32[5]{0:T(128)S(1)}, u32[]{:S(2)}) copy-start(f32[5]{0:T(128)S(1)} %get-tuple-element.105) | copy-start | bytes 64
  70.1 4.7 %slice-start.1 = ((s8[5242880]{0:T(1024)(128)(4,1)}), s8[4194304]{0:T(1024)(128)(4,1)S(1)}, s32[]{:S(2)}) async-start(s8[5242880]{0:T(1024)(128)(4,1)} %bitcast.88), calls=%async_computation.7 | async-start | bytes 8388608
  70.1 4.7 %copy-start.18 = (bf16[2560,320]{0,1:T(8,128)(2,1)S(1)}, bf16[2560,320]{0,1:T(8,128)(2,1)}, u32[]{:S(2)}) copy-start(bf16[2560,320]{0,1:T(8,128)(2,1)} %param.26) | copy-start | bytes 4915204
  76.8 11.1 %copy-start.6 = (bf16[1024,320]{0,1:T(8,128)(2,1)}, bf16[1024,320]{0,1:T(8,128)(2,1)S(1)}, u32[]{:S(2)}) copy-start(bf16[1024,320]{0,1:T(8,128)(2,1)S(1)} %convolution_convert_fusion.2) | copy-start | bytes 1966084
  76.9 10.0 %collective-permute-start = (bf16[3,576]{0,1:T(8,128)(2,1)S(1)}, bf16[3,576]{0,1:T(8,128)(2,1)S(1)}, u32[]{:S(2)}, u32[]{:S(2)}) collective-permute-start(bf16[3,576]{0,1:T(8,128)(2,1)S(1)} %pad_maximum_fusion.3), channel_id=1, source_target_pairs={{0,16},{16,32},{32,48},{48,64},{64,80},{80,96},{96,112},{112,128},... | collective-permute-start | bytes 10376 | tf_op jit(solution)/shard_map/ppermute | solution.py:18
  97.8 3.3 copy-start.15
  101.2 9.5 %collective-permute-start.3 = (f32[5,65,128]{2,1,0:T(8,128)S(1)}, f32[5,65,128]{2,1,0:T(8,128)S(1)}, u32[]{:S(2)}, u32[]{:S(2)}) collective-permute-start(f32[5,65,128]{2,1,0:T(8,128)S(1)} %pad_maximum_fusion.1), channel_id=1, source_target_pairs={{0,48},{16,64},{32,80},{48,96},{64,112},{80,128},{96,144},{112,160... | collective-permute-start | bytes 499208 | tf_op jit(solution)/shard_map/ppermute | solution.py:23
  103.7 10.1 %collective-permute-start.2 = (f32[5,65,128]{2,1,0:T(8,128)S(1)}, f32[5,65,128]{2,1,0:T(8,128)S(1)}, u32[]{:S(2)}, u32[]{:S(2)}) collective-permute-start(f32[5,65,128]{2,1,0:T(8,128)S(1)} %pad_maximum_fusion.1), channel_id=1, source_target_pairs={{0,32},{16,48},{32,64},{48,80},{64,96},{80,112},{96,128},{112,144}... | collective-permute-start | bytes 499208 | tf_op jit(solution)/shard_map/ppermute | solution.py:23
  107.5 11.5 %collective-permute-start.1 = (f32[5,65,128]{2,1,0:T(8,128)S(1)}, f32[5,65,128]{2,1,0:T(8,128)S(1)}, u32[]{:S(2)}, u32[]{:S(2)}) collective-permute-start(f32[5,65,128]{2,1,0:T(8,128)S(1)} %pad_maximum_fusion.1), channel_id=1, source_target_pairs={{0,16},{16,32},{32,48},{48,64},{64,80},{80,96},{96,112},{112,128},... | collective-permute-start | bytes 499208 | tf_op jit(solution)/shard_map/ppermute | solution.py:23
  110.3 13.6 %copy-start.3 = (f32[4,256,5,64]{1,0,3,2:T(4,128)S(1)}, f32[4,256,5,64]{1,0,3,2:T(4,128)}, u32[]{:S(2)}) copy-start(f32[4,256,5,64]{1,0,3,2:T(4,128)} %reshape.160) | copy-start | bytes 3932164
  110.4 13.6 %copy-start.9 = (pred[256,256]{1,0:T(8,128)(4,1)S(1)}, pred[256,256]{1,0:T(8,128)(4,1)}, u32[]{:S(2)}) copy-start(pred[256,256]{1,0:T(8,128)(4,1)} %iota_compare_fusion) | copy-start | bytes 196612
  120.6 13.3 %collective-permute-start.5 = (f32[5,65,128]{2,1,0:T(8,128)}, f32[5,65,128]{2,1,0:T(8,128)}, u32[]{:S(2)}, u32[]{:S(2)}) collective-permute-start(f32[5,65,128]{2,1,0:T(8,128)} %pad_maximum_fusion.2), channel_id=1, source_target_pairs={{0,128},{16,144},{32,160},{48,176},{64,192},{80,208},{96,224},{112... | collective-permute-start | bytes 499208 | tf_op jit(solution)/shard_map/ppermute | solution.py:23
  131.0 10.4 %copy-start.4 = (f32[4,256,5,64]{1,0,3,2:T(4,128)S(1)}, f32[4,256,5,64]{1,0,3,2:T(4,128)}, u32[]{:S(2)}) copy-start(f32[4,256,5,64]{1,0,3,2:T(4,128)} %reshape.160) | copy-start | bytes 3932164
  131.0 10.4 %copy-start.13 = (f32[4,5]{1,0:T(4,128)S(1)}, f32[4,5]{1,0:T(4,128)}, u32[]{:S(2)}) copy-start(f32[4,5]{1,0:T(4,128)} %get-tuple-element.113) | copy-start | bytes 244
  131.0 10.4 %copy-start.17 = (f32[5]{0:T(128)S(1)}, f32[5]{0:T(128)}, u32[]{:S(2)}) copy-start(f32[5]{0:T(128)} %param.33) | copy-start | bytes 64
  131.2 9.0 %collective-permute-start.6 = (f32[5,65,128]{2,1,0:T(8,128)}, f32[5,65,128]{2,1,0:T(8,128)S(1)}, u32[]{:S(2)}, u32[]{:S(2)}) collective-permute-start(f32[5,65,128]{2,1,0:T(8,128)} %pad_maximum_fusion.2), channel_id=1, source_target_pairs={{0,192},{16,208},{32,224},{48,240},{1,193},{17,209},{33,225},{49,2... | collective-permute-start | bytes 499208 | tf_op jit(solution)/shard_map/ppermute | solution.py:23
  132.0 8.1 %collective-permute-start.4 = (f32[5,65,128]{2,1,0:T(8,128)}, f32[5,65,128]{2,1,0:T(8,128)S(1)}, u32[]{:S(2)}, u32[]{:S(2)}) collective-permute-start(f32[5,65,128]{2,1,0:T(8,128)} %pad_maximum_fusion.2), channel_id=1, source_target_pairs={{0,64},{16,80},{32,96},{48,112},{64,128},{80,144},{96,160},{112,17... | collective-permute-start | bytes 499208 | tf_op jit(solution)/shard_map/ppermute | solution.py:23
  140.1 5.1 %slice-start.2 = ((s8[5242880]{0:T(1024)(128)(4,1)}), s8[4194304]{0:T(1024)(128)(4,1)S(1)}, s32[]{:S(2)}) async-start(s8[5242880]{0:T(1024)(128)(4,1)} %bitcast.90), calls=%async_computation.8 | async-start | bytes 8388608
  141.4 3.8 %slice-start.3 = ((s8[5242880]{0:T(1024)(128)(4,1)}), s8[1048576]{0:T(1024)(128)(4,1)S(1)}, s32[]{:S(2)}) async-start(s8[5242880]{0:T(1024)(128)(4,1)} %bitcast.90), calls=%async_computation.9 | async-start | bytes 2097152
  144.9 1.4 copy-start.19
  149.5 4.2 %copy-start.20 = (f32[320]{0:T(512)S(1)}, f32[320]{0:T(512)}, u32[]{:S(2)}) copy-start(f32[320]{0:T(512)} %param.34) | copy-start | bytes 3844
  161.3 108.2 %all-gather.5.cloned.1.call-start = ((), (), s32[]{:S(2)}) async-start(), calls=%async_computation.3 | async-start | bytes 5570560 | tf_op jit(solution)/shard_map/all_gather | solution.py:157
  223.6 2.6 copy-start.12
  227.6 122.6 %reduce-scatter.9.cloned.1.call-start = ((), (), s32[]{:S(2)}) async-start(), calls=%async_computation.5 | async-start | bytes 5570560
  (5 other events, 5.1 us)
Sparse Core Ops, SparseCore 0:
  9.2 46.1 all-gather.2
  161.4 60.1 reduce-scatter.6
  227.7 41.7 all-gather.4
  286.4 63.7 reduce-scatter.8

commit v2 on v1

--- a/solution.py
+++ b/solution.py
@@ -45,6 +45,21 @@
         upto = join_packed(older, upto)
         stride *= 4
     return before
+
+
+def gather_group(rows):
+    across = lax.all_gather(rows, "z", axis=0)
+    both = lax.all_gather(across, "core", axis=0)
+    return jnp.swapaxes(both, 0, 1).reshape((-1,) + rows.shape[1:])
+
+
+def scatter_group(rows):
+    chips = lax.axis_size("z")
+    cores = lax.axis_size("core")
+    blocks = rows.reshape((chips, cores, -1) + rows.shape[1:])
+    blocks = jnp.swapaxes(blocks, 0, 1)
+    on_chip = lax.psum_scatter(blocks, "core", scatter_dimension=0)
+    return lax.psum_scatter(on_chip, "z", scatter_dimension=0)
 
 
 def rms_rows(values, gain):
@@ -85,7 +100,7 @@
     w_up,
     w_down,
 ):
-    gathered = lax.all_gather(tokens, "tp", axis=0, tiled=True)
+    gathered = gather_group(tokens)
     normed = rms_rows(gathered, norm1_gain).astype(jnp.bfloat16)
     bc_rows = jnp.dot(normed, w_bc, preferred_element_type=jnp.float32).astype(jnp.bfloat16)
     group_len = gathered.shape[0]
@@ -145,52 +160,50 @@
     extra = extra.at[:, 0].set(squares_hi).at[:, 1].set(squares_lo)
     piece = (gated * ssm_gain).astype(jnp.bfloat16)
     product = jnp.dot(piece, w_out, preferred_element_type=jnp.float32).astype(jnp.bfloat16)
-    reduced = lax.psum_scatter(
-        jnp.concatenate([product, extra], axis=1), "tp", scatter_dimension=0, tiled=True
-    )
+    reduced = scatter_group(jnp.concatenate([product, extra], axis=1))
     width = w_out.shape[1]
     squares_own = reduced[:, width].astype(jnp.float32) + reduced[:, width + 1].astype(jnp.float32)
     scale = lax.rsqrt(squares_own / (HEADS * HEAD_DIM) + EPS)
     mixer_own = reduced[:, :width].astype(jnp.float32) * scale[:, None]
     resid = (tokens.astype(jnp.float32) + mixer_own).astype(jnp.bfloat16)
     normed_own = rms_rows(resid, norm2_gain).astype(jnp.bfloat16)
-    mlp_in = lax.all_gather(normed_own, "tp", axis=0, tiled=True)
+    mlp_in = gather_group(normed_own)
     mlp_gate = jnp.dot(mlp_in, w_gate, preferred_element_type=jnp.float32)
     mlp_up = jnp.dot(mlp_in, w_up, preferred_element_type=jnp.float32)
     hidden = (jax.nn.silu(mlp_gate) * mlp_up).astype(jnp.bfloat16)
     piece = hidden
-    mlp_down = lax.psum_scatter(
-        jnp.dot(piece, w_down, preferred_element_type=jnp.float32).astype(jnp.bfloat16),
-        "tp",
-        scatter_dimension=0,
-        tiled=True,
+    mlp_down = scatter_group(
+        jnp.dot(piece, w_down, preferred_element_type=jnp.float32).astype(jnp.bfloat16)
     ).astype(jnp.float32)
     return (resid.astype(jnp.float32) + mlp_down).astype(jnp.bfloat16)
 
 
 def solution(mesh):
+    cores = 2
+    devices = mesh.devices.reshape(mesh.shape["ctx"], mesh.shape["tp"] // cores, cores)
+    split = jax.sharding.Mesh(devices, ("ctx", "z", "core"))
     return jax.shard_map(
         local,
-        mesh=mesh,
+        mesh=split,
         in_specs=(
-            P(("ctx", "tp"), None),
-            P(),
-            P(None, "tp"),
-            P(None, "tp"),
-            P(),
-            P(None, "tp"),
-            P("tp"),
-            P("tp"),
-            P(None, "tp"),
-            P(),
-            P("tp"),
-            P("tp"),
-            P("tp", None),
-            P(),
-            P(None, "tp"),
-            P(None, "tp"),
-            P("tp", None),
+            P(("ctx", "z", "core"), None),
+            P(),
+            P(None, ("z", "core")),
+            P(None, ("z", "core")),
+            P(),
+            P(None, ("z", "core")),
+            P(("z", "core")),
+            P(("z", "core")),
+            P(None, ("z", "core")),
+            P(),
+            P(("z", "core")),
+            P(("z", "core")),
+            P(("z", "core"), None),
+            P(),
+            P(None, ("z", "core")),
+            P(None, ("z", "core")),
+            P(("z", "core"), None),
         ),
-        out_specs=P(("ctx", "tp"), None),
+        out_specs=P(("ctx", "z", "core"), None),
         check_vma=False,
     )

time: 362 us -> 501 us (1.38)
  waiting for transfers between devices: 229 us -> 332 us
  local copies, waits for them, and re-layouts: 23 us -> 46.6 us
  other arithmetic: 31.8 us -> 42.2 us
    reduce_scatter x0 -> x4, waiting for transfers between devices: none -> 185 us  [the longest x2 139 us: scatter_group(): return lax.psum_scatter(on_chip, 'z', scatter_dimension=0)]
    unnamed x6 -> x8, waiting for transfers between devices: 124 us -> 0.82 us
    all_gather x2 -> x4, waiting for transfers between devices: 85.2 us -> 126 us  [the longest x2 87.8 us: gather_group(): across = lax.all_gather(rows, 'z', axis=0)]
    reshape x0 -> x2, local copies, waits for them, and re-layouts: none -> 21.3 us  [scatter_group(): blocks = rows.reshape((chips, cores, -1) + rows.shape[1:])]
    convert_element_type x0 -> x1, other arithmetic: none -> 7.94 us  [rms_rows(): wide = values.astype(jnp.float32)]
    convert_element_type x0 -> x1, local copies, waits for them, and re-layouts: none -> 5.13 us  [rms_rows(): wide = values.astype(jnp.float32)]
  transfers between devices with their start and end apart: 11 -> 15, of which waited for: 8 -> 12; matrix products, arithmetic and copies ran while one was open for 4% -> 2% of each run, Pallas kernels for 0% -> 0%
where the time goes in v2:
time: 501 us; the launch traced here: 499 us
  waiting for transfers between devices  332 us (66%)
  local copies, waits for them, and re-layouts  46.6 us (9%)
  matrix products  44.3 us (9%)
  other arithmetic  42.2 us (8%)
  starting transfers between devices  19.4 us (4%)
  between operations  14.1 us (3%)
    reduce_scatter x2, waiting for transfers between devices, scatter_group(): return lax.psum_scatter(on_chip, 'z', scatter_dimension=0)  139 us
    all_gather x2, waiting for transfers between devices, gather_group(): across = lax.all_gather(rows, 'z', axis=0)  87.8 us
    reduce_scatter x2, waiting for transfers between devices, scatter_group(): on_chip = lax.psum_scatter(blocks, 'core', scatter_dimension=0)  46.1 us
    all_gather x2, waiting for transfers between devices, gather_group(): both = lax.all_gather(across, 'core', axis=0)  38.6 us
    reshape x2, local copies, waits for them, and re-layouts, scatter_group(): blocks = rows.reshape((chips, cores, -1) + rows.shape[1:])  21.3 us
    ppermute x6, starting transfers between devices, shifted(): lax.ppermute(value, axis, [(source, source + steps) for source in range(c...  15.2 us
    ppermute x6, waiting for transfers between devices, shifted(): lax.ppermute(value, axis, [(source, source + steps) for source in range(c...  13.6 us
    dot_general x1, matrix products, local(): jnp.dot(piece, w_down, preferred_element_type=jnp.float32)  10.8 us
  transfers between devices with their start and end apart: 15, of which 12 were waited for; matrix products, arithmetic and copies ran while one was open for 2% of the time, Pallas kernels for 0%

profile of v2, /device:TPU:2, one launch (start us, length us, event | category | flops | bytes accessed | tf_op | source)
XLA Modules:
  0.0 498.8 jit_solution(9172083207476593763)
XLA Ops:
  7.3 46.9 %all-gather.9.cloned.1.call-done = bf16[512,2560]{1,0:T(8,128)(2,1)} async-done(((bf16[64,2560]{1,0:T(8,128)(2,1)}), bf16[512,2560]{1,0:T(8,128)(2,1)}) %all-gather.9.cloned.1.call-update) | async-done | bytes 2621456 | tf_op jit(solution)/shard_map/all_gather | solution.py:51
  56.9 18.2 %all-gather.11.cloned.1.call-done = bf16[16,64,2560]{2,1,0:T(8,128)(2,1)} async-done(((bf16[8,64,2560]{2,1,0:T(8,128)(2,1)}), bf16[16,64,2560]{2,1,0:T(8,128)(2,1)}) %all-gather.11.cloned.1.call-update) | async-done | bytes 5242896 | tf_op jit(solution)/shard_map/all_gather | solution.py:52
  75.1 3.6 fusion.1
  78.8 7.9 %convert_bitcast_fusion = f32[8,2,64,2560]{3,2,0,1:T(8,128)} fusion(bf16[16,64,2560]{2,1,0:T(8,128)(2,1)} %all-gather.11.cloned.1.call-done), kind=kLoop, calls=%fused_computation.5 | loop fusion | flops 2621440 | bytes 15728640 | tf_op jit(solution)/shard_map/convert_element_type | solution.py:66
  86.8 5.1 %copy.188 = f32[8,2,64,2560]{3,2,1,0:T(8,128)S(1)} copy(f32[8,2,64,2560]{3,2,0,1:T(8,128)} %convert_bitcast_fusion) | data formatting | bytes 20971520 | tf_op jit(solution)/shard_map/convert_element_type | solution.py:66
  91.9 3.3 fusion.3
  95.2 4.0 negate_multiply_fusion
  99.3 6.0 %reduce-window.6 = f32[4,5,2,128]{3,2,1,0:T(2,128)S(1)} reduce-window(f32[4,5,2,128]{3,2,1,0:T(2,128)S(1)} %copy.195, f32[]{:T(128)} %constant.92.clone.1), window={size=1x1x1x128 pad=0_0x0_0x0_0x127_0}, to_apply=%region_1.2 | reduce-window | flops 650240 | bytes 40964 | tf_op jit(solution)/shard_map/reduce-window
  106.3 4.6 convolution_convert_fusion.3
  113.1 3.6 collective-permute-start
  117.4 5.8 %collective-permute-done = bf16[3,576]{0,1:T(8,128)(2,1)S(1)} collective-permute-done((bf16[3,576]{0,1:T(8,128)(2,1)S(1)}, bf16[3,576]{0,1:T(8,128)(2,1)S(1)}, u32[]{:S(2)}, u32[]{:S(2)}) %collective-permute-start) | collective-permute-done | bytes 3488 | tf_op jit(solution)/shard_map/ppermute | solution.py:18
  134.0 3.2 while.15
  139.9 3.6 collective-permute-start.2
  143.5 2.8 collective-permute-start.1
  146.7 3.4 collective-permute-done.2
  150.1 5.2 %collective-permute-done.1 = f32[5,65,128]{2,1,0:T(8,128)S(1)} collective-permute-done((f32[5,65,128]{2,1,0:T(8,128)S(1)}, f32[5,65,128]{2,1,0:T(8,128)S(1)}, u32[]{:S(2)}, u32[]{:S(2)}) %collective-permute-start.1) | collective-permute-done | bytes 166432 | tf_op jit(solution)/shard_map/ppermute | solution.py:23
  156.8 3.3 collective-permute-start.5
  160.1 7.1 %fusion.17 = f32[4,256,5,64]{1,3,2,0:T(8,128)} fusion(f32[4,256,5]{1,2,0:T(8,128)S(1)} %copy.199, f32[4,256,256]{2,1,0:T(8,128)S(1)} %fusion.43, pred[256,256]{1,0:T(8,128)(4,1)S(1)} %copy-done.9, f32[4,256,5,64]{1,0,3,2:T(4,128)S(1)} %copy-done.2, f32[4,256,5]{1,2,0:T(8,128)S(1)} %bitcast.143), kind=kOutput, calls=%fused_computation.31 | convolution fusion | flops 1012203520 | bytes 3776512 | tf_op jit(solution)/shard_map/btsh,bshp->bthp/dot_general | solution.py:133
  171.2 5.1 %collective-permute-done.4 = f32[5,65,128]{2,1,0:T(8,128)S(1)} collective-permute-done((f32[5,65,128]{2,1,0:T(8,128)}, f32[5,65,128]{2,1,0:T(8,128)S(1)}, u32[]{:S(2)}, u32[]{:S(2)}) %collective-permute-start.4) | collective-permute-done | bytes 166432 | tf_op jit(solution)/shard_map/ppermute | solution.py:23
  182.3 3.1 multiply_reduce_fusion
  189.6 4.8 convolution_convert_fusion.1
  197.1 11.0 %copy.211 = bf16[8,2,64,2688]{2,3,0,1:T(8,128)(2,1)} copy(bf16[8,2,64,2688]{3,2,1,0:T(8,128)(2,1)} %bitcast.121) | data formatting | bytes 11010048 | tf_op jit(solution)/shard_map/reshape | solution.py:59
  208.2 21.3 %reduce-scatter.5.cloned.1.call-done = bf16[1,8,64,2688]{2,3,1,0:T(8,128)(2,1)} async-done(((bf16[2,8,64,2688]{2,3,1,0:T(8,128)(2,1)}), bf16[1,8,64,2688]{2,3,1,0:T(8,128)(2,1)}) %reduce-scatter.5.cloned.1.call-update) | async-done | bytes 2752528 | tf_op jit(solution)/shard_map/reduce_scatter | solution.py:61
  230.8 70.1 %reduce-scatter.7.cloned.1.call-done = bf16[1,64,2688]{1,2,0:T(8,128)(2,1)} async-done(((bf16[8,64,2688]{1,2,0:T(8,128)(2,1)}), bf16[1,64,2688]{1,2,0:T(8,128)(2,1)}) %reduce-scatter.7.cloned.1.call-update) | async-done | bytes 344080 | tf_op jit(solution)/shard_map/reduce_scatter | solution.py:62
  304.6 40.9 %all-gather.13.cloned.1.call-done = bf16[512,2560]{1,0:T(8,128)(2,1)} async-done(((bf16[64,2560]{1,0:T(8,128)(2,1)}), bf16[512,2560]{1,0:T(8,128)(2,1)}) %all-gather.13.cloned.1.call-update) | async-done | bytes 2621456 | tf_op jit(solution)/shard_map/all_gather | solution.py:51
  345.8 20.4 %all-gather.15.cloned.1.call-done = bf16[16,64,2560]{2,1,0:T(8,128)(2,1)} async-done(((bf16[8,64,2560]{2,1,0:T(8,128)(2,1)}), bf16[16,64,2560]{2,1,0:T(8,128)(2,1)}) %all-gather.15.cloned.1.call-update) | async-done | bytes 5242896 | tf_op jit(solution)/shard_map/all_gather | solution.py:52
  366.2 3.1 copy.213
  371.6 3.0 fusion.70
  374.6 10.8 %convolution_convert_fusion = bf16[1024,2560]{1,0:T(8,128)(2,1)} fusion(bf16[320,2560]{1,0:T(8,128)(2,1)} %param.39, bf16[1024,2560]{1,0:T(8,128)(2,1)} %bitcast.127, bf16[2560,320]{0,1:T(8,128)(2,1)} %param.38, f32[1024,320]{0,1:T(8,128)} %fusion.70), kind=kOutput, calls=%fused_computation.10 | convolution fusion | flops 3360030720 | bytes 15073280 | tf_op jit(solution)/shard_map/dot_general | solution.py:176
  385.4 10.3 %copy.214 = bf16[8,2,64,2560]{2,3,0,1:T(8,128)(2,1)} copy(bf16[8,2,64,2560]{3,2,1,0:T(8,128)(2,1)} %bitcast.129) | data formatting | bytes 10485760 | tf_op jit(solution)/shard_map/reshape | solution.py:59
  395.8 24.8 %reduce-scatter.9.cloned.1.call-done = bf16[1,8,64,2560]{2,3,1,0:T(8,128)(2,1)} async-done(((bf16[2,8,64,2560]{2,3,1,0:T(8,128)(2,1)}), bf16[1,8,64,2560]{2,3,1,0:T(8,128)(2,1)}) %reduce-scatter.9.cloned.1.call-update) | async-done | bytes 2621456 | tf_op jit(solution)/shard_map/reduce_scatter | solution.py:61
  420.6 69.1 %reduce-scatter.11.cloned.1.call-done = bf16[1,64,2560]{1,2,0:T(8,128)(2,1)} async-done(((bf16[8,64,2560]{1,2,0:T(8,128)(2,1)}), bf16[1,64,2560]{1,2,0:T(8,128)(2,1)}) %reduce-scatter.11.cloned.1.call-update) | async-done | bytes 327696 | tf_op jit(solution)/shard_map/reduce_scatter | solution.py:62
  (172 shorter events, 52.4 us)
Async XLA Ops:
  6.5 183.0 %copy-start = (bf16[320,2560]{1,0:T(8,128)(2,1)S(1)}, bf16[320,2560]{1,0:T(8,128)(2,1)}, u32[]{:S(2)}) copy-start(bf16[320,2560]{1,0:T(8,128)(2,1)} %param.35) | copy-start | bytes 4915204
  6.5 47.7 %all-gather.9.cloned.1.call-start = ((), (), s32[]{:S(2)}) async-start(), calls=%async_computation.8 | async-start | bytes 2949120 | tf_op jit(solution)/shard_map/all_gather | solution.py:51
  7.3 67.9 %all-gather.11.cloned.1.call-start = ((), (), s32[]{:S(2)}) async-start(), calls=%async_computation.9 | async-start | bytes 7864320 | tf_op jit(solution)/shard_map/all_gather | solution.py:52
  54.3 175.2 %reduce-scatter.5.cloned.1.call-start = ((), (), s32[]{:S(2)}) async-start(), calls=%async_computation.4 | async-start | bytes 16515072 | tf_op jit(solution)/shard_map/reduce_scatter | solution.py:61
  86.8 5.1 %copy-start.11 = (f32[2560]{0:T(1024)S(1)}, f32[2560]{0:T(1024)}, u32[]{:S(2)}) copy-start(f32[2560]{0:T(1024)} %param.24) | copy-start | bytes 30724
  105.6 5.4 %slice-start = ((s8[5242880]{0:T(1024)(128)(4,1)}), s8[1048576]{0:T(1024)(128)(4,1)S(1)}, s32[]{:S(2)}) async-start(s8[5242880]{0:T(1024)(128)(4,1)} %bitcast.117), calls=%async_computation.12 | async-start | bytes 2097152
  106.0 11.3 %copy-start.15 = (f32[5]{0:T(128)}, f32[5]{0:T(128)S(1)}, u32[]{:S(2)}) copy-start(f32[5]{0:T(128)S(1)} %get-tuple-element.103) | copy-start | bytes 64
  106.3 4.7 slice-start.1
  106.3 4.7 copy-start.20
  113.0 11.1 %copy-start.6 = (bf16[1024,320]{0,1:T(8,128)(2,1)}, bf16[1024,320]{0,1:T(8,128)(2,1)S(1)}, u32[]{:S(2)}) copy-start(bf16[1024,320]{0,1:T(8,128)(2,1)S(1)} %convolution_convert_fusion.2) | copy-start | bytes 1966084
  113.1 10.0 %collective-permute-start = (bf16[3,576]{0,1:T(8,128)(2,1)S(1)}, bf16[3,576]{0,1:T(8,128)(2,1)S(1)}, u32[]{:S(2)}, u32[]{:S(2)}) collective-permute-start(bf16[3,576]{0,1:T(8,128)(2,1)S(1)} %pad_maximum_fusion.3), channel_id=1, source_target_pairs={{0,16},{16,32},{32,48},{48,64},{64,80},{80,96},{96,112},{112,128},... | collective-permute-start | bytes 10376 | tf_op jit(solution)/shard_map/ppermute | solution.py:18
  137.3 9.4 %collective-permute-start.3 = (f32[5,65,128]{2,1,0:T(8,128)S(1)}, f32[5,65,128]{2,1,0:T(8,128)S(1)}, u32[]{:S(2)}, u32[]{:S(2)}) collective-permute-start(f32[5,65,128]{2,1,0:T(8,128)S(1)} %pad_maximum_fusion.1), channel_id=1, source_target_pairs={{0,48},{16,64},{32,80},{48,96},{64,112},{80,128},{96,144},{112,160... | collective-permute-start | bytes 499208 | tf_op jit(solution)/shard_map/ppermute | solution.py:23
  139.9 10.2 %collective-permute-start.2 = (f32[5,65,128]{2,1,0:T(8,128)S(1)}, f32[5,65,128]{2,1,0:T(8,128)S(1)}, u32[]{:S(2)}, u32[]{:S(2)}) collective-permute-start(f32[5,65,128]{2,1,0:T(8,128)S(1)} %pad_maximum_fusion.1), channel_id=1, source_target_pairs={{0,32},{16,48},{32,64},{48,80},{64,96},{80,112},{96,128},{112,144}... | collective-permute-start | bytes 499208 | tf_op jit(solution)/shard_map/ppermute | solution.py:23
  143.5 11.8 %collective-permute-start.1 = (f32[5,65,128]{2,1,0:T(8,128)S(1)}, f32[5,65,128]{2,1,0:T(8,128)S(1)}, u32[]{:S(2)}, u32[]{:S(2)}) collective-permute-start(f32[5,65,128]{2,1,0:T(8,128)S(1)} %pad_maximum_fusion.1), channel_id=1, source_target_pairs={{0,16},{16,32},{32,48},{48,64},{64,80},{80,96},{96,112},{112,128},... | collective-permute-start | bytes 499208 | tf_op jit(solution)/shard_map/ppermute | solution.py:23
  146.3 13.8 %copy-start.2 = (f32[4,256,5,64]{1,0,3,2:T(4,128)S(1)}, f32[4,256,5,64]{1,0,3,2:T(4,128)}, u32[]{:S(2)}) copy-start(f32[4,256,5,64]{1,0,3,2:T(4,128)} %reshape.187) | copy-start | bytes 3932164
  146.3 13.8 %copy-start.9 = (pred[256,256]{1,0:T(8,128)(4,1)S(1)}, pred[256,256]{1,0:T(8,128)(4,1)}, u32[]{:S(2)}) copy-start(pred[256,256]{1,0:T(8,128)(4,1)} %iota_compare_fusion) | copy-start | bytes 196612
  156.8 13.6 %collective-permute-start.5 = (f32[5,65,128]{2,1,0:T(8,128)}, f32[5,65,128]{2,1,0:T(8,128)}, u32[]{:S(2)}, u32[]{:S(2)}) collective-permute-start(f32[5,65,128]{2,1,0:T(8,128)} %pad_maximum_fusion.2), channel_id=1, source_target_pairs={{0,128},{16,144},{32,160},{48,176},{64,192},{80,208},{96,224},{112... | collective-permute-start | bytes 499208 | tf_op jit(solution)/shard_map/ppermute | solution.py:23
  167.2 10.2 %copy-start.3 = (f32[4,256,5,64]{1,0,3,2:T(4,128)S(1)}, f32[4,256,5,64]{1,0,3,2:T(4,128)}, u32[]{:S(2)}) copy-start(f32[4,256,5,64]{1,0,3,2:T(4,128)} %reshape.187) | copy-start | bytes 3932164
  167.2 10.2 %copy-start.13 = (f32[4,5]{1,0:T(4,128)S(1)}, f32[4,5]{1,0:T(4,128)}, u32[]{:S(2)}) copy-start(f32[4,5]{1,0:T(4,128)} %get-tuple-element.111) | copy-start | bytes 244
  167.2 10.2 %copy-start.19 = (f32[5]{0:T(128)S(1)}, f32[5]{0:T(128)}, u32[]{:S(2)}) copy-start(f32[5]{0:T(128)} %param.33) | copy-start | bytes 64
  167.4 9.0 %collective-permute-start.6 = (f32[5,65,128]{2,1,0:T(8,128)}, f32[5,65,128]{2,1,0:T(8,128)S(1)}, u32[]{:S(2)}, u32[]{:S(2)}) collective-permute-start(f32[5,65,128]{2,1,0:T(8,128)} %pad_maximum_fusion.2), channel_id=1, source_target_pairs={{0,192},{16,208},{32,224},{48,240},{1,193},{17,209},{33,225},{49,2... | collective-permute-start | bytes 499208 | tf_op jit(solution)/shard_map/ppermute | solution.py:23
  168.2 8.1 %collective-permute-start.4 = (f32[5,65,128]{2,1,0:T(8,128)}, f32[5,65,128]{2,1,0:T(8,128)S(1)}, u32[]{:S(2)}, u32[]{:S(2)}) collective-permute-start(f32[5,65,128]{2,1,0:T(8,128)} %pad_maximum_fusion.2), channel_id=1, source_target_pairs={{0,64},{16,80},{32,96},{48,112},{64,128},{80,144},{96,160},{112,17... | collective-permute-start | bytes 499208 | tf_op jit(solution)/shard_map/ppermute | solution.py:23
  170.3 10.9 %slice-start.2 = ((s8[5242880]{0:T(1024)(128)(4,1)}), s8[4194304]{0:T(1024)(128)(4,1)S(1)}, s32[]{:S(2)}) async-start(s8[5242880]{0:T(1024)(128)(4,1)} %bitcast.119), calls=%async_computation.14 | async-start | bytes 8388608
  185.5 4.1 copy-start.23
  208.2 92.8 %reduce-scatter.7.cloned.1.call-start = ((), (), s32[]{:S(2)}) async-start(), calls=%async_computation.5 | async-start | bytes 6193152 | tf_op jit(solution)/shard_map/reduce_scatter | solution.py:62
  229.5 73.6 %copy-start.12 = (f32[2560]{0:T(1024)S(1)}, f32[2560]{0:T(1024)}, u32[]{:S(2)}) copy-start(f32[2560]{0:T(1024)} %param.36) | copy-start | bytes 30724
  229.5 115.9 %all-gather.13.cloned.1.call-start = ((), (), s32[]{:S(2)}) async-start(), calls=%async_computation.10 | async-start | bytes 2949120 | tf_op jit(solution)/shard_map/all_gather | solution.py:51
  304.5 61.7 %all-gather.15.cloned.1.call-start = ((), (), s32[]{:S(2)}) async-start(), calls=%async_computation.11 | async-start | bytes 7864320 | tf_op jit(solution)/shard_map/all_gather | solution.py:52
  345.5 75.1 %reduce-scatter.9.cloned.1.call-start = ((), (), s32[]{:S(2)}) async-start(), calls=%async_computation.6 | async-start | bytes 15728640 | tf_op jit(solution)/shard_map/reduce_scatter | solution.py:61
  366.2 5.4 %copy-start.22 = (bf16[2560,320]{0,1:T(8,128)(2,1)S(1)}, bf16[2560,320]{0,1:T(8,128)(2,1)}, u32[]{:S(2)}) copy-start(bf16[2560,320]{0,1:T(8,128)(2,1)} %param.37) | copy-start | bytes 4915204
  395.7 94.0 %reduce-scatter.11.cloned.1.call-start = ((), (), s32[]{:S(2)}) async-start(), calls=%async_computation.7 | async-start | bytes 5898240 | tf_op jit(solution)/shard_map/reduce_scatter | solution.py:62
  420.6 71.3 %copy-start.1 = (bf16[320,2560]{1,0:T(8,128)(2,1)S(1)}, bf16[320,2560]{1,0:T(8,128)(2,1)}, u32[]{:S(2)}) copy-start(bf16[320,2560]{1,0:T(8,128)(2,1)} %param.35) | copy-start | bytes 4915204
  (13 other events, 26.5 us)
Sparse Core Ops, SparseCore 0:
  9.1 45.0 all-gather.8
  56.0 19.0 all-gather.10
  208.3 21.1 reduce-scatter.4
  231.9 68.9 reduce-scatter.6
  304.6 40.7 all-gather.12
  347.1 19.0 all-gather.14
  395.8 24.7 reduce-scatter.8
  423.2 66.5 reduce-scatter.10

commit v3 on v1

--- a/solution.py
+++ b/solution.py
@@ -61,11 +61,6 @@
     return result
 
 
-def carry_step(state, pieces):
-    decay_now, fresh = pieces
-    return (decay_now[:, None, None] * state + fresh, state)
-
-
 def local(
     tokens,
     norm1_gain,
@@ -103,7 +98,8 @@
     block_count = group_len // BLOCK_LEN
     log_blocks = log_decay.reshape(block_count, BLOCK_LEN, head_count)
     step_blocks = dt_step.reshape(block_count, BLOCK_LEN, head_count)
-    cum_decay = jnp.cumsum(log_blocks, axis=1)
+    lower = jnp.tril(jnp.ones((BLOCK_LEN, BLOCK_LEN), jnp.float32))
+    cum_decay = jnp.einsum("ts,bsh->bth", lower, log_blocks, precision=lax.Precision.HIGHEST)
     b_mat = conv_bcm[:, :STATE_DIM].reshape(block_count, BLOCK_LEN, STATE_DIM)
     c_mat = conv_bcm[:, STATE_DIM:].reshape(block_count, BLOCK_LEN, STATE_DIM)
     scores = jnp.einsum("btn,bsn->bts", c_mat, b_mat, preferred_element_type=jnp.float32)
@@ -125,7 +121,12 @@
     )
     block_decay = jnp.exp(block_last)
     zero_state = jnp.zeros((head_count, HEAD_DIM, STATE_DIM), jnp.float32)
-    local_final, local_in = lax.scan(carry_step, zero_state, (block_decay, block_states))
+    running = zero_state
+    entering = []
+    for block in range(block_count):
+        entering.append(running)
+        running = block_decay[block][:, None, None] * running + block_states[block]
+    local_final, local_in = running, jnp.stack(entering)
     total_log = jnp.sum(block_last, axis=0)
     prior_decay = jnp.exp(jnp.cumsum(block_last, axis=0) - block_last)
     packed = jnp.concatenate(
@@ -145,16 +146,15 @@
     extra = extra.at[:, 0].set(squares_hi).at[:, 1].set(squares_lo)
     piece = (gated * ssm_gain).astype(jnp.bfloat16)
     product = jnp.dot(piece, w_out, preferred_element_type=jnp.float32).astype(jnp.bfloat16)
-    reduced = lax.psum_scatter(
-        jnp.concatenate([product, extra], axis=1), "tp", scatter_dimension=0, tiled=True
-    )
+    reduced = lax.psum(jnp.concatenate([product, extra], axis=1), "tp")
     width = w_out.shape[1]
-    squares_own = reduced[:, width].astype(jnp.float32) + reduced[:, width + 1].astype(jnp.float32)
-    scale = lax.rsqrt(squares_own / (HEADS * HEAD_DIM) + EPS)
-    mixer_own = reduced[:, :width].astype(jnp.float32) * scale[:, None]
-    resid = (tokens.astype(jnp.float32) + mixer_own).astype(jnp.bfloat16)
-    normed_own = rms_rows(resid, norm2_gain).astype(jnp.bfloat16)
-    mlp_in = lax.all_gather(normed_own, "tp", axis=0, tiled=True)
+    squares_all = reduced[:, width].astype(jnp.float32) + reduced[:, width + 1].astype(jnp.float32)
+    scale = lax.rsqrt(squares_all / (HEADS * HEAD_DIM) + EPS)
+    mixer_all = reduced[:, :width].astype(jnp.float32) * scale[:, None]
+    resid_all = (gathered.astype(jnp.float32) + mixer_all).astype(jnp.bfloat16)
+    mlp_in = rms_rows(resid_all, norm2_gain).astype(jnp.bfloat16)
+    own_rows = tokens.shape[0]
+    resid = lax.dynamic_slice_in_dim(resid_all, lax.axis_index("tp") * own_rows, own_rows, 0)
     mlp_gate = jnp.dot(mlp_in, w_gate, preferred_element_type=jnp.float32)
     mlp_up = jnp.dot(mlp_in, w_up, preferred_element_type=jnp.float32)
     hidden = (jax.nn.silu(mlp_gate) * mlp_up).astype(jnp.bfloat16)

time: 362 us -> 375 us (1.036)
  waiting for transfers between devices: 229 us -> 245 us
  matrix products: 44.9 us -> 38.7 us
    psum x0 -> x1, waiting for transfers between devices: none -> 128 us  [local(): reduced = lax.psum(jnp.concatenate([product, extra], axis=1), 'tp')]
    unnamed x6 -> x4, waiting for transfers between devices: 124 us -> 65.8 us
    all_gather x1 -> x0, waiting for transfers between devices: 41.6 us -> none  [local(): mlp_in = lax.all_gather(normed_own, 'tp', axis=0, tiled=True)]
    ppermute x6, waiting for transfers between devices: 13.8 us -> 3.14 us  [shifted(): lax.ppermute(value, axis, [(source, source + steps) for source in range(c...]
    all_gather x0 -> x1, local copies, waits for them, and re-layouts: none -> 7.99 us  [local(): gathered = lax.all_gather(tokens, 'tp', axis=0, tiled=True)]
    another operation x6 -> x3, other arithmetic: 9.58 us -> 2.67 us
    reduce_sum x2, other arithmetic: 5.17 us -> 9.74 us  [rms_rows(): jnp.mean(wide * wide, axis=-1, keepdims=True) + EPS]
    dot_general x1, matrix products: 5.94 us -> 2.08 us  [local(): mlp_gate = jnp.dot(mlp_in, w_gate, preferred_element_type=jnp.float32)]
  transfers between devices with their start and end apart: 11 -> 10, of which waited for: 8 -> 5; matrix products, arithmetic and copies ran while one was open for 4% -> 4% of each run, Pallas kernels for 0% -> 0%
where the time goes in v3:
time: 375 us; the launch traced here: 374 us
  waiting for transfers between devices  245 us (65%)
  matrix products  38.7 us (10%)
  other arithmetic  31.7 us (8%)
  local copies, waits for them, and re-layouts  25.4 us (7%)
  starting transfers between devices  19.5 us (5%)
  between operations  13.8 us (4%)
    psum x1, waiting for transfers between devices, local(): reduced = lax.psum(jnp.concatenate([product, extra], axis=1), 'tp')  128 us
    unnamed x4, waiting for transfers between devices  65.8 us
    all_gather x1, waiting for transfers between devices, local(): gathered = lax.all_gather(tokens, 'tp', axis=0, tiled=True)  42.5 us
    ppermute x6, starting transfers between devices, shifted(): lax.ppermute(value, axis, [(source, source + steps) for source in range(c...  15.6 us
    dot_general x1, matrix products, local(): jnp.dot(piece, w_down, preferred_element_type=jnp.float32)  10.2 us
    reduce_sum x2, other arithmetic, rms_rows(): jnp.mean(wide * wide, axis=-1, keepdims=True) + EPS  9.74 us
    unnamed x84, local copies, waits for them, and re-layouts  8.22 us
    all_gather x1, local copies, waits for them, and re-layouts, local(): gathered = lax.all_gather(tokens, 'tp', axis=0, tiled=True)  7.99 us
  transfers between devices with their start and end apart: 10, of which 5 were waited for; matrix products, arithmetic and copies ran while one was open for 4% of the time, Pallas kernels for 0%

profile of v3, /device:TPU:2, one launch (start us, length us, event | category | flops | bytes accessed | tf_op | source)
XLA Modules:
  0.0 374.0 jit_solution(4330493021203087898)
XLA Ops:
  11.4 1.4 fusion.95
  12.8 42.5 %all-gather.2.cloned.1.call-done = bf16[1024,2560]{1,0:T(8,128)(2,1)} async-done(((bf16[64,2560]{1,0:T(8,128)(2,1)}), bf16[1024,2560]{1,0:T(8,128)(2,1)}) %all-gather.2.cloned.1.call-update) | async-done | bytes 5242896 | tf_op jit(solution)/shard_map/all_gather | solution.py:83
  55.3 8.0 %copy.72 = bf16[1024,2560]{0,1:T(8,128)(2,1)} copy(bf16[1024,2560]{1,0:T(8,128)(2,1)} %all-gather.2.cloned.1.call-done) | data formatting | bytes 10485760 | tf_op jit(solution)/shard_map/all_gather | solution.py:83
  63.3 3.8 %fusion.3 = f32[1024]{0:T(1024)S(1)} fusion(bf16[1024,2560]{0,1:T(8,128)(2,1)} %copy.72), kind=kLoop, calls=%fused_computation.8 | loop fusion | flops 7863296 | bytes 5246976 | tf_op jit(solution)/shard_map/reduce_sum | solution.py:52
  68.6 1.9 negate_multiply_fusion
  72.6 5.0 %convolution_convert_fusion.2 = bf16[1024,320]{0,1:T(8,128)(2,1)S(1)} fusion(bf16[2560,320]{0,1:T(8,128)(2,1)} %param.24, bf16[1024,2560]{0,1:T(8,128)(2,1)} %copy-done.3), kind=kOutput, calls=%fused_computation.34 | convolution fusion | flops 1678049280 | bytes 7536640 | tf_op jit(solution)/shard_map/dot_general | solution.py:90
  77.8 1.6 convolution_convert_fusion.3
  79.5 3.6 collective-permute-start
  84.2 5.3 %collective-permute-done = bf16[3,576]{0,1:T(8,128)(2,1)S(1)} collective-permute-done((bf16[3,576]{0,1:T(8,128)(2,1)S(1)}, bf16[3,576]{0,1:T(8,128)(2,1)S(1)}, u32[]{:S(2)}, u32[]{:S(2)}) %collective-permute-start) | collective-permute-done | bytes 3488 | tf_op jit(solution)/shard_map/ppermute | solution.py:18
  90.4 2.4 fusion.54
  92.9 1.9 reshape.152
  97.5 1.8 fusion.36
  101.7 1.9 collective-permute-start.1
  103.7 4.0 %collective-permute-start.2 = (f32[5,65,128]{2,1,0:T(8,128)}, f32[5,65,128]{2,1,0:T(8,128)}, u32[]{:S(2)}, u32[]{:S(2)}) collective-permute-start(f32[5,65,128]{2,1,0:T(8,128)} %pad_maximum_fusion.1), channel_id=1, source_target_pairs={{0,32},{16,48},{32,64},{48,80},{64,96},{80,112},{96,128},{112,144}... | collective-permute-start | bytes 499208 | tf_op jit(solution)/shard_map/ppermute | solution.py:23
  107.7 4.3 %collective-permute-start.3 = (f32[5,65,128]{2,1,0:T(8,128)}, f32[5,65,128]{2,1,0:T(8,128)}, u32[]{:S(2)}, u32[]{:S(2)}) collective-permute-start(f32[5,65,128]{2,1,0:T(8,128)} %pad_maximum_fusion.1), channel_id=1, source_target_pairs={{0,48},{16,64},{32,80},{48,96},{64,112},{80,128},{96,144},{112,160... | collective-permute-start | bytes 499208 | tf_op jit(solution)/shard_map/ppermute | solution.py:23
  112.3 7.1 %fusion.24 = f32[4,256,5,64]{1,3,2,0:T(8,128)} fusion(f32[4,256,5]{1,2,0:T(8,128)S(1)} %copy-done.13, f32[4,256,256]{2,1,0:T(8,128)S(1)} %fusion.58, pred[256,256]{1,0:T(8,128)(4,1)S(1)} %copy-done.14, f32[4,256,5,64]{1,0,3,2:T(4,128)S(1)} %reshape.152, f32[4,256,5]{1,2,0:T(8,128)S(1)} %bitcast.114), kind=kOutput, calls=%fused_computation.31 | convolution fusion | flops 1012203520 | bytes 3776512 | tf_op jit(solution)/shard_map/btsh,bshp->bthp/dot_general | solution.py:114
  120.6 1.5 multiply_add_fusion
  122.1 3.2 collective-permute-start.4
  125.4 1.3 collective-permute-start.5
  127.7 3.1 collective-permute-done.4
  134.3 2.2 multiply_reduce_fusion
  136.5 1.3 broadcast_select_fusion
  137.9 5.2 %convolution_convert_fusion.1 = bf16[1024,2560]{0,1:T(8,128)(2,1)} fusion(bf16[320,2560]{1,0:T(8,128)(2,1)S(1)} %copy-done, f32[320]{0:T(512)S(1)} %copy-done.34, f32[1024,320]{0,1:T(8,128)S(1)} %bitcast.110, f32[1024,320]{0,1:T(8,128)S(1)} %get-tuple-element.65), kind=kOutput, calls=%fused_computation.13 | convolution fusion | flops 1682636800 | bytes 9504000 | tf_op jit(solution)/shard_map/dot_general | solution.py:148
  143.2 5.6 %pad_maximum_fusion = bf16[1024,2688]{0,1:T(8,128)(2,1)} fusion(bf16[1024,128]{0,1:T(8,128)(2,1)S(1)} %scatter.9, bf16[1024,2560]{0,1:T(8,128)(2,1)} %convolution_convert_fusion.1), kind=kLoop, calls=%fused_computation.14 | loop fusion | flops 11010048 | bytes 11010048 | tf_op jit(solution)/shard_map/concatenate | solution.py:149
  149.1 128.2 %all-reduce.3.cloned.1.call-done = bf16[1024,2688]{0,1:T(8,128)(2,1)} async-done(((bf16[1024,2688]{0,1:T(8,128)(2,1)}), bf16[1024,2688]{0,1:T(8,128)(2,1)}) %all-reduce.3.cloned.1.call-update) | async-done | bytes 5505040 | tf_op jit(solution)/shard_map/psum | solution.py:149
  278.1 6.0 %fusion = (f32[1024]{0:T(1024)S(1)}, bf16[1024,2560]{0,1:T(8,128)(2,1)S(1)}) fusion(f32[1024]{0:T(1024)S(1)} %bitcast.116, bf16[1024,2688]{0,1:T(8,128)(2,1)} %all-reduce.3.cloned.1.call-done, bf16[1024,2560]{0,1:T(8,128)(2,1)} %copy.72), kind=kLoop, calls=%fused_computation.5 | loop fusion | flops 20970496 | bytes 15736832 | tf_op jit(solution)/shard_map/reduce_sum | solution.py:52
  284.1 2.3 copy-done.6
  286.4 2.1 fusion.18
  288.5 10.2 %convolution_convert_fusion = bf16[1024,2560]{1,0:T(8,128)(2,1)} fusion(bf16[320,2560]{1,0:T(8,128)(2,1)S(1)} %copy-done.31, bf16[2560,320]{0,1:T(8,128)(2,1)} %param.36, bf16[1024,2560]{0,1:T(8,128)(2,1)} %copy-done.6, f32[2560]{0:T(1024)S(1)} %copy-done.33, f32[1024]{0:T(1024)S(1)} %add_rsqrt_fusion, f32[1024,320]{0,1:T(8,128)S(1)} %fusion.18), kind=kOutput, calls=%fused_computation.12 | convolution fusion | flops 3370516480 | bytes 15087616 | tf_op jit(solution)/shard_map/dot_general | solution.py:163
  298.7 65.0 %reduce-scatter.4.cloned.1.call-done = bf16[64,2560]{1,0:T(8,128)(2,1)} async-done(((bf16[1024,2560]{1,0:T(8,128)(2,1)}), bf16[64,2560]{1,0:T(8,128)(2,1)}) %reduce-scatter.4.cloned.1.call-update) | async-done | bytes 327696
  363.7 1.4 copy.95
  365.2 1.4 add_convert_fusion
  (141 shorter events, 23.8 us)
Async XLA Ops:
  6.5 131.4 %copy-start = (bf16[320,2560]{1,0:T(8,128)(2,1)S(1)}, bf16[320,2560]{1,0:T(8,128)(2,1)}, u32[]{:S(2)}) copy-start(bf16[320,2560]{1,0:T(8,128)(2,1)} %param.33) | copy-start | bytes 4915204
  6.5 48.8 %all-gather.2.cloned.1.call-start = ((), (), s32[]{:S(2)}) async-start(), calls=%async_computation.1 | async-start | bytes 5570560 | tf_op jit(solution)/shard_map/all_gather | solution.py:83
  7.3 270.0 %all-reduce.3.cloned.1.call-start = ((), (), s32[]{:S(2)}) async-start(), calls=%async_computation.2 | async-start | bytes 11010048 | tf_op jit(solution)/shard_map/psum | solution.py:149
  63.3 4.0 %copy-start.2 = (bf16[1024,2560]{0,1:T(8,128)(2,1)S(1)}, bf16[1024,2560]{0,1:T(8,128)(2,1)}, u32[]{:S(2)}) copy-start(bf16[1024,2560]{0,1:T(8,128)(2,1)} %copy.72) | copy-start | bytes 15728644
  63.3 4.0 %copy-start.16 = (f32[2560]{0:T(1024)S(1)}, f32[2560]{0:T(1024)}, u32[]{:S(2)}) copy-start(f32[2560]{0:T(1024)} %param.22) | copy-start | bytes 30724
  71.0 6.8 %slice-start = ((s8[5242880]{0:T(1024)(128)(4,1)}), s8[1048576]{0:T(1024)(128)(4,1)S(1)}, s32[]{:S(2)}) async-start(s8[5242880]{0:T(1024)(128)(4,1)} %bitcast.102), calls=%async_computation.4 | async-start | bytes 2097152
  71.5 12.1 %copy-start.19 = (f32[5]{0:T(128)}, f32[5]{0:T(128)S(1)}, u32[]{:S(2)}) copy-start(f32[5]{0:T(128)S(1)} %get-tuple-element.29) | copy-start | bytes 64
  72.6 5.1 %slice-start.1 = ((s8[5242880]{0:T(1024)(128)(4,1)}), s8[4194304]{0:T(1024)(128)(4,1)S(1)}, s32[]{:S(2)}) async-start(s8[5242880]{0:T(1024)(128)(4,1)} %bitcast.102), calls=%async_computation.5 | async-start | bytes 8388608
  72.6 5.1 %copy-start.32 = (bf16[2560,256]{1,0:T(8,128)(2,1)S(1)}, bf16[2560,256]{1,0:T(8,128)(2,1)}, u32[]{:S(2)}) copy-start(bf16[2560,256]{1,0:T(8,128)(2,1)} %param.25) | copy-start | bytes 3932164
  79.5 10.0 %collective-permute-start = (bf16[3,576]{0,1:T(8,128)(2,1)S(1)}, bf16[3,576]{0,1:T(8,128)(2,1)S(1)}, u32[]{:S(2)}, u32[]{:S(2)}) collective-permute-start(bf16[3,576]{0,1:T(8,128)(2,1)S(1)} %pad_maximum_fusion.3), channel_id=1, source_target_pairs={{0,16},{16,32},{32,48},{48,64},{64,80},{80,96},{96,112},{112,128},... | collective-permute-start | bytes 10376 | tf_op jit(solution)/shard_map/ppermute | solution.py:18
  97.5 3.4 copy-start.20
  99.4 12.9 %copy-start.13 = (f32[4,256,5]{1,2,0:T(8,128)S(1)}, f32[4,256,5]{1,2,0:T(8,128)}, u32[]{:S(2)}) copy-start(f32[4,256,5]{1,2,0:T(8,128)} %copy-done.12) | copy-start | bytes 61444
  99.4 12.9 %copy-start.14 = (pred[256,256]{1,0:T(8,128)(4,1)S(1)}, pred[256,256]{1,0:T(8,128)(4,1)}, u32[]{:S(2)}) copy-start(pred[256,256]{1,0:T(8,128)(4,1)} %iota_compare_fusion) | copy-start | bytes 196612
  101.7 17.8 %collective-permute-start.1 = (f32[5,65,128]{2,1,0:T(8,128)}, f32[5,65,128]{2,1,0:T(8,128)}, u32[]{:S(2)}, u32[]{:S(2)}) collective-permute-start(f32[5,65,128]{2,1,0:T(8,128)} %pad_maximum_fusion.1), channel_id=1, source_target_pairs={{0,16},{16,32},{32,48},{48,64},{64,80},{80,96},{96,112},{112,128},... | collective-permute-start | bytes 499208 | tf_op jit(solution)/shard_map/ppermute | solution.py:23
  103.7 15.9 %collective-permute-start.2 = (f32[5,65,128]{2,1,0:T(8,128)}, f32[5,65,128]{2,1,0:T(8,128)}, u32[]{:S(2)}, u32[]{:S(2)}) collective-permute-start(f32[5,65,128]{2,1,0:T(8,128)} %pad_maximum_fusion.1), channel_id=1, source_target_pairs={{0,32},{16,48},{32,64},{48,80},{64,96},{80,112},{96,128},{112,144}... | collective-permute-start | bytes 499208 | tf_op jit(solution)/shard_map/ppermute | solution.py:23
  107.7 11.9 %collective-permute-start.3 = (f32[5,65,128]{2,1,0:T(8,128)}, f32[5,65,128]{2,1,0:T(8,128)}, u32[]{:S(2)}, u32[]{:S(2)}) collective-permute-start(f32[5,65,128]{2,1,0:T(8,128)} %pad_maximum_fusion.1), channel_id=1, source_target_pairs={{0,48},{16,64},{32,80},{48,96},{64,112},{80,128},{96,144},{112,160... | collective-permute-start | bytes 499208 | tf_op jit(solution)/shard_map/ppermute | solution.py:23
  112.3 8.2 %copy-start.21 = (f32[5]{0:T(128)S(1)}, f32[5]{0:T(128)}, u32[]{:S(2)}) copy-start(f32[5]{0:T(128)} %copy-done.19) | copy-start | bytes 64
  112.3 8.2 %copy-start.18 = (f32[5]{0:T(128)S(1)}, f32[5]{0:T(128)}, u32[]{:S(2)}) copy-start(f32[5]{0:T(128)} %get-tuple-element.58) | copy-start | bytes 64
  112.3 8.2 %copy-start.28 = (f32[5]{0:T(128)S(1)}, f32[5]{0:T(128)}, u32[]{:S(2)}) copy-start(f32[5]{0:T(128)} %exp.74) | copy-start | bytes 64
  119.6 5.8 %copy-start.5 = (f32[4,5,64,128]{3,2,1,0:T(8,128)S(1)}, f32[4,5,64,128]{3,2,1,0:T(8,128)}, u32[]{:S(2)}) copy-start(f32[4,5,64,128]{3,2,1,0:T(8,128)} %copy-done.4) | copy-start | bytes 1966084
  122.0 8.9 %copy-start.7 = (f32[4,256,5,64]{1,3,2,0:T(8,128)S(1)}, f32[4,256,5,64]{1,3,2,0:T(8,128)}, u32[]{:S(2)}) copy-start(f32[4,256,5,64]{1,3,2,0:T(8,128)} %fusion.24) | copy-start | bytes 3932164
  122.0 8.9 %copy-start.10 = (f32[4,256,5]{1,2,0:T(8,128)S(1)}, f32[4,256,5]{1,2,0:T(8,128)}, u32[]{:S(2)}) copy-start(f32[4,256,5]{1,2,0:T(8,128)} %get-tuple-element.48) | copy-start | bytes 61444
  122.0 8.9 %copy-start.26 = (f32[5]{0:T(128)S(1)}, f32[5]{0:T(128)}, u32[]{:S(2)}) copy-start(f32[5]{0:T(128)} %param.31) | copy-start | bytes 64
  122.1 8.9 %copy-start.27 = (f32[4]{0:T(128)S(1)}, f32[4]{0:T(128)}, u32[]{:S(2)}) copy-start(f32[4]{0:T(128)} %pad.11.clone) | copy-start | bytes 52
  122.1 8.7 %collective-permute-start.4 = (f32[5,65,128]{2,1,0:T(8,128)S(1)}, f32[5,65,128]{2,1,0:T(8,128)S(1)}, u32[]{:S(2)}, u32[]{:S(2)}) collective-permute-start(f32[5,65,128]{2,1,0:T(8,128)S(1)} %pad_maximum_fusion.2), channel_id=1, source_target_pairs={{0,64},{16,80},{32,96},{48,112},{64,128},{80,144},{96,160},{112,17... | collective-permute-start | bytes 499208 | tf_op jit(solution)/shard_map/ppermute | solution.py:23
  125.4 5.4 %collective-permute-start.5 = (f32[5,65,128]{2,1,0:T(8,128)S(1)}, f32[5,65,128]{2,1,0:T(8,128)S(1)}, u32[]{:S(2)}, u32[]{:S(2)}) collective-permute-start(f32[5,65,128]{2,1,0:T(8,128)S(1)} %pad_maximum_fusion.2), channel_id=1, source_target_pairs={{0,128},{16,144},{32,160},{48,176},{64,192},{80,208},{96,224},{112... | collective-permute-start | bytes 499208 | tf_op jit(solution)/shard_map/ppermute | solution.py:23
  126.7 4.1 %collective-permute-start.6 = (f32[5,65,128]{2,1,0:T(8,128)S(1)}, f32[5,65,128]{2,1,0:T(8,128)S(1)}, u32[]{:S(2)}, u32[]{:S(2)}) collective-permute-start(f32[5,65,128]{2,1,0:T(8,128)S(1)} %pad_maximum_fusion.2), channel_id=1, source_target_pairs={{0,192},{16,208},{32,224},{48,240},{1,193},{17,209},{33,225},{49,2... | collective-permute-start | bytes 499208 | tf_op jit(solution)/shard_map/ppermute | solution.py:23
  134.3 3.6 copy-start.34
  148.8 215.0 %reduce-scatter.4.cloned.1.call-start = ((), (), s32[]{:S(2)}) async-start(), calls=%async_computation.3 | async-start | bytes 5570560
  278.1 8.4 %copy-start.30 = (bf16[2560,320]{0,1:T(8,128)(2,1)S(1)}, bf16[2560,320]{0,1:T(8,128)(2,1)}, u32[]{:S(2)}) copy-start(bf16[2560,320]{0,1:T(8,128)(2,1)} %param.35) | copy-start | bytes 4915204
  278.1 8.3 %copy-start.33 = (f32[2560]{0:T(1024)S(1)}, f32[2560]{0:T(1024)}, u32[]{:S(2)}) copy-start(f32[2560]{0:T(1024)} %param.34) | copy-start | bytes 30724
  363.7 3.8 %copy-start.1 = (bf16[320,2560]{1,0:T(8,128)(2,1)S(1)}, bf16[320,2560]{1,0:T(8,128)(2,1)}, u32[]{:S(2)}) copy-start(bf16[320,2560]{1,0:T(8,128)(2,1)} %param.33) | copy-start | bytes 4915204
  (18 other events, 24.0 us)
Sparse Core Ops, SparseCore 0:
  9.2 46.1 all-gather.1
  148.9 128.3 all-reduce.2
  298.8 64.8 reduce-scatter.3

commit v4 on v3

--- a/solution.py
+++ b/solution.py
@@ -45,6 +45,13 @@
         upto = join_packed(older, upto)
         stride *= 4
     return before
+
+
+def sum_partials(rows):
+    count = lax.axis_size("tp")
+    parts = lax.all_to_all(rows, "tp", 0, 0, tiled=True)
+    parts = parts.reshape((count, -1) + rows.shape[1:]).astype(jnp.float32)
+    return jnp.sum(parts, axis=0)
 
 
 def rms_rows(values, gain):
@@ -146,25 +153,21 @@
     extra = extra.at[:, 0].set(squares_hi).at[:, 1].set(squares_lo)
     piece = (gated * ssm_gain).astype(jnp.bfloat16)
     product = jnp.dot(piece, w_out, preferred_element_type=jnp.float32).astype(jnp.bfloat16)
-    reduced = lax.psum(jnp.concatenate([product, extra], axis=1), "tp")
+    reduced = sum_partials(jnp.concatenate([product, extra], axis=1))
     width = w_out.shape[1]
-    squares_all = reduced[:, width].astype(jnp.float32) + reduced[:, width + 1].astype(jnp.float32)
-    scale = lax.rsqrt(squares_all / (HEADS * HEAD_DIM) + EPS)
-    mixer_all = reduced[:, :width].astype(jnp.float32) * scale[:, None]
-    resid_all = (gathered.astype(jnp.float32) + mixer_all).astype(jnp.bfloat16)
-    mlp_in = rms_rows(resid_all, norm2_gain).astype(jnp.bfloat16)
-    own_rows = tokens.shape[0]
-    resid = lax.dynamic_slice_in_dim(resid_all, lax.axis_index("tp") * own_rows, own_rows, 0)
+    squares_own = reduced[:, width] + reduced[:, width + 1]
+    scale = lax.rsqrt(squares_own / (HEADS * HEAD_DIM) + EPS)
+    mixer_own = reduced[:, :width] * scale[:, None]
+    resid = (tokens.astype(jnp.float32) + mixer_own).astype(jnp.bfloat16)
+    normed_own = rms_rows(resid, norm2_gain).astype(jnp.bfloat16)
+    mlp_in = lax.all_gather(normed_own, "tp", axis=0, tiled=True)
     mlp_gate = jnp.dot(mlp_in, w_gate, preferred_element_type=jnp.float32)
     mlp_up = jnp.dot(mlp_in, w_up, preferred_element_type=jnp.float32)
     hidden = (jax.nn.silu(mlp_gate) * mlp_up).astype(jnp.bfloat16)
     piece = hidden
-    mlp_down = lax.psum_scatter(
-        jnp.dot(piece, w_down, preferred_element_type=jnp.float32).astype(jnp.bfloat16),
-        "tp",
-        scatter_dimension=0,
-        tiled=True,
-    ).astype(jnp.float32)
+    mlp_down = sum_partials(
+        jnp.dot(piece, w_down, preferred_element_type=jnp.float32).astype(jnp.bfloat16)
+    )
     return (resid.astype(jnp.float32) + mlp_down).astype(jnp.bfloat16)
 
 

time: 375 us -> 461 us (1.23)
  blocking collectives: 0 us -> 249 us
  waiting for transfers between devices: 245 us -> 95.3 us
  local copies, waits for them, and re-layouts: 25.4 us -> 11.8 us
    all_to_all x0 -> x2, blocking collectives: none -> 249 us  [sum_partials(): parts = lax.all_to_all(rows, 'tp', 0, 0, tiled=True)]
    psum x1 -> x0, waiting for transfers between devices: 128 us -> none  [local(): reduced = lax.psum(jnp.concatenate([product, extra], axis=1), 'tp')]
    unnamed x4 -> x2, waiting for transfers between devices: 65.8 us -> 0.73 us
    all_gather x0 -> x1, waiting for transfers between devices: none -> 38.4 us  [local(): mlp_in = lax.all_gather(normed_own, 'tp', axis=0, tiled=True)]
    all_gather x1 -> x0, local copies, waits for them, and re-layouts: 7.99 us -> none  [local(): gathered = lax.all_gather(tokens, 'tp', axis=0, tiled=True)]
    reduce_sum x2, other arithmetic: 9.74 us -> 4.01 us  [rms_rows(): jnp.mean(wide * wide, axis=-1, keepdims=True) + EPS]
    unnamed x84 -> x65, local copies, waits for them, and re-layouts: 8.22 us -> 3.01 us
  transfers between devices with their start and end apart: 10 -> 9, of which waited for: 5 -> 5; matrix products, arithmetic and copies ran while one was open for 4% -> 3% of each run, Pallas kernels for 0% -> 0%
where the time goes in v4:
time: 461 us; the launch traced here: 458 us
  blocking collectives  249 us (54%)
  waiting for transfers between devices  95.3 us (21%)
  matrix products  42.4 us (9%)
  other arithmetic  27.2 us (6%)
  starting transfers between devices  17.9 us (4%)
  between operations  14 us (3%)
  local copies, waits for them, and re-layouts  11.8 us (3%)
    all_to_all x2, blocking collectives, sum_partials(): parts = lax.all_to_all(rows, 'tp', 0, 0, tiled=True)  249 us
    all_gather x1, waiting for transfers between devices, local(): gathered = lax.all_gather(tokens, 'tp', axis=0, tiled=True)  43.2 us
    all_gather x1, waiting for transfers between devices, local(): mlp_in = lax.all_gather(normed_own, 'tp', axis=0, tiled=True)  38.4 us
    ppermute x6, starting transfers between devices, shifted(): lax.ppermute(value, axis, [(source, source + steps) for source in range(c...  14.5 us
    dot_general x1, matrix products, local(): jnp.dot(piece, w_down, preferred_element_type=jnp.float32)  10 us
  transfers between devices with their start and end apart: 9, of which 5 were waited for; matrix products, arithmetic and copies ran while one was open for 3% of the time, Pallas kernels for 0%

profile of v4, /device:TPU:2, one launch (start us, length us, event | category | flops | bytes accessed | tf_op | source)
XLA Modules:
  0.0 457.7 jit_solution(14053518944985812004)
XLA Ops:
  12.1 43.2 %all-gather.3.cloned.1.call-done = bf16[1024,2560]{1,0:T(8,128)(2,1)} async-done(((bf16[64,2560]{1,0:T(8,128)(2,1)}), bf16[1024,2560]{1,0:T(8,128)(2,1)}) %all-gather.3.cloned.1.call-update) | async-done | bytes 5242896 | tf_op jit(solution)/shard_map/all_gather | solution.py:90
  55.3 3.7 fusion
  59.4 1.3 fusion.2
  60.7 1.5 negate_multiply_fusion
  64.3 4.6 %convolution_convert_fusion.3 = bf16[1024,256]{0,1:T(8,128)(2,1)S(1)} fusion(bf16[1024,2560]{1,0:T(8,128)(2,1)} %copy-done.2, bf16[2560,256]{1,0:T(8,128)(2,1)} %param.25), kind=kOutput, calls=%fused_computation.41 | convolution fusion | flops 1342439424 | bytes 7077888 | tf_op jit(solution)/shard_map/dot_general | solution.py:92
  69.0 1.9 convolution_convert_fusion.2
  71.1 3.4 collective-permute-start
  75.6 5.5 %collective-permute-done = bf16[3,576]{0,1:T(8,128)(2,1)S(1)} collective-permute-done((bf16[3,576]{0,1:T(8,128)(2,1)S(1)}, bf16[3,576]{0,1:T(8,128)(2,1)S(1)}, u32[]{:S(2)}, u32[]{:S(2)}) %collective-permute-start) | collective-permute-done | bytes 3488 | tf_op jit(solution)/shard_map/ppermute | solution.py:18
  81.3 1.1 multiply_convert_fusion.2
  83.8 2.5 fusion.44
  86.3 1.9 reshape.160
  88.2 2.7 fusion.23
  90.9 1.3 fusion.66
  93.0 2.5 collective-permute-start.3
  95.5 3.6 collective-permute-start.2
  99.1 3.0 collective-permute-start.1
  102.5 7.1 %fusion.16 = f32[4,256,5,64]{1,3,2,0:T(8,128)} fusion(f32[4,256,5]{1,2,0:T(8,128)S(1)} %copy-done.10, f32[4,256,256]{2,1,0:T(8,128)S(1)} %fusion.49, pred[256,256]{1,0:T(8,128)(4,1)S(1)} %copy-done.11, f32[4,256,5,64]{1,0,3,2:T(4,128)S(1)} %reshape.160, f32[4,256,5]{1,2,0:T(8,128)S(1)} %bitcast.118), kind=kOutput, calls=%fused_computation.25 | convolution fusion | flops 1012203520 | bytes 3776512 | tf_op jit(solution)/shard_map/btsh,bshp->bthp/dot_general | solution.py:121
  109.7 1.4 collective-permute-done.1
  112.6 1.5 multiply_add_fusion
  114.1 2.8 collective-permute-start.5
  116.9 1.2 multiply_add_fusion.1
  118.8 1.9 collective-permute-start.4
  120.7 6.1 %collective-permute-done.4 = f32[5,65,128]{2,1,0:T(8,128)S(1)} collective-permute-done((f32[5,65,128]{2,1,0:T(8,128)S(1)}, f32[5,65,128]{2,1,0:T(8,128)S(1)}, u32[]{:S(2)}, u32[]{:S(2)}) %collective-permute-start.4) | collective-permute-done | bytes 166432 | tf_op jit(solution)/shard_map/ppermute | solution.py:23
  130.3 3.1 multiply_reduce_fusion
  133.7 2.1 fusion.48
  135.8 5.0 %convolution_convert_fusion.1 = bf16[1024,2560]{1,0:T(8,128)(2,1)} fusion(bf16[320,2560]{1,0:T(8,128)(2,1)S(1)} %copy-done, f32[320]{0:T(512)S(1)} %copy-done.24, f32[1024,320]{0,1:T(8,128)S(1)} %bitcast.114, f32[1024,320]{0,1:T(8,128)S(1)} %copy-done.25), kind=kOutput, calls=%fused_computation.8 | convolution fusion | flops 1682636800 | bytes 9504000 | tf_op jit(solution)/shard_map/dot_general | solution.py:155
  141.8 2.9 pad_maximum_fusion
  144.6 127.6 %all_to_all.18 = bf16[16,64,2688]{2,1,0:T(8,128)(2,1)S(1)} all-to-all(bf16[16,64,2688]{2,1,0:T(8,128)(2,1)S(1)} %bitcast.108), channel_id=1, replica_groups=mesh['ctx'=16,'tp'=16] {'tp'}, dimensions={0} | all-to-all | bytes 11010048 | tf_op jit(solution)/shard_map/all_to_all | solution.py:52
  274.6 38.4 %all-gather.5.cloned.1.call-done = bf16[1024,2560]{1,0:T(8,128)(2,1)} async-done(((bf16[64,2560]{1,0:T(8,128)(2,1)}), bf16[1024,2560]{1,0:T(8,128)(2,1)}) %all-gather.5.cloned.1.call-update) | async-done | bytes 5242896 | tf_op jit(solution)/shard_map/all_gather | solution.py:163
  313.0 4.9 %fusion.89 = f32[1024,320]{0,1:T(8,128)S(1)} fusion(bf16[1024,2560]{1,0:T(8,128)(2,1)} %all-gather.5.cloned.1.call-done, bf16[2560,320]{0,1:T(8,128)(2,1)} %param.35), kind=kOutput, calls=%fused_computation.165 | convolution fusion | flops 1677721600 | bytes 8192000 | tf_op jit(solution)/shard_map/dot_general | solution.py:164
  317.9 10.0 %convolution_convert_fusion = bf16[1024,2560]{1,0:T(8,128)(2,1)} fusion(bf16[320,2560]{1,0:T(8,128)(2,1)S(1)} %copy-done.23, bf16[1024,2560]{1,0:T(8,128)(2,1)} %all-gather.5.cloned.1.call-done, bf16[2560,320]{0,1:T(8,128)(2,1)} %param.36, f32[1024,320]{0,1:T(8,128)S(1)} %fusion.89), kind=kOutput, calls=%fused_computation.7 | convolution fusion | flops 3360030720 | bytes 15073280 | tf_op jit(solution)/shard_map/dot_general | solution.py:169
  327.9 121.4 %all_to_all.19 = bf16[16,64,2560]{2,1,0:T(8,128)(2,1)S(1)} all-to-all(bf16[16,64,2560]{2,1,0:T(8,128)(2,1)} %bitcast.109), channel_id=1, replica_groups=mesh['ctx'=16,'tp'=16] {'tp'}, dimensions={0} | all-to-all | bytes 10485760 | tf_op jit(solution)/shard_map/all_to_all | solution.py:52
  (122 shorter events, 22.8 us)
Async XLA Ops:
  6.5 129.3 %copy-start = (bf16[320,2560]{1,0:T(8,128)(2,1)S(1)}, bf16[320,2560]{1,0:T(8,128)(2,1)}, u32[]{:S(2)}) copy-start(bf16[320,2560]{1,0:T(8,128)(2,1)} %param.33) | copy-start | bytes 4915204
  6.5 48.8 %all-gather.3.cloned.1.call-start = ((), (), s32[]{:S(2)}) async-start(), calls=%async_computation.2 | async-start | bytes 5570560 | tf_op jit(solution)/shard_map/all_gather | solution.py:90
  7.3 305.7 %all-gather.5.cloned.1.call-start = ((), (), s32[]{:S(2)}) async-start(), calls=%async_computation.3 | async-start | bytes 5570560 | tf_op jit(solution)/shard_map/all_gather | solution.py:163
  12.1 47.0 %copy-start.13 = (f32[2560]{0:T(1024)S(1)}, f32[2560]{0:T(1024)}, u32[]{:S(2)}) copy-start(f32[2560]{0:T(1024)} %param.22) | copy-start | bytes 30724
  55.3 4.0 copy-start.3
  60.7 2.3 copy-start.2
  63.0 6.0 %slice-start = ((s8[5242880]{0:T(1024)(128)(4,1)}), s8[1048576]{0:T(1024)(128)(4,1)S(1)}, s32[]{:S(2)}) async-start(s8[5242880]{0:T(1024)(128)(4,1)} %bitcast.104), calls=%async_computation.4 | async-start | bytes 2097152
  63.3 5.6 %copy-start.9 = (f32[4,256,5]{1,2,0:T(8,128)}, f32[4,256,5]{1,2,0:T(8,128)S(1)}, u32[]{:S(2)}) copy-start(f32[4,256,5]{1,2,0:T(8,128)S(1)} %convolution_bitcast_fusion) | copy-start | bytes 61444
  63.5 11.5 %copy-start.16 = (f32[5]{0:T(128)}, f32[5]{0:T(128)S(1)}, u32[]{:S(2)}) copy-start(f32[5]{0:T(128)S(1)} %get-tuple-element.29) | copy-start | bytes 64
  64.3 4.7 %slice-start.1 = ((s8[5242880]{0:T(1024)(128)(4,1)}), s8[4194304]{0:T(1024)(128)(4,1)S(1)}, s32[]{:S(2)}) async-start(s8[5242880]{0:T(1024)(128)(4,1)} %bitcast.104), calls=%async_computation.5 | async-start | bytes 8388608
  64.3 4.7 %copy-start.21 = (bf16[2560,320]{0,1:T(8,128)(2,1)S(1)}, bf16[2560,320]{0,1:T(8,128)(2,1)}, u32[]{:S(2)}) copy-start(bf16[2560,320]{0,1:T(8,128)(2,1)} %param.24) | copy-start | bytes 4915204
  70.9 10.4 %copy-start.7 = (bf16[1024,320]{0,1:T(8,128)(2,1)}, bf16[1024,320]{0,1:T(8,128)(2,1)S(1)}, u32[]{:S(2)}) copy-start(bf16[1024,320]{0,1:T(8,128)(2,1)S(1)} %convolution_convert_fusion.2) | copy-start | bytes 1966084
  71.1 10.0 %collective-permute-start = (bf16[3,576]{0,1:T(8,128)(2,1)S(1)}, bf16[3,576]{0,1:T(8,128)(2,1)S(1)}, u32[]{:S(2)}, u32[]{:S(2)}) collective-permute-start(bf16[3,576]{0,1:T(8,128)(2,1)S(1)} %pad_maximum_fusion.3), channel_id=1, source_target_pairs={{0,16},{16,32},{32,48},{48,64},{64,80},{80,96},{96,112},{112,128},... | collective-permute-start | bytes 10376 | tf_op jit(solution)/shard_map/ppermute | solution.py:18
  88.2 2.7 copy-start.15
  88.2 4.0 copy-start.17
  90.9 11.6 %copy-start.10 = (f32[4,256,5]{1,2,0:T(8,128)S(1)}, f32[4,256,5]{1,2,0:T(8,128)}, u32[]{:S(2)}) copy-start(f32[4,256,5]{1,2,0:T(8,128)} %copy-done.9) | copy-start | bytes 61444
  90.9 11.6 %copy-start.11 = (pred[256,256]{1,0:T(8,128)(4,1)S(1)}, pred[256,256]{1,0:T(8,128)(4,1)}, u32[]{:S(2)}) copy-start(pred[256,256]{1,0:T(8,128)(4,1)} %iota_compare_fusion) | copy-start | bytes 196612
  93.0 16.8 %collective-permute-start.3 = (f32[5,65,128]{2,1,0:T(8,128)}, f32[5,65,128]{2,1,0:T(8,128)}, u32[]{:S(2)}, u32[]{:S(2)}) collective-permute-start(f32[5,65,128]{2,1,0:T(8,128)} %pad_maximum_fusion.1), channel_id=1, source_target_pairs={{0,48},{16,64},{32,80},{48,96},{64,112},{80,128},{96,144},{112,160... | collective-permute-start | bytes 499208 | tf_op jit(solution)/shard_map/ppermute | solution.py:23
  95.5 14.2 %collective-permute-start.2 = (f32[5,65,128]{2,1,0:T(8,128)}, f32[5,65,128]{2,1,0:T(8,128)}, u32[]{:S(2)}, u32[]{:S(2)}) collective-permute-start(f32[5,65,128]{2,1,0:T(8,128)} %pad_maximum_fusion.1), channel_id=1, source_target_pairs={{0,32},{16,48},{32,64},{48,80},{64,96},{80,112},{96,128},{112,144}... | collective-permute-start | bytes 499208 | tf_op jit(solution)/shard_map/ppermute | solution.py:23
  99.1 12.0 %collective-permute-start.1 = (f32[5,65,128]{2,1,0:T(8,128)}, f32[5,65,128]{2,1,0:T(8,128)}, u32[]{:S(2)}, u32[]{:S(2)}) collective-permute-start(f32[5,65,128]{2,1,0:T(8,128)} %pad_maximum_fusion.1), channel_id=1, source_target_pairs={{0,16},{16,32},{32,48},{48,64},{64,80},{80,96},{96,112},{112,128},... | collective-permute-start | bytes 499208 | tf_op jit(solution)/shard_map/ppermute | solution.py:23
  114.0 12.9 %copy-start.5 = (f32[4,256,5,64]{1,3,2,0:T(8,128)S(1)}, f32[4,256,5,64]{1,3,2,0:T(8,128)}, u32[]{:S(2)}) copy-start(f32[4,256,5,64]{1,3,2,0:T(8,128)} %fusion.16) | copy-start | bytes 3932164
  114.0 12.9 %copy-start.19 = (f32[5]{0:T(128)S(1)}, f32[5]{0:T(128)}, u32[]{:S(2)}) copy-start(f32[5]{0:T(128)} %param.31) | copy-start | bytes 64
  114.1 12.9 %copy-start.20 = (f32[4]{0:T(128)S(1)}, f32[4]{0:T(128)}, u32[]{:S(2)}) copy-start(f32[4]{0:T(128)} %pad.11.clone) | copy-start | bytes 52
  114.1 6.6 %collective-permute-start.5 = (f32[5,65,128]{2,1,0:T(8,128)S(1)}, f32[5,65,128]{2,1,0:T(8,128)S(1)}, u32[]{:S(2)}, u32[]{:S(2)}) collective-permute-start(f32[5,65,128]{2,1,0:T(8,128)S(1)} %pad_maximum_fusion.2), channel_id=1, source_target_pairs={{0,128},{16,144},{32,160},{48,176},{64,192},{80,208},{96,224},{112... | collective-permute-start | bytes 499208 | tf_op jit(solution)/shard_map/ppermute | solution.py:23
  118.1 8.8 %collective-permute-start.6 = (f32[5,65,128]{2,1,0:T(8,128)S(1)}, f32[5,65,128]{2,1,0:T(8,128)S(1)}, u32[]{:S(2)}, u32[]{:S(2)}) collective-permute-start(f32[5,65,128]{2,1,0:T(8,128)S(1)} %pad_maximum_fusion.2), channel_id=1, source_target_pairs={{0,192},{16,208},{32,224},{48,240},{1,193},{17,209},{33,225},{49,2... | collective-permute-start | bytes 499208 | tf_op jit(solution)/shard_map/ppermute | solution.py:23
  118.8 8.1 %collective-permute-start.4 = (f32[5,65,128]{2,1,0:T(8,128)S(1)}, f32[5,65,128]{2,1,0:T(8,128)S(1)}, u32[]{:S(2)}, u32[]{:S(2)}) collective-permute-start(f32[5,65,128]{2,1,0:T(8,128)S(1)} %pad_maximum_fusion.2), channel_id=1, source_target_pairs={{0,64},{16,80},{32,96},{48,112},{64,128},{80,144},{96,160},{112,17... | collective-permute-start | bytes 499208 | tf_op jit(solution)/shard_map/ppermute | solution.py:23
  126.9 2.3 slice-start.2
  127.0 2.4 slice-start.3
  133.4 2.4 copy-start.24
  133.7 2.2 copy-start.25
  135.8 5.0 %copy-start.6 = (bf16[1024,1]{1,0:T(8,128)(2,1)S(1)}, bf16[1024,1]{1,0:T(8,128)(2,1)}, u32[]{:S(2)}) copy-start(bf16[1024,1]{1,0:T(8,128)(2,1)} %get-tuple-element.44) | copy-start | bytes 6148
  274.6 43.2 %copy-start.23 = (bf16[320,2560]{1,0:T(8,128)(2,1)S(1)}, bf16[320,2560]{1,0:T(8,128)(2,1)}, u32[]{:S(2)}) copy-start(bf16[320,2560]{1,0:T(8,128)(2,1)} %param.37) | copy-start | bytes 4915204
  (7 other events, 8.3 us)
Sparse Core Ops, SparseCore 0:
  9.2 46.1 all-gather.2
  274.7 38.1 all-gather.4

commit v5 on v1

--- a/solution.py
+++ b/solution.py
@@ -61,11 +61,6 @@
     return result
 
 
-def carry_step(state, pieces):
-    decay_now, fresh = pieces
-    return (decay_now[:, None, None] * state + fresh, state)
-
-
 def local(
     tokens,
     norm1_gain,
@@ -103,7 +98,8 @@
     block_count = group_len // BLOCK_LEN
     log_blocks = log_decay.reshape(block_count, BLOCK_LEN, head_count)
     step_blocks = dt_step.reshape(block_count, BLOCK_LEN, head_count)
-    cum_decay = jnp.cumsum(log_blocks, axis=1)
+    lower = jnp.tril(jnp.ones((BLOCK_LEN, BLOCK_LEN), jnp.float32))
+    cum_decay = jnp.einsum("ts,bsh->bth", lower, log_blocks, precision=lax.Precision.HIGHEST)
     b_mat = conv_bcm[:, :STATE_DIM].reshape(block_count, BLOCK_LEN, STATE_DIM)
     c_mat = conv_bcm[:, STATE_DIM:].reshape(block_count, BLOCK_LEN, STATE_DIM)
     scores = jnp.einsum("btn,bsn->bts", c_mat, b_mat, preferred_element_type=jnp.float32)
@@ -125,7 +121,12 @@
     )
     block_decay = jnp.exp(block_last)
     zero_state = jnp.zeros((head_count, HEAD_DIM, STATE_DIM), jnp.float32)
-    local_final, local_in = lax.scan(carry_step, zero_state, (block_decay, block_states))
+    running = zero_state
+    entering = []
+    for block in range(block_count):
+        entering.append(running)
+        running = block_decay[block][:, None, None] * running + block_states[block]
+    local_final, local_in = running, jnp.stack(entering)
     total_log = jnp.sum(block_last, axis=0)
     prior_decay = jnp.exp(jnp.cumsum(block_last, axis=0) - block_last)
     packed = jnp.concatenate(
@@ -141,8 +142,9 @@
     squares = jnp.sum(gated * gated, axis=-1)
     squares_hi = squares.astype(jnp.bfloat16)
     squares_lo = (squares - squares_hi.astype(jnp.float32)).astype(jnp.bfloat16)
-    extra = jnp.zeros((group_len, 128), jnp.bfloat16)
-    extra = extra.at[:, 0].set(squares_hi).at[:, 1].set(squares_lo)
+    extra = jnp.concatenate(
+        [squares_hi[:, None], squares_lo[:, None], jnp.zeros((group_len, 126), jnp.bfloat16)], axis=1
+    )
     piece = (gated * ssm_gain).astype(jnp.bfloat16)
     product = jnp.dot(piece, w_out, preferred_element_type=jnp.float32).astype(jnp.bfloat16)
     reduced = lax.psum_scatter(

time: 362 us -> 348 us (0.961)
  other arithmetic: 31.8 us -> 16.9 us
  local copies, waits for them, and re-layouts: 23 us -> 28.8 us
  waiting for transfers between devices: 229 us -> 225 us
    another operation x6 -> x0, other arithmetic: 9.58 us -> none
    concatenate x0 -> x1, local copies, waits for them, and re-layouts: none -> 9.16 us  [local(): jnp.concatenate([product, extra], axis=1)]
    ppermute x6, waiting for transfers between devices: 13.8 us -> 8.55 us  [shifted(): lax.ppermute(value, axis, [(source, source + steps) for source in range(c...]
    unnamed x60 -> x70, local copies, waits for them, and re-layouts: 7.89 us -> 6.76 us
where the time goes in v5:
time: 348 us; the launch traced here: 347 us
  waiting for transfers between devices  225 us (65%)
  matrix products  44.3 us (13%)
  local copies, waits for them, and re-layouts  28.8 us (8%)
  starting transfers between devices  18.3 us (5%)
  other arithmetic  16.9 us (5%)
  between operations  13.7 us (4%)
    unnamed x6, waiting for transfers between devices  125 us
    all_gather x1, waiting for transfers between devices, local(): gathered = lax.all_gather(tokens, 'tp', axis=0, tiled=True)  44.5 us
    all_gather x1, waiting for transfers between devices, local(): mlp_in = lax.all_gather(normed_own, 'tp', axis=0, tiled=True)  41.4 us
    ppermute x6, starting transfers between devices, shifted(): lax.ppermute(value, axis, [(source, source + steps) for source in range(c...  14.5 us
    dot_general x1, matrix products, local(): jnp.dot(piece, w_down, preferred_element_type=jnp.float32)  10.3 us
    concatenate x1, local copies, waits for them, and re-layouts, local(): jnp.concatenate([product, extra], axis=1)  9.16 us
    ppermute x6, waiting for transfers between devices, shifted(): lax.ppermute(value, axis, [(source, source + steps) for source in range(c...  8.55 us
    dot_general x1, matrix products, local(): jnp.einsum('btsh,bshp->bthp', mixed_w, scaled, precision=lax.Precision.HI...  7.07 us
  transfers between devices with their start and end apart: 11, of which 8 were waited for; matrix products, arithmetic and copies ran while one was open for 4% of the time, Pallas kernels for 0%

profile of v5, /device:TPU:2, one launch (start us, length us, event | category | flops | bytes accessed | tf_op | source)
XLA Modules:
  0.0 347.2 jit_solution(3456935286433493581)
XLA Ops:
  10.9 44.5 %all-gather.3.cloned.1.call-done = bf16[1024,2560]{1,0:T(8,128)(2,1)} async-done(((bf16[64,2560]{1,0:T(8,128)(2,1)}), bf16[1024,2560]{1,0:T(8,128)(2,1)}) %all-gather.3.cloned.1.call-update) | async-done | bytes 5242896 | tf_op jit(solution)/shard_map/all_gather | solution.py:83
  55.3 3.7 %fusion = f32[1024]{0:T(1024)S(1)} fusion(bf16[1024,2560]{1,0:T(8,128)(2,1)} %all-gather.3.cloned.1.call-done), kind=kLoop, calls=%fused_computation.2 | loop fusion | flops 7863296 | bytes 5246976 | tf_op jit(solution)/shard_map/reduce_sum | solution.py:52
  59.4 1.3 fusion.2
  60.7 1.5 negate_multiply_fusion
  64.3 4.6 %convolution_convert_fusion.3 = bf16[1024,256]{0,1:T(8,128)(2,1)S(1)} fusion(bf16[1024,2560]{1,0:T(8,128)(2,1)} %copy-done.2, bf16[2560,256]{1,0:T(8,128)(2,1)} %param.21), kind=kOutput, calls=%fused_computation.46 | convolution fusion | flops 1342439424 | bytes 7077888 | tf_op jit(solution)/shard_map/dot_general | solution.py:85
  69.0 1.9 convolution_convert_fusion.2
  71.1 3.4 collective-permute-start
  75.7 5.4 %collective-permute-done = bf16[3,576]{0,1:T(8,128)(2,1)S(1)} collective-permute-done((bf16[3,576]{0,1:T(8,128)(2,1)S(1)}, bf16[3,576]{0,1:T(8,128)(2,1)S(1)}, u32[]{:S(2)}, u32[]{:S(2)}) %collective-permute-start) | collective-permute-done | bytes 3488 | tf_op jit(solution)/shard_map/ppermute | solution.py:18
  81.3 1.1 multiply_convert_fusion.2
  83.8 2.4 fusion.42
  86.3 1.9 reshape.106
  88.2 1.8 fusion.27
  91.7 2.5 collective-permute-start.3
  94.3 3.6 %collective-permute-start.2 = (f32[5,65,128]{2,1,0:T(8,128)}, f32[5,65,128]{2,1,0:T(8,128)}, u32[]{:S(2)}, u32[]{:S(2)}) collective-permute-start(f32[5,65,128]{2,1,0:T(8,128)} %pad_maximum_fusion), channel_id=1, source_target_pairs={{0,32},{16,48},{32,64},{48,80},{64,96},{80,112},{96,128},{112,144}... | collective-permute-start | bytes 499208 | tf_op jit(solution)/shard_map/ppermute | solution.py:23
  97.9 3.0 collective-permute-start.1
  101.3 7.1 %fusion.16 = f32[4,256,5,64]{1,3,2,0:T(8,128)} fusion(f32[4,256,5]{1,2,0:T(8,128)S(1)} %copy-done.11, f32[4,256,256]{2,1,0:T(8,128)S(1)} %fusion.46, pred[256,256]{1,0:T(8,128)(4,1)S(1)} %copy-done.12, f32[4,256,5,64]{1,0,3,2:T(4,128)S(1)} %reshape.106, f32[4,256,5]{1,2,0:T(8,128)S(1)} %bitcast.118), kind=kOutput, calls=%fused_computation.25 | convolution fusion | flops 1012203520 | bytes 3776512 | tf_op jit(solution)/shard_map/btsh,bshp->bthp/dot_general | solution.py:114
  108.6 1.4 collective-permute-done.1
  111.4 1.5 multiply_add_fusion
  112.9 2.8 collective-permute-start.5
  116.5 1.9 collective-permute-start.4
  118.8 6.8 %collective-permute-done.4 = f32[5,65,128]{2,1,0:T(8,128)S(1)} collective-permute-done((f32[5,65,128]{2,1,0:T(8,128)S(1)}, f32[5,65,128]{2,1,0:T(8,128)S(1)}, u32[]{:S(2)}, u32[]{:S(2)}) %collective-permute-start.4) | collective-permute-done | bytes 166432 | tf_op jit(solution)/shard_map/ppermute | solution.py:23
  129.1 3.1 multiply_reduce_fusion
  132.6 6.3 %convolution_convert_fusion.1 = bf16[1024,2560]{1,0:T(8,128)(2,1)} fusion(bf16[320,2560]{1,0:T(8,128)(2,1)S(1)} %copy-done, f32[320]{0:T(512)S(1)} %copy-done.25, f32[1024,320]{0,1:T(8,128)S(1)} %bitcast.114, f32[1024,320]{0,1:T(8,128)} %get-tuple-element.41), kind=kOutput, calls=%fused_computation.6 | convolution fusion | flops 1682636800 | bytes 9504000 | tf_op jit(solution)/shard_map/dot_general | solution.py:149
  139.0 9.2 %concatenate.23 = bf16[1024,2688]{1,0:T(8,128)(2,1)} concatenate(bf16[1024,2560]{1,0:T(8,128)(2,1)} %convolution_convert_fusion.1, bf16[1024,1]{1,0:T(8,128)(2,1)S(1)} %copy.83, bf16[1024,1]{1,0:T(8,128)(2,1)S(1)} %copy.84, bf16[1024,126]{1,0:T(8,128)(2,1)S(1)} %broadcast_in_dim.64), dimensions={1} | concatenate | bytes 11010048 | tf_op jit(solution)/shard_map/concatenate | solution.py:151
  149.5 60.6 %reduce-scatter.7.cloned.1.call-done = bf16[64,2688]{1,0:T(8,128)(2,1)} async-done(((bf16[1024,2688]{1,0:T(8,128)(2,1)}), bf16[64,2688]{1,0:T(8,128)(2,1)}) %reduce-scatter.7.cloned.1.call-update) | async-done | bytes 344080
  214.6 41.4 %all-gather.5.cloned.1.call-done = bf16[1024,2560]{1,0:T(8,128)(2,1)} async-done(((bf16[64,2560]{1,0:T(8,128)(2,1)}), bf16[1024,2560]{1,0:T(8,128)(2,1)}) %all-gather.5.cloned.1.call-update) | async-done | bytes 5242896 | tf_op jit(solution)/shard_map/all_gather | solution.py:159
  256.0 5.9 %fusion.82 = f32[1024,320]{0,1:T(8,128)} fusion(bf16[1024,2560]{1,0:T(8,128)(2,1)} %all-gather.5.cloned.1.call-done, bf16[2560,320]{0,1:T(8,128)(2,1)} %param.31), kind=kOutput, calls=%fused_computation.152 | convolution fusion | flops 1677721600 | bytes 8192000 | tf_op jit(solution)/shard_map/dot_general | solution.py:160
  261.9 10.3 %convolution_convert_fusion = bf16[1024,2560]{1,0:T(8,128)(2,1)} fusion(bf16[320,2560]{1,0:T(8,128)(2,1)S(1)} %copy-done.24, bf16[1024,2560]{1,0:T(8,128)(2,1)} %all-gather.5.cloned.1.call-done, bf16[2560,320]{0,1:T(8,128)(2,1)} %param.32, f32[1024,320]{0,1:T(8,128)} %fusion.82), kind=kOutput, calls=%fused_computation.5 | convolution fusion | flops 3360030720 | bytes 15073280 | tf_op jit(solution)/shard_map/dot_general | solution.py:165
  272.3 64.0 %reduce-scatter.9.cloned.1.call-done = bf16[64,2560]{1,0:T(8,128)(2,1)} async-done(((bf16[1024,2560]{1,0:T(8,128)(2,1)}), bf16[64,2560]{1,0:T(8,128)(2,1)}) %reduce-scatter.9.cloned.1.call-update) | async-done | bytes 327696
  336.2 1.4 copy.99
  337.6 1.0 fusion.23
  338.7 2.0 copy.88
  (132 shorter events, 24.1 us)
Async XLA Ops:
  6.5 126.1 %copy-start = (bf16[320,2560]{1,0:T(8,128)(2,1)S(1)}, bf16[320,2560]{1,0:T(8,128)(2,1)}, u32[]{:S(2)}) copy-start(bf16[320,2560]{1,0:T(8,128)(2,1)} %param.29) | copy-start | bytes 4915204
  6.5 48.8 %all-gather.3.cloned.1.call-start = ((), (), s32[]{:S(2)}) async-start(), calls=%async_computation.2 | async-start | bytes 5570560 | tf_op jit(solution)/shard_map/all_gather | solution.py:83
  7.3 202.9 %reduce-scatter.7.cloned.1.call-start = ((), (), s32[]{:S(2)}) async-start(), calls=%async_computation.4 | async-start | bytes 5849088
  10.9 48.2 %copy-start.14 = (f32[2560]{0:T(1024)S(1)}, f32[2560]{0:T(1024)}, u32[]{:S(2)}) copy-start(f32[2560]{0:T(1024)} %param.18) | copy-start | bytes 30724
  55.3 4.0 %copy-start.3 = (bf16[1024,2560]{1,0:T(8,128)(2,1)S(1)}, bf16[1024,2560]{1,0:T(8,128)(2,1)}, u32[]{:S(2)}) copy-start(bf16[1024,2560]{1,0:T(8,128)(2,1)} %all-gather.3.cloned.1.call-done) | copy-start | bytes 15728644
  63.0 6.0 %slice-start = ((s8[5242880]{0:T(1024)(128)(4,1)}), s8[1048576]{0:T(1024)(128)(4,1)S(1)}, s32[]{:S(2)}) async-start(s8[5242880]{0:T(1024)(128)(4,1)} %bitcast.106), calls=%async_computation.6 | async-start | bytes 2097152
  63.3 5.6 %copy-start.10 = (f32[4,256,5]{1,2,0:T(8,128)}, f32[4,256,5]{1,2,0:T(8,128)S(1)}, u32[]{:S(2)}) copy-start(f32[4,256,5]{1,2,0:T(8,128)S(1)} %convolution_bitcast_fusion) | copy-start | bytes 61444
  63.6 11.5 %copy-start.17 = (f32[5]{0:T(128)}, f32[5]{0:T(128)S(1)}, u32[]{:S(2)}) copy-start(f32[5]{0:T(128)S(1)} %get-tuple-element.5) | copy-start | bytes 64
  64.3 4.7 %slice-start.1 = ((s8[5242880]{0:T(1024)(128)(4,1)}), s8[4194304]{0:T(1024)(128)(4,1)S(1)}, s32[]{:S(2)}) async-start(s8[5242880]{0:T(1024)(128)(4,1)} %bitcast.106), calls=%async_computation.7 | async-start | bytes 8388608
  64.3 4.7 %copy-start.22 = (bf16[2560,320]{0,1:T(8,128)(2,1)S(1)}, bf16[2560,320]{0,1:T(8,128)(2,1)}, u32[]{:S(2)}) copy-start(bf16[2560,320]{0,1:T(8,128)(2,1)} %param.20) | copy-start | bytes 4915204
  71.0 10.4 %copy-start.8 = (bf16[1024,320]{0,1:T(8,128)(2,1)}, bf16[1024,320]{0,1:T(8,128)(2,1)S(1)}, u32[]{:S(2)}) copy-start(bf16[1024,320]{0,1:T(8,128)(2,1)S(1)} %convolution_convert_fusion.2) | copy-start | bytes 1966084
  71.1 10.0 %collective-permute-start = (bf16[3,576]{0,1:T(8,128)(2,1)S(1)}, bf16[3,576]{0,1:T(8,128)(2,1)S(1)}, u32[]{:S(2)}, u32[]{:S(2)}) collective-permute-start(bf16[3,576]{0,1:T(8,128)(2,1)S(1)} %pad_maximum_fusion.2), channel_id=1, source_target_pairs={{0,16},{16,32},{32,48},{48,64},{64,80},{80,96},{96,112},{112,128},... | collective-permute-start | bytes 10376 | tf_op jit(solution)/shard_map/ppermute | solution.py:18
  88.1 2.7 copy-start.16
  88.2 2.8 copy-start.18
  90.9 10.4 %copy-start.11 = (f32[4,256,5]{1,2,0:T(8,128)S(1)}, f32[4,256,5]{1,2,0:T(8,128)}, u32[]{:S(2)}) copy-start(f32[4,256,5]{1,2,0:T(8,128)} %copy-done.10) | copy-start | bytes 61444
  90.9 10.4 %copy-start.12 = (pred[256,256]{1,0:T(8,128)(4,1)S(1)}, pred[256,256]{1,0:T(8,128)(4,1)}, u32[]{:S(2)}) copy-start(pred[256,256]{1,0:T(8,128)(4,1)} %iota_compare_fusion) | copy-start | bytes 196612
  91.7 16.8 %collective-permute-start.3 = (f32[5,65,128]{2,1,0:T(8,128)}, f32[5,65,128]{2,1,0:T(8,128)}, u32[]{:S(2)}, u32[]{:S(2)}) collective-permute-start(f32[5,65,128]{2,1,0:T(8,128)} %pad_maximum_fusion), channel_id=1, source_target_pairs={{0,48},{16,64},{32,80},{48,96},{64,112},{80,128},{96,144},{112,160... | collective-permute-start | bytes 499208 | tf_op jit(solution)/shard_map/ppermute | solution.py:23
  94.3 14.3 %collective-permute-start.2 = (f32[5,65,128]{2,1,0:T(8,128)}, f32[5,65,128]{2,1,0:T(8,128)}, u32[]{:S(2)}, u32[]{:S(2)}) collective-permute-start(f32[5,65,128]{2,1,0:T(8,128)} %pad_maximum_fusion), channel_id=1, source_target_pairs={{0,32},{16,48},{32,64},{48,80},{64,96},{80,112},{96,128},{112,144}... | collective-permute-start | bytes 499208 | tf_op jit(solution)/shard_map/ppermute | solution.py:23
  97.9 12.0 %collective-permute-start.1 = (f32[5,65,128]{2,1,0:T(8,128)}, f32[5,65,128]{2,1,0:T(8,128)}, u32[]{:S(2)}, u32[]{:S(2)}) collective-permute-start(f32[5,65,128]{2,1,0:T(8,128)} %pad_maximum_fusion), channel_id=1, source_target_pairs={{0,16},{16,32},{32,48},{48,64},{64,80},{80,96},{96,112},{112,128},... | collective-permute-start | bytes 499208 | tf_op jit(solution)/shard_map/ppermute | solution.py:23
  108.5 7.2 %copy-start.5 = (f32[4,5,64,128]{3,2,1,0:T(8,128)S(1)}, f32[4,5,64,128]{3,2,1,0:T(8,128)}, u32[]{:S(2)}) copy-start(f32[4,5,64,128]{3,2,1,0:T(8,128)} %copy-done.4) | copy-start | bytes 1966084
  112.8 12.9 %copy-start.7 = (f32[4,256,5,64]{1,3,2,0:T(8,128)S(1)}, f32[4,256,5,64]{1,3,2,0:T(8,128)}, u32[]{:S(2)}) copy-start(f32[4,256,5,64]{1,3,2,0:T(8,128)} %fusion.16) | copy-start | bytes 3932164
  112.8 12.9 %copy-start.20 = (f32[5]{0:T(128)S(1)}, f32[5]{0:T(128)}, u32[]{:S(2)}) copy-start(f32[5]{0:T(128)} %param.27) | copy-start | bytes 64
  112.9 12.9 %copy-start.21 = (f32[4]{0:T(128)S(1)}, f32[4]{0:T(128)}, u32[]{:S(2)}) copy-start(f32[4]{0:T(128)} %pad.4.clone) | copy-start | bytes 52
  112.9 5.9 %collective-permute-start.5 = (f32[5,65,128]{2,1,0:T(8,128)S(1)}, f32[5,65,128]{2,1,0:T(8,128)S(1)}, u32[]{:S(2)}, u32[]{:S(2)}) collective-permute-start(f32[5,65,128]{2,1,0:T(8,128)S(1)} %pad_maximum_fusion.1), channel_id=1, source_target_pairs={{0,128},{16,144},{32,160},{48,176},{64,192},{80,208},{96,224},{112... | collective-permute-start | bytes 499208 | tf_op jit(solution)/shard_map/ppermute | solution.py:23
  115.8 9.8 %collective-permute-start.6 = (f32[5,65,128]{2,1,0:T(8,128)S(1)}, f32[5,65,128]{2,1,0:T(8,128)S(1)}, u32[]{:S(2)}, u32[]{:S(2)}) collective-permute-start(f32[5,65,128]{2,1,0:T(8,128)S(1)} %pad_maximum_fusion.1), channel_id=1, source_target_pairs={{0,192},{16,208},{32,224},{48,240},{1,193},{17,209},{33,225},{49,2... | collective-permute-start | bytes 499208 | tf_op jit(solution)/shard_map/ppermute | solution.py:23
  116.5 9.1 %collective-permute-start.4 = (f32[5,65,128]{2,1,0:T(8,128)S(1)}, f32[5,65,128]{2,1,0:T(8,128)S(1)}, u32[]{:S(2)}, u32[]{:S(2)}) collective-permute-start(f32[5,65,128]{2,1,0:T(8,128)S(1)} %pad_maximum_fusion.1), channel_id=1, source_target_pairs={{0,64},{16,80},{32,96},{48,112},{64,128},{80,144},{96,160},{112,17... | collective-permute-start | bytes 499208 | tf_op jit(solution)/shard_map/ppermute | solution.py:23
  125.8 2.4 slice-start.3
  129.1 3.6 %copy-start.25 = (f32[320]{0:T(512)S(1)}, f32[320]{0:T(512)}, u32[]{:S(2)}) copy-start(f32[320]{0:T(512)} %param.28) | copy-start | bytes 3844
  148.2 107.8 %all-gather.5.cloned.1.call-start = ((), (), s32[]{:S(2)}) async-start(), calls=%async_computation.3 | async-start | bytes 5570560 | tf_op jit(solution)/shard_map/all_gather | solution.py:159
  214.3 47.6 %copy-start.24 = (bf16[320,2560]{1,0:T(8,128)(2,1)S(1)}, bf16[320,2560]{1,0:T(8,128)(2,1)}, u32[]{:S(2)}) copy-start(bf16[320,2560]{1,0:T(8,128)(2,1)} %param.33) | copy-start | bytes 4915204
  214.3 121.9 %reduce-scatter.9.cloned.1.call-start = ((), (), s32[]{:S(2)}) async-start(), calls=%async_computation.5 | async-start | bytes 5570560
  336.2 4.5 %copy-start.1 = (bf16[320,2560]{1,0:T(8,128)(2,1)S(1)}, bf16[320,2560]{1,0:T(8,128)(2,1)}, u32[]{:S(2)}) copy-start(bf16[320,2560]{1,0:T(8,128)(2,1)} %param.29) | copy-start | bytes 4915204
  (9 other events, 12.2 us)
Sparse Core Ops, SparseCore 0:
  9.2 46.1 all-gather.2
  148.3 61.7 reduce-scatter.6
  214.4 41.4 all-gather.4
  272.4 63.7 reduce-scatter.8

commit v6 on v5

--- a/solution.py
+++ b/solution.py
@@ -142,15 +142,18 @@
     squares = jnp.sum(gated * gated, axis=-1)
     squares_hi = squares.astype(jnp.bfloat16)
     squares_lo = (squares - squares_hi.astype(jnp.float32)).astype(jnp.bfloat16)
+    width = w_out.shape[1]
+    pad_cols = 128
     extra = jnp.concatenate(
-        [squares_hi[:, None], squares_lo[:, None], jnp.zeros((group_len, 126), jnp.bfloat16)], axis=1
-    )
+        [squares_hi[:, None], squares_lo[:, None]], axis=1
+    ).astype(jnp.float32)
+    extra = jnp.pad(extra, ((0, 0), (width, pad_cols - 2)))
     piece = (gated * ssm_gain).astype(jnp.bfloat16)
-    product = jnp.dot(piece, w_out, preferred_element_type=jnp.float32).astype(jnp.bfloat16)
-    reduced = lax.psum_scatter(
-        jnp.concatenate([product, extra], axis=1), "tp", scatter_dimension=0, tiled=True
-    )
-    width = w_out.shape[1]
+    w_out_wide = jnp.pad(w_out, ((0, 0), (0, pad_cols)))
+    product = (jnp.dot(piece, w_out_wide, preferred_element_type=jnp.float32) + extra).astype(
+        jnp.bfloat16
+    )
+    reduced = lax.psum_scatter(product, "tp", scatter_dimension=0, tiled=True)
     squares_own = reduced[:, width].astype(jnp.float32) + reduced[:, width + 1].astype(jnp.float32)
     scale = lax.rsqrt(squares_own / (HEADS * HEAD_DIM) + EPS)
     mixer_own = reduced[:, :width].astype(jnp.float32) * scale[:, None]

time: 348 us -> 342 us (0.983)
  local copies, waits for them, and re-layouts: 28.8 us -> 19.7 us
    concatenate x1, local copies, waits for them, and re-layouts: 9.16 us -> 0.2 us  [local(): jnp.concatenate([squares_hi[:, None], squares_lo[:, None]], axis=1)]
    unnamed x70 -> x66, local copies, waits for them, and re-layouts: 6.76 us -> 7.16 us
where the time goes in v6:
time: 342 us; the launch traced here: 341 us
  waiting for transfers between devices  226 us (66%)
  matrix products  45.5 us (13%)
  local copies, waits for them, and re-layouts  19.7 us (6%)
  starting transfers between devices  18.3 us (5%)
  other arithmetic  18.1 us (5%)
  between operations  13.7 us (4%)
    unnamed x6, waiting for transfers between devices  125 us
    all_gather x1, waiting for transfers between devices, local(): gathered = lax.all_gather(tokens, 'tp', axis=0, tiled=True)  44.5 us
    all_gather x1, waiting for transfers between devices, local(): mlp_in = lax.all_gather(normed_own, 'tp', axis=0, tiled=True)  41.8 us
    ppermute x6, starting transfers between devices, shifted(): lax.ppermute(value, axis, [(source, source + steps) for source in range(c...  14.5 us
    dot_general x1, matrix products, local(): jnp.dot(piece, w_down, preferred_element_type=jnp.float32)  10.3 us
    ppermute x6, waiting for transfers between devices, shifted(): lax.ppermute(value, axis, [(source, source + steps) for source in range(c...  8.55 us
    dot_general x1, matrix products, local(): jnp.dot(piece, w_out_wide, preferred_element_type=jnp.float32) + extra  7.54 us
    unnamed x66, local copies, waits for them, and re-layouts  7.16 us
  transfers between devices with their start and end apart: 11, of which 8 were waited for; matrix products, arithmetic and copies ran while one was open for 4% of the time, Pallas kernels for 0%

profile of v6, /device:TPU:2, one launch (start us, length us, event | category | flops | bytes accessed | tf_op | source)
XLA Modules:
  0.0 340.9 jit_solution(10707998645141900073)
XLA Ops:
  10.9 44.5 %all-gather.3.cloned.1.call-done = bf16[1024,2560]{1,0:T(8,128)(2,1)} async-done(((bf16[64,2560]{1,0:T(8,128)(2,1)}), bf16[1024,2560]{1,0:T(8,128)(2,1)}) %all-gather.3.cloned.1.call-update) | async-done | bytes 5242896 | tf_op jit(solution)/shard_map/all_gather | solution.py:83
  55.3 3.7 %fusion = f32[1024]{0:T(1024)S(1)} fusion(bf16[1024,2560]{1,0:T(8,128)(2,1)} %all-gather.3.cloned.1.call-done), kind=kLoop, calls=%fused_computation.3 | loop fusion | flops 7863296 | bytes 5246976 | tf_op jit(solution)/shard_map/reduce_sum | solution.py:52
  59.4 1.3 fusion.2
  60.7 1.5 negate_multiply_fusion
  64.3 4.6 %convolution_convert_fusion.2 = bf16[1024,256]{0,1:T(8,128)(2,1)S(1)} fusion(bf16[1024,2560]{1,0:T(8,128)(2,1)} %copy-done.1, bf16[2560,256]{1,0:T(8,128)(2,1)} %param.21), kind=kOutput, calls=%fused_computation.47 | convolution fusion | flops 1342439424 | bytes 7077888 | tf_op jit(solution)/shard_map/dot_general | solution.py:85
  69.0 1.9 convolution_convert_fusion.1
  71.1 3.4 collective-permute-start
  75.5 5.6 %collective-permute-done = bf16[3,576]{0,1:T(8,128)(2,1)S(1)} collective-permute-done((bf16[3,576]{0,1:T(8,128)(2,1)S(1)}, bf16[3,576]{0,1:T(8,128)(2,1)S(1)}, u32[]{:S(2)}, u32[]{:S(2)}) %collective-permute-start) | collective-permute-done | bytes 3488 | tf_op jit(solution)/shard_map/ppermute | solution.py:18
  81.4 1.1 multiply_convert_fusion.2
  83.9 2.4 fusion.43
  86.3 1.9 reshape.106
  88.2 1.8 fusion.28
  91.8 2.5 collective-permute-start.3
  94.3 3.6 %collective-permute-start.2 = (f32[5,65,128]{2,1,0:T(8,128)}, f32[5,65,128]{2,1,0:T(8,128)}, u32[]{:S(2)}, u32[]{:S(2)}) collective-permute-start(f32[5,65,128]{2,1,0:T(8,128)} %pad_maximum_fusion), channel_id=1, source_target_pairs={{0,32},{16,48},{32,64},{48,80},{64,96},{80,112},{96,128},{112,144}... | collective-permute-start | bytes 499208 | tf_op jit(solution)/shard_map/ppermute | solution.py:23
  97.9 3.0 collective-permute-start.1
  101.3 7.1 %fusion.17 = f32[4,256,5,64]{1,3,2,0:T(8,128)} fusion(f32[4,256,5]{1,2,0:T(8,128)S(1)} %copy-done.10, f32[4,256,256]{2,1,0:T(8,128)S(1)} %fusion.47, pred[256,256]{1,0:T(8,128)(4,1)S(1)} %copy-done.11, f32[4,256,5,64]{1,0,3,2:T(4,128)S(1)} %reshape.106, f32[4,256,5]{1,2,0:T(8,128)S(1)} %bitcast.117), kind=kOutput, calls=%fused_computation.26 | convolution fusion | flops 1012203520 | bytes 3776512 | tf_op jit(solution)/shard_map/btsh,bshp->bthp/dot_general | solution.py:114
  108.6 1.4 collective-permute-done.1
  111.4 1.5 multiply_add_fusion
  112.9 2.8 collective-permute-start.5
  116.5 1.9 collective-permute-start.4
  118.8 6.8 %collective-permute-done.4 = f32[5,65,128]{2,1,0:T(8,128)S(1)} collective-permute-done((f32[5,65,128]{2,1,0:T(8,128)S(1)}, f32[5,65,128]{2,1,0:T(8,128)S(1)}, u32[]{:S(2)}, u32[]{:S(2)}) %collective-permute-start.4) | collective-permute-done | bytes 166432 | tf_op jit(solution)/shard_map/ppermute | solution.py:23
  129.1 3.2 multiply_reduce_fusion
  132.5 7.5 %add_convert_fusion = bf16[1024,2688]{1,0:T(8,128)(2,1)} fusion(bf16[1024,2]{1,0:T(8,128)(2,1)S(1)} %copy.81, bf16[320,2560]{1,0:T(8,128)(2,1)} %param.29, f32[320]{0:T(512)S(1)} %copy-done.23, f32[1024,320]{0,1:T(8,128)S(1)} %bitcast.113, f32[1024,320]{0,1:T(8,128)} %get-tuple-element.41), kind=kOutput, calls=%fused_computation.2 | convolution fusion | flops 1772158976 | bytes 9770240 | tf_op jit(solution)/shard_map/dot_general | solution.py:153
  141.4 60.4 %reduce-scatter.7.cloned.1.call-done = bf16[64,2688]{1,0:T(8,128)(2,1)} async-done(((bf16[1024,2688]{1,0:T(8,128)(2,1)}), bf16[64,2688]{1,0:T(8,128)(2,1)}) %reduce-scatter.7.cloned.1.call-update) | async-done | bytes 344080
  203.9 1.1 copy.102
  205.0 1.4 fusion.21
  207.9 41.8 %all-gather.5.cloned.1.call-done = bf16[1024,2560]{1,0:T(8,128)(2,1)} async-done(((bf16[64,2560]{1,0:T(8,128)(2,1)}), bf16[1024,2560]{1,0:T(8,128)(2,1)}) %all-gather.5.cloned.1.call-update) | async-done | bytes 5242896 | tf_op jit(solution)/shard_map/all_gather | solution.py:162
  249.7 5.9 %fusion.84 = f32[1024,320]{0,1:T(8,128)} fusion(bf16[1024,2560]{1,0:T(8,128)(2,1)} %all-gather.5.cloned.1.call-done, bf16[2560,320]{0,1:T(8,128)(2,1)} %param.31), kind=kOutput, calls=%fused_computation.155 | convolution fusion | flops 1677721600 | bytes 8192000 | tf_op jit(solution)/shard_map/dot_general | solution.py:163
  255.6 10.3 %convolution_convert_fusion = bf16[1024,2560]{1,0:T(8,128)(2,1)} fusion(bf16[320,2560]{1,0:T(8,128)(2,1)S(1)} %copy-done, bf16[1024,2560]{1,0:T(8,128)(2,1)} %all-gather.5.cloned.1.call-done, bf16[2560,320]{0,1:T(8,128)(2,1)} %param.32, f32[1024,320]{0,1:T(8,128)} %fusion.84), kind=kOutput, calls=%fused_computation.6 | convolution fusion | flops 3360030720 | bytes 15073280 | tf_op jit(solution)/shard_map/dot_general | solution.py:168
  266.0 64.0 %reduce-scatter.9.cloned.1.call-done = bf16[64,2560]{1,0:T(8,128)(2,1)} async-done(((bf16[1024,2560]{1,0:T(8,128)(2,1)}), bf16[64,2560]{1,0:T(8,128)(2,1)}) %reduce-scatter.9.cloned.1.call-update) | async-done | bytes 327696
  330.0 1.3 copy.96
  332.3 2.0 copy.85
  (126 shorter events, 23.9 us)
Async XLA Ops:
  6.5 249.1 %copy-start = (bf16[320,2560]{1,0:T(8,128)(2,1)S(1)}, bf16[320,2560]{1,0:T(8,128)(2,1)}, u32[]{:S(2)}) copy-start(bf16[320,2560]{1,0:T(8,128)(2,1)} %param.33) | copy-start | bytes 4915204
  6.5 48.8 %all-gather.3.cloned.1.call-start = ((), (), s32[]{:S(2)}) async-start(), calls=%async_computation.2 | async-start | bytes 5570560 | tf_op jit(solution)/shard_map/all_gather | solution.py:83
  7.3 194.6 %reduce-scatter.7.cloned.1.call-start = ((), (), s32[]{:S(2)}) async-start(), calls=%async_computation.4 | async-start | bytes 5849088
  10.9 48.2 %copy-start.13 = (f32[2560]{0:T(1024)S(1)}, f32[2560]{0:T(1024)}, u32[]{:S(2)}) copy-start(f32[2560]{0:T(1024)} %param.18) | copy-start | bytes 30724
  55.3 4.0 %copy-start.2 = (bf16[1024,2560]{1,0:T(8,128)(2,1)S(1)}, bf16[1024,2560]{1,0:T(8,128)(2,1)}, u32[]{:S(2)}) copy-start(bf16[1024,2560]{1,0:T(8,128)(2,1)} %all-gather.3.cloned.1.call-done) | copy-start | bytes 15728644
  60.7 2.3 copy-start.1
  63.0 6.0 %slice-start = ((s8[5242880]{0:T(1024)(128)(4,1)}), s8[1048576]{0:T(1024)(128)(4,1)S(1)}, s32[]{:S(2)}) async-start(s8[5242880]{0:T(1024)(128)(4,1)} %bitcast.105), calls=%async_computation.6 | async-start | bytes 2097152
  63.3 5.6 %copy-start.9 = (f32[4,256,5]{1,2,0:T(8,128)}, f32[4,256,5]{1,2,0:T(8,128)S(1)}, u32[]{:S(2)}) copy-start(f32[4,256,5]{1,2,0:T(8,128)S(1)} %convolution_bitcast_fusion) | copy-start | bytes 61444
  63.5 11.5 %copy-start.16 = (f32[5]{0:T(128)}, f32[5]{0:T(128)S(1)}, u32[]{:S(2)}) copy-start(f32[5]{0:T(128)S(1)} %get-tuple-element.5) | copy-start | bytes 64
  64.3 4.7 %slice-start.1 = ((s8[5242880]{0:T(1024)(128)(4,1)}), s8[4194304]{0:T(1024)(128)(4,1)S(1)}, s32[]{:S(2)}) async-start(s8[5242880]{0:T(1024)(128)(4,1)} %bitcast.105), calls=%async_computation.7 | async-start | bytes 8388608
  64.3 4.7 %copy-start.21 = (bf16[2560,320]{0,1:T(8,128)(2,1)S(1)}, bf16[2560,320]{0,1:T(8,128)(2,1)}, u32[]{:S(2)}) copy-start(bf16[2560,320]{0,1:T(8,128)(2,1)} %param.20) | copy-start | bytes 4915204
  71.0 10.4 %copy-start.7 = (bf16[1024,320]{0,1:T(8,128)(2,1)}, bf16[1024,320]{0,1:T(8,128)(2,1)S(1)}, u32[]{:S(2)}) copy-start(bf16[1024,320]{0,1:T(8,128)(2,1)S(1)} %convolution_convert_fusion.1) | copy-start | bytes 1966084
  71.1 10.0 %collective-permute-start = (bf16[3,576]{0,1:T(8,128)(2,1)S(1)}, bf16[3,576]{0,1:T(8,128)(2,1)S(1)}, u32[]{:S(2)}, u32[]{:S(2)}) collective-permute-start(bf16[3,576]{0,1:T(8,128)(2,1)S(1)} %pad_maximum_fusion.2), channel_id=1, source_target_pairs={{0,16},{16,32},{32,48},{48,64},{64,80},{80,96},{96,112},{112,128},... | collective-permute-start | bytes 10376 | tf_op jit(solution)/shard_map/ppermute | solution.py:18
  88.2 2.7 copy-start.15
  88.2 2.8 copy-start.17
  90.9 10.4 %copy-start.10 = (f32[4,256,5]{1,2,0:T(8,128)S(1)}, f32[4,256,5]{1,2,0:T(8,128)}, u32[]{:S(2)}) copy-start(f32[4,256,5]{1,2,0:T(8,128)} %copy-done.9) | copy-start | bytes 61444
  90.9 10.4 %copy-start.11 = (pred[256,256]{1,0:T(8,128)(4,1)S(1)}, pred[256,256]{1,0:T(8,128)(4,1)}, u32[]{:S(2)}) copy-start(pred[256,256]{1,0:T(8,128)(4,1)} %iota_compare_fusion) | copy-start | bytes 196612
  91.8 16.8 %collective-permute-start.3 = (f32[5,65,128]{2,1,0:T(8,128)}, f32[5,65,128]{2,1,0:T(8,128)}, u32[]{:S(2)}, u32[]{:S(2)}) collective-permute-start(f32[5,65,128]{2,1,0:T(8,128)} %pad_maximum_fusion), channel_id=1, source_target_pairs={{0,48},{16,64},{32,80},{48,96},{64,112},{80,128},{96,144},{112,160... | collective-permute-start | bytes 499208 | tf_op jit(solution)/shard_map/ppermute | solution.py:23
  94.3 14.3 %collective-permute-start.2 = (f32[5,65,128]{2,1,0:T(8,128)}, f32[5,65,128]{2,1,0:T(8,128)}, u32[]{:S(2)}, u32[]{:S(2)}) collective-permute-start(f32[5,65,128]{2,1,0:T(8,128)} %pad_maximum_fusion), channel_id=1, source_target_pairs={{0,32},{16,48},{32,64},{48,80},{64,96},{80,112},{96,128},{112,144}... | collective-permute-start | bytes 499208 | tf_op jit(solution)/shard_map/ppermute | solution.py:23
  97.9 12.0 %collective-permute-start.1 = (f32[5,65,128]{2,1,0:T(8,128)}, f32[5,65,128]{2,1,0:T(8,128)}, u32[]{:S(2)}, u32[]{:S(2)}) collective-permute-start(f32[5,65,128]{2,1,0:T(8,128)} %pad_maximum_fusion), channel_id=1, source_target_pairs={{0,16},{16,32},{32,48},{48,64},{64,80},{80,96},{96,112},{112,128},... | collective-permute-start | bytes 499208 | tf_op jit(solution)/shard_map/ppermute | solution.py:23
  108.5 7.2 %copy-start.4 = (f32[4,5,64,128]{3,2,1,0:T(8,128)S(1)}, f32[4,5,64,128]{3,2,1,0:T(8,128)}, u32[]{:S(2)}) copy-start(f32[4,5,64,128]{3,2,1,0:T(8,128)} %copy-done.3) | copy-start | bytes 1966084
  112.9 12.9 %copy-start.6 = (f32[4,256,5,64]{1,3,2,0:T(8,128)S(1)}, f32[4,256,5,64]{1,3,2,0:T(8,128)}, u32[]{:S(2)}) copy-start(f32[4,256,5,64]{1,3,2,0:T(8,128)} %fusion.17) | copy-start | bytes 3932164
  112.9 12.9 %copy-start.19 = (f32[5]{0:T(128)S(1)}, f32[5]{0:T(128)}, u32[]{:S(2)}) copy-start(f32[5]{0:T(128)} %param.27) | copy-start | bytes 64
  112.9 12.9 %copy-start.20 = (f32[4]{0:T(128)S(1)}, f32[4]{0:T(128)}, u32[]{:S(2)}) copy-start(f32[4]{0:T(128)} %pad.20.clone) | copy-start | bytes 52
  112.9 5.9 %collective-permute-start.5 = (f32[5,65,128]{2,1,0:T(8,128)S(1)}, f32[5,65,128]{2,1,0:T(8,128)S(1)}, u32[]{:S(2)}, u32[]{:S(2)}) collective-permute-start(f32[5,65,128]{2,1,0:T(8,128)S(1)} %pad_maximum_fusion.1), channel_id=1, source_target_pairs={{0,128},{16,144},{32,160},{48,176},{64,192},{80,208},{96,224},{112... | collective-permute-start | bytes 499208 | tf_op jit(solution)/shard_map/ppermute | solution.py:23
  115.9 9.8 %collective-permute-start.6 = (f32[5,65,128]{2,1,0:T(8,128)S(1)}, f32[5,65,128]{2,1,0:T(8,128)S(1)}, u32[]{:S(2)}, u32[]{:S(2)}) collective-permute-start(f32[5,65,128]{2,1,0:T(8,128)S(1)} %pad_maximum_fusion.1), channel_id=1, source_target_pairs={{0,192},{16,208},{32,224},{48,240},{1,193},{17,209},{33,225},{49,2... | collective-permute-start | bytes 499208 | tf_op jit(solution)/shard_map/ppermute | solution.py:23
  116.5 9.1 %collective-permute-start.4 = (f32[5,65,128]{2,1,0:T(8,128)S(1)}, f32[5,65,128]{2,1,0:T(8,128)S(1)}, u32[]{:S(2)}, u32[]{:S(2)}) collective-permute-start(f32[5,65,128]{2,1,0:T(8,128)S(1)} %pad_maximum_fusion.1), channel_id=1, source_target_pairs={{0,64},{16,80},{32,96},{48,112},{64,128},{80,144},{96,160},{112,17... | collective-permute-start | bytes 499208 | tf_op jit(solution)/shard_map/ppermute | solution.py:23
  125.8 2.4 slice-start.3
  129.1 3.4 %copy-start.23 = (f32[320]{0:T(512)S(1)}, f32[320]{0:T(512)}, u32[]{:S(2)}) copy-start(f32[320]{0:T(512)} %param.28) | copy-start | bytes 3844
  140.1 109.6 %all-gather.5.cloned.1.call-start = ((), (), s32[]{:S(2)}) async-start(), calls=%async_computation.3 | async-start | bytes 5570560 | tf_op jit(solution)/shard_map/all_gather | solution.py:162
  203.9 2.6 copy-start.14
  207.8 122.1 %reduce-scatter.9.cloned.1.call-start = ((), (), s32[]{:S(2)}) async-start(), calls=%async_computation.5 | async-start | bytes 5570560
  (7 other events, 9.2 us)
Sparse Core Ops, SparseCore 0:
  9.2 46.1 all-gather.2
  140.2 61.5 reduce-scatter.6
  207.9 41.7 all-gather.4
  266.1 63.8 reduce-scatter.8

commit v7 on v6

--- a/solution.py
+++ b/solution.py
@@ -159,18 +159,23 @@
     mixer_own = reduced[:, :width].astype(jnp.float32) * scale[:, None]
     resid = (tokens.astype(jnp.float32) + mixer_own).astype(jnp.bfloat16)
     normed_own = rms_rows(resid, norm2_gain).astype(jnp.bfloat16)
-    mlp_in = lax.all_gather(normed_own, "tp", axis=0, tiled=True)
-    mlp_gate = jnp.dot(mlp_in, w_gate, preferred_element_type=jnp.float32)
-    mlp_up = jnp.dot(mlp_in, w_up, preferred_element_type=jnp.float32)
-    hidden = (jax.nn.silu(mlp_gate) * mlp_up).astype(jnp.bfloat16)
-    piece = hidden
-    mlp_down = lax.psum_scatter(
-        jnp.dot(piece, w_down, preferred_element_type=jnp.float32).astype(jnp.bfloat16),
-        "tp",
-        scatter_dimension=0,
-        tiled=True,
-    ).astype(jnp.float32)
-    return (resid.astype(jnp.float32) + mlp_down).astype(jnp.bfloat16)
+    halves = 2
+    rows = normed_own.shape[0] // halves
+    outs = []
+    for half in range(halves):
+        own = slice(half * rows, (half + 1) * rows)
+        mlp_in = lax.all_gather(normed_own[own], "tp", axis=0, tiled=True)
+        mlp_gate = jnp.dot(mlp_in, w_gate, preferred_element_type=jnp.float32)
+        mlp_up = jnp.dot(mlp_in, w_up, preferred_element_type=jnp.float32)
+        hidden = (jax.nn.silu(mlp_gate) * mlp_up).astype(jnp.bfloat16)
+        mlp_down = lax.psum_scatter(
+            jnp.dot(hidden, w_down, preferred_element_type=jnp.float32).astype(jnp.bfloat16),
+            "tp",
+            scatter_dimension=0,
+            tiled=True,
+        ).astype(jnp.float32)
+        outs.append((resid[own].astype(jnp.float32) + mlp_down).astype(jnp.bfloat16))
+    return jnp.concatenate(outs, axis=0)
 
 
 def solution(mesh):

time: 342 us -> 427 us (1.25)
  waiting for transfers between devices: 226 us -> 300 us
  local copies, waits for them, and re-layouts: 19.7 us -> 24.6 us
    unnamed x6 -> x9, waiting for transfers between devices: 125 us -> 175 us
    all_gather x1 -> x2, waiting for transfers between devices: 41.8 us -> 68.7 us  [local(): mlp_in = lax.all_gather(normed_own[own], 'tp', axis=0, tiled=True)]
    dot_general x1 -> x2, matrix products: 10.3 us -> 12.6 us  [local(): jnp.dot(hidden, w_down, preferred_element_type=jnp.float32)]
    unnamed x66 -> x85, local copies, waits for them, and re-layouts: 7.16 us -> 9.37 us
  transfers between devices with their start and end apart: 11 -> 13, of which waited for: 8 -> 8; matrix products, arithmetic and copies ran while one was open for 4% -> 8% of each run, Pallas kernels for 0% -> 0%
where the time goes in v7:
time: 427 us; the launch traced here: 426 us
  waiting for transfers between devices  300 us (70%)
  matrix products  49.3 us (12%)
  local copies, waits for them, and re-layouts  24.6 us (6%)
  starting transfers between devices  19.3 us (5%)
  other arithmetic  18.5 us (4%)
  between operations  14.2 us (3%)
    unnamed x9, waiting for transfers between devices  175 us
    all_gather x2, waiting for transfers between devices, local(): mlp_in = lax.all_gather(normed_own[own], 'tp', axis=0, tiled=True)  68.7 us
    all_gather x1, waiting for transfers between devices, local(): gathered = lax.all_gather(tokens, 'tp', axis=0, tiled=True)  43.9 us
    ppermute x6, starting transfers between devices, shifted(): lax.ppermute(value, axis, [(source, source + steps) for source in range(c...  15.5 us
    dot_general x2, matrix products, local(): jnp.dot(hidden, w_down, preferred_element_type=jnp.float32)  12.6 us
    unnamed x85, local copies, waits for them, and re-layouts  9.37 us
  transfers between devices with their start and end apart: 13, of which 8 were waited for; matrix products, arithmetic and copies ran while one was open for 8% of the time, Pallas kernels for 0%

profile of v7, /device:TPU:2, one launch (start us, length us, event | category | flops | bytes accessed | tf_op | source)
XLA Modules:
  0.0 426.0 jit_solution(13787827623834736924)
XLA Ops:
  11.4 43.9 %all-gather.4.cloned.1.call-done = bf16[1024,2560]{1,0:T(8,128)(2,1)} async-done(((bf16[64,2560]{1,0:T(8,128)(2,1)}), bf16[1024,2560]{1,0:T(8,128)(2,1)}) %all-gather.4.cloned.1.call-update) | async-done | bytes 5242896 | tf_op jit(solution)/shard_map/all_gather | solution.py:83
  55.3 3.7 fusion
  60.7 2.3 negate_multiply_fusion
  64.7 5.0 %convolution_convert_fusion.2 = bf16[1024,320]{0,1:T(8,128)(2,1)S(1)} fusion(bf16[1024,2560]{1,0:T(8,128)(2,1)} %copy-done.1, bf16[2560,320]{0,1:T(8,128)(2,1)} %param.20), kind=kOutput, calls=%fused_computation.26 | convolution fusion | flops 1678049280 | bytes 7536640 | tf_op jit(solution)/shard_map/dot_general | solution.py:90
  69.9 1.6 convolution_convert_fusion.3
  71.6 3.4 collective-permute-start
  76.1 5.4 %collective-permute-done = bf16[3,576]{0,1:T(8,128)(2,1)S(1)} collective-permute-done((bf16[3,576]{0,1:T(8,128)(2,1)S(1)}, bf16[3,576]{0,1:T(8,128)(2,1)S(1)}, u32[]{:S(2)}, u32[]{:S(2)}) %collective-permute-start) | collective-permute-done | bytes 3488 | tf_op jit(solution)/shard_map/ppermute | solution.py:18
  82.2 2.5 fusion.53
  84.7 1.9 reshape.106
  89.4 1.8 fusion.26
  92.9 1.9 collective-permute-start.1
  94.8 4.0 collective-permute-start.2
  98.8 4.4 %collective-permute-start.3 = (f32[5,65,128]{2,1,0:T(8,128)}, f32[5,65,128]{2,1,0:T(8,128)}, u32[]{:S(2)}, u32[]{:S(2)}) collective-permute-start(f32[5,65,128]{2,1,0:T(8,128)} %pad_maximum_fusion.1), channel_id=1, source_target_pairs={{0,48},{16,64},{32,80},{48,96},{64,112},{80,128},{96,144},{112,160... | collective-permute-start | bytes 499208 | tf_op jit(solution)/shard_map/ppermute | solution.py:23
  103.7 7.1 %fusion.17 = f32[4,256,5,64]{1,3,2,0:T(8,128)} fusion(f32[4,256,5]{1,2,0:T(8,128)S(1)} %copy-done.12, f32[4,256,256]{2,1,0:T(8,128)S(1)} %fusion.59, pred[256,256]{1,0:T(8,128)(4,1)S(1)} %copy-done.13, f32[4,256,5,64]{1,0,3,2:T(4,128)S(1)} %reshape.106, f32[4,256,5]{1,2,0:T(8,128)S(1)} %bitcast.123), kind=kOutput, calls=%fused_computation.25 | convolution fusion | flops 1012203520 | bytes 3776512 | tf_op jit(solution)/shard_map/btsh,bshp->bthp/dot_general | solution.py:114
  111.9 1.5 multiply_add_fusion
  113.5 1.8 collective-permute-start.5
  115.4 2.7 collective-permute-start.4
  118.8 6.9 %collective-permute-done.4 = f32[5,65,128]{2,1,0:T(8,128)S(1)} collective-permute-done((f32[5,65,128]{2,1,0:T(8,128)S(1)}, f32[5,65,128]{2,1,0:T(8,128)S(1)}, u32[]{:S(2)}, u32[]{:S(2)}) %collective-permute-start.4) | collective-permute-done | bytes 166432 | tf_op jit(solution)/shard_map/ppermute | solution.py:23
  129.2 3.2 multiply_reduce_fusion
  132.6 7.5 %add_convert_fusion = bf16[1024,2688]{1,0:T(8,128)(2,1)} fusion(bf16[1024,2]{1,0:T(8,128)(2,1)S(1)} %copy.82, bf16[320,2560]{1,0:T(8,128)(2,1)} %param.29, f32[320]{0:T(512)S(1)} %copy-done.32, f32[1024,320]{0,1:T(8,128)S(1)} %bitcast.119, f32[1024,320]{0,1:T(8,128)} %get-tuple-element.45), kind=kOutput, calls=%fused_computation.2 | convolution fusion | flops 1772158976 | bytes 9770240 | tf_op jit(solution)/shard_map/dot_general | solution.py:153
  141.5 61.9 %reduce-scatter.10.cloned.1.call-done = bf16[64,2688]{1,0:T(8,128)(2,1)} async-done(((bf16[1024,2688]{1,0:T(8,128)(2,1)}), bf16[64,2688]{1,0:T(8,128)(2,1)}) %reduce-scatter.10.cloned.1.call-update) | async-done | bytes 344080
  209.5 2.0 copy.86
  212.6 38.0 %all-gather.8.cloned.1.call-done = bf16[512,2560]{1,0:T(8,128)(2,1)} async-done(((bf16[32,2560]{1,0:T(8,128)(2,1)}), bf16[512,2560]{1,0:T(8,128)(2,1)}) %all-gather.8.cloned.1.call-update) | async-done | bytes 2621456 | tf_op jit(solution)/shard_map/all_gather | solution.py:167
  250.5 3.2 fusion.99
  253.8 6.3 %convolution_convert_fusion = bf16[512,2560]{1,0:T(8,128)(2,1)} fusion(bf16[320,2560]{1,0:T(8,128)(2,1)S(1)} %copy-done, bf16[512,2560]{1,0:T(8,128)(2,1)} %all-gather.8.cloned.1.call-done, bf16[2560,320]{0,1:T(8,128)(2,1)} %param.32, f32[512,320]{0,1:T(8,128)S(1)} %fusion.99), kind=kOutput, calls=%fused_computation.12 | convolution fusion | flops 1680015360 | bytes 9175040 | tf_op jit(solution)/shard_map/dot_general | solution.py:172
  260.2 30.7 %all-gather.6.cloned.1.call-done = bf16[512,2560]{1,0:T(8,128)(2,1)} async-done(((bf16[32,2560]{1,0:T(8,128)(2,1)}), bf16[512,2560]{1,0:T(8,128)(2,1)}) %all-gather.6.cloned.1.call-update) | async-done | bytes 2621456 | tf_op jit(solution)/shard_map/all_gather | solution.py:167
  290.9 3.3 fusion.98
  294.2 6.3 %convolution_convert_fusion.1 = bf16[512,2560]{1,0:T(8,128)(2,1)} fusion(bf16[320,2560]{1,0:T(8,128)(2,1)S(1)} %copy-done, bf16[512,2560]{1,0:T(8,128)(2,1)} %all-gather.6.cloned.1.call-done, bf16[2560,320]{0,1:T(8,128)(2,1)} %param.32, f32[512,320]{0,1:T(8,128)S(1)} %fusion.98), kind=kOutput, calls=%fused_computation.13 | convolution fusion | flops 1680015360 | bytes 9175040 | tf_op jit(solution)/shard_map/dot_general | solution.py:172
  300.5 52.2 %reduce-scatter.14.cloned.1.call-done = bf16[32,2560]{1,0:T(8,128)(2,1)} async-done(((bf16[512,2560]{1,0:T(8,128)(2,1)}), bf16[32,2560]{1,0:T(8,128)(2,1)}) %reduce-scatter.14.cloned.1.call-update) | async-done | bytes 163856
  353.9 60.5 %reduce-scatter.12.cloned.1.call-done = bf16[32,2560]{1,0:T(8,128)(2,1)} async-done(((bf16[512,2560]{1,0:T(8,128)(2,1)}), bf16[32,2560]{1,0:T(8,128)(2,1)}) %reduce-scatter.12.cloned.1.call-update) | async-done | bytes 163856
  414.3 2.0 copy.99
  416.3 1.5 add_convert_fusion.2
  (157 shorter events, 31.6 us)
Async XLA Ops:
  6.5 247.2 %copy-start = (bf16[320,2560]{1,0:T(8,128)(2,1)S(1)}, bf16[320,2560]{1,0:T(8,128)(2,1)}, u32[]{:S(2)}) copy-start(bf16[320,2560]{1,0:T(8,128)(2,1)} %param.33) | copy-start | bytes 4915204
  6.5 48.8 %all-gather.4.cloned.1.call-start = ((), (), s32[]{:S(2)}) async-start(), calls=%async_computation.3 | async-start | bytes 5570560 | tf_op jit(solution)/shard_map/all_gather | solution.py:83
  7.3 196.1 %reduce-scatter.10.cloned.1.call-start = ((), (), s32[]{:S(2)}) async-start(), calls=%async_computation.6 | async-start | bytes 5849088
  11.4 47.7 %copy-start.15 = (f32[2560]{0:T(1024)S(1)}, f32[2560]{0:T(1024)}, u32[]{:S(2)}) copy-start(f32[2560]{0:T(1024)} %param.18) | copy-start | bytes 30724
  55.3 4.0 copy-start.2
  63.0 6.8 %slice-start = ((s8[5242880]{0:T(1024)(128)(4,1)}), s8[1048576]{0:T(1024)(128)(4,1)S(1)}, s32[]{:S(2)}) async-start(s8[5242880]{0:T(1024)(128)(4,1)} %bitcast.111), calls=%async_computation.9 | async-start | bytes 2097152
  63.6 12.0 %copy-start.19 = (f32[5]{0:T(128)}, f32[5]{0:T(128)S(1)}, u32[]{:S(2)}) copy-start(f32[5]{0:T(128)S(1)} %get-tuple-element.5) | copy-start | bytes 64
  64.7 5.1 %slice-start.1 = ((s8[5242880]{0:T(1024)(128)(4,1)}), s8[4194304]{0:T(1024)(128)(4,1)S(1)}, s32[]{:S(2)}) async-start(s8[5242880]{0:T(1024)(128)(4,1)} %bitcast.111), calls=%async_computation.10 | async-start | bytes 8388608
  64.7 5.2 %copy-start.31 = (bf16[2560,256]{1,0:T(8,128)(2,1)S(1)}, bf16[2560,256]{1,0:T(8,128)(2,1)}, u32[]{:S(2)}) copy-start(bf16[2560,256]{1,0:T(8,128)(2,1)} %param.21) | copy-start | bytes 3932164
  71.6 10.0 %collective-permute-start = (bf16[3,576]{0,1:T(8,128)(2,1)S(1)}, bf16[3,576]{0,1:T(8,128)(2,1)S(1)}, u32[]{:S(2)}, u32[]{:S(2)}) collective-permute-start(bf16[3,576]{0,1:T(8,128)(2,1)S(1)} %pad_maximum_fusion.3), channel_id=1, source_target_pairs={{0,16},{16,32},{32,48},{48,64},{64,80},{80,96},{96,112},{112,128},... | collective-permute-start | bytes 10376 | tf_op jit(solution)/shard_map/ppermute | solution.py:18
  92.0 11.6 %copy-start.12 = (f32[4,256,5]{1,2,0:T(8,128)S(1)}, f32[4,256,5]{1,2,0:T(8,128)}, u32[]{:S(2)}) copy-start(f32[4,256,5]{1,2,0:T(8,128)} %copy-done.11) | copy-start | bytes 61444
  92.0 11.6 %copy-start.13 = (pred[256,256]{1,0:T(8,128)(4,1)S(1)}, pred[256,256]{1,0:T(8,128)(4,1)}, u32[]{:S(2)}) copy-start(pred[256,256]{1,0:T(8,128)(4,1)} %iota_compare_fusion) | copy-start | bytes 196612
  92.9 18.0 %collective-permute-start.1 = (f32[5,65,128]{2,1,0:T(8,128)}, f32[5,65,128]{2,1,0:T(8,128)}, u32[]{:S(2)}, u32[]{:S(2)}) collective-permute-start(f32[5,65,128]{2,1,0:T(8,128)} %pad_maximum_fusion.1), channel_id=1, source_target_pairs={{0,16},{16,32},{32,48},{48,64},{64,80},{80,96},{96,112},{112,128},... | collective-permute-start | bytes 499208 | tf_op jit(solution)/shard_map/ppermute | solution.py:23
  94.8 16.1 %collective-permute-start.2 = (f32[5,65,128]{2,1,0:T(8,128)}, f32[5,65,128]{2,1,0:T(8,128)}, u32[]{:S(2)}, u32[]{:S(2)}) collective-permute-start(f32[5,65,128]{2,1,0:T(8,128)} %pad_maximum_fusion.1), channel_id=1, source_target_pairs={{0,32},{16,48},{32,64},{48,80},{64,96},{80,112},{96,128},{112,144}... | collective-permute-start | bytes 499208 | tf_op jit(solution)/shard_map/ppermute | solution.py:23
  98.8 12.1 %collective-permute-start.3 = (f32[5,65,128]{2,1,0:T(8,128)}, f32[5,65,128]{2,1,0:T(8,128)}, u32[]{:S(2)}, u32[]{:S(2)}) collective-permute-start(f32[5,65,128]{2,1,0:T(8,128)} %pad_maximum_fusion.1), channel_id=1, source_target_pairs={{0,48},{16,64},{32,80},{48,96},{64,112},{80,128},{96,144},{112,160... | collective-permute-start | bytes 499208 | tf_op jit(solution)/shard_map/ppermute | solution.py:23
  103.6 8.2 %copy-start.21 = (f32[5]{0:T(128)S(1)}, f32[5]{0:T(128)}, u32[]{:S(2)}) copy-start(f32[5]{0:T(128)} %copy-done.19) | copy-start | bytes 64
  103.6 8.3 %copy-start.18 = (f32[5]{0:T(128)S(1)}, f32[5]{0:T(128)}, u32[]{:S(2)}) copy-start(f32[5]{0:T(128)} %get-tuple-element.38) | copy-start | bytes 64
  103.7 8.3 %copy-start.29 = (f32[5]{0:T(128)S(1)}, f32[5]{0:T(128)}, u32[]{:S(2)}) copy-start(f32[5]{0:T(128)} %exp.78) | copy-start | bytes 64
  110.9 4.3 %copy-start.4 = (f32[4,5,64,128]{3,2,1,0:T(8,128)S(1)}, f32[4,5,64,128]{3,2,1,0:T(8,128)}, u32[]{:S(2)}) copy-start(f32[4,5,64,128]{3,2,1,0:T(8,128)} %copy-done.3) | copy-start | bytes 1966084
  113.4 12.5 %copy-start.6 = (f32[4,256,5,64]{1,3,2,0:T(8,128)S(1)}, f32[4,256,5,64]{1,3,2,0:T(8,128)}, u32[]{:S(2)}) copy-start(f32[4,256,5,64]{1,3,2,0:T(8,128)} %fusion.17) | copy-start | bytes 3932164
  113.4 12.5 %copy-start.9 = (f32[4,256,5]{1,2,0:T(8,128)S(1)}, f32[4,256,5]{1,2,0:T(8,128)}, u32[]{:S(2)}) copy-start(f32[4,256,5]{1,2,0:T(8,128)} %get-tuple-element.30) | copy-start | bytes 61444
  113.4 12.5 %copy-start.27 = (f32[5]{0:T(128)S(1)}, f32[5]{0:T(128)}, u32[]{:S(2)}) copy-start(f32[5]{0:T(128)} %param.27) | copy-start | bytes 64
  113.4 12.5 %copy-start.28 = (f32[4]{0:T(128)S(1)}, f32[4]{0:T(128)}, u32[]{:S(2)}) copy-start(f32[4]{0:T(128)} %pad.22.clone) | copy-start | bytes 52
  113.5 5.3 %collective-permute-start.5 = (f32[5,65,128]{2,1,0:T(8,128)S(1)}, f32[5,65,128]{2,1,0:T(8,128)S(1)}, u32[]{:S(2)}, u32[]{:S(2)}) collective-permute-start(f32[5,65,128]{2,1,0:T(8,128)S(1)} %pad_maximum_fusion.2), channel_id=1, source_target_pairs={{0,128},{16,144},{32,160},{48,176},{64,192},{80,208},{96,224},{112... | collective-permute-start | bytes 499208 | tf_op jit(solution)/shard_map/ppermute | solution.py:23
  115.4 10.4 %collective-permute-start.4 = (f32[5,65,128]{2,1,0:T(8,128)S(1)}, f32[5,65,128]{2,1,0:T(8,128)S(1)}, u32[]{:S(2)}, u32[]{:S(2)}) collective-permute-start(f32[5,65,128]{2,1,0:T(8,128)S(1)} %pad_maximum_fusion.2), channel_id=1, source_target_pairs={{0,64},{16,80},{32,96},{48,112},{64,128},{80,144},{96,160},{112,17... | collective-permute-start | bytes 499208 | tf_op jit(solution)/shard_map/ppermute | solution.py:23
  118.1 7.7 %collective-permute-start.6 = (f32[5,65,128]{2,1,0:T(8,128)S(1)}, f32[5,65,128]{2,1,0:T(8,128)S(1)}, u32[]{:S(2)}, u32[]{:S(2)}) collective-permute-start(f32[5,65,128]{2,1,0:T(8,128)S(1)} %pad_maximum_fusion.2), channel_id=1, source_target_pairs={{0,192},{16,208},{32,224},{48,240},{1,193},{17,209},{33,225},{49,2... | collective-permute-start | bytes 499208 | tf_op jit(solution)/shard_map/ppermute | solution.py:23
  129.2 3.4 copy-start.32
  140.2 110.3 %all-gather.8.cloned.1.call-start = ((), (), s32[]{:S(2)}) async-start(), calls=%async_computation.5 | async-start | bytes 2785280 | tf_op jit(solution)/shard_map/all_gather | solution.py:167
  204.3 3.7 copy-start.16
  211.5 79.4 %all-gather.6.cloned.1.call-start = ((), (), s32[]{:S(2)}) async-start(), calls=%async_computation.4 | async-start | bytes 2785280 | tf_op jit(solution)/shard_map/all_gather | solution.py:167
  212.5 140.1 %reduce-scatter.14.cloned.1.call-start = ((), (), s32[]{:S(2)}) async-start(), calls=%async_computation.8 | async-start | bytes 2785280
  260.1 154.2 %reduce-scatter.12.cloned.1.call-start = ((), (), s32[]{:S(2)}) async-start(), calls=%async_computation.7 | async-start | bytes 2785280
  (19 other events, 26.1 us)
Sparse Core Ops, SparseCore 0:
  9.2 46.1 all-gather.3
  140.3 62.9 reduce-scatter.9
  211.7 38.8 all-gather.7
  252.2 38.6 all-gather.5
  293.3 59.3 reduce-scatter.13
  355.0 59.2 reduce-scatter.11

commit v8 on v6

--- a/solution.py
+++ b/solution.py
@@ -99,7 +99,7 @@
     log_blocks = log_decay.reshape(block_count, BLOCK_LEN, head_count)
     step_blocks = dt_step.reshape(block_count, BLOCK_LEN, head_count)
     lower = jnp.tril(jnp.ones((BLOCK_LEN, BLOCK_LEN), jnp.float32))
-    cum_decay = jnp.einsum("ts,bsh->bth", lower, log_blocks, precision=lax.Precision.HIGHEST)
+    cum_decay = jnp.einsum("ts,bsh->bth", lower, log_blocks, precision=lax.Precision.HIGH)
     b_mat = conv_bcm[:, :STATE_DIM].reshape(block_count, BLOCK_LEN, STATE_DIM)
     c_mat = conv_bcm[:, STATE_DIM:].reshape(block_count, BLOCK_LEN, STATE_DIM)
     scores = jnp.einsum("btn,bsn->bts", c_mat, b_mat, preferred_element_type=jnp.float32)
@@ -111,13 +111,13 @@
     )
     scaled = inner_wide * step_blocks[..., None]
     mixed_w = scores[..., None] * weights
-    y_intra = jnp.einsum("btsh,bshp->bthp", mixed_w, scaled, precision=lax.Precision.HIGHEST)
+    y_intra = jnp.einsum("btsh,bshp->bthp", mixed_w, scaled, precision=lax.Precision.HIGH)
     block_last = cum_decay[:, -1, :]
     tail_decay = jnp.exp(block_last[:, None, :] - cum_decay)
     b_wide = b_mat.astype(jnp.float32)
     c_wide = c_mat.astype(jnp.float32)
     block_states = jnp.einsum(
-        "bsh,bshp,bsn->bhpn", tail_decay, scaled, b_wide, precision=lax.Precision.HIGHEST
+        "bsh,bshp,bsn->bhpn", tail_decay, scaled, b_wide, precision=lax.Precision.HIGH
     )
     block_decay = jnp.exp(block_last)
     zero_state = jnp.zeros((head_count, HEAD_DIM, STATE_DIM), jnp.float32)
@@ -135,7 +135,7 @@
     incoming = exclusive_prefix(packed, "ctx")[:, :HEAD_DIM, :]
     state_in = local_in + prior_decay[:, :, None, None] * incoming[None]
     y_inter = jnp.exp(cum_decay)[..., None] * jnp.einsum(
-        "btn,bhpn->bthp", c_wide, state_in, precision=lax.Precision.HIGHEST
+        "btn,bhpn->bthp", c_wide, state_in, precision=lax.Precision.HIGH
     )
     ssm_out = y_intra + y_inter + d_skip[None, None, :, None] * inner_wide
     gated = ssm_out.reshape(group_len, channels) * jax.nn.silu(gate_z)

time: 342 us -> 341 us (level)
  transfers between devices with their start and end apart: 11 -> 11, of which waited for: 8 -> 8; matrix products, arithmetic and copies ran while one was open for 4% -> 3% of each run, Pallas kernels for 0% -> 0%
where the time goes in v8:
time: 341 us; the launch traced here: 340 us
  waiting for transfers between devices  228 us (67%)
  matrix products  42.4 us (12%)
  local copies, waits for them, and re-layouts  19.9 us (6%)
  starting transfers between devices  18.3 us (5%)
  other arithmetic  18.1 us (5%)
  between operations  13.7 us (4%)
    unnamed x6, waiting for transfers between devices  125 us
    all_gather x1, waiting for transfers between devices, local(): gathered = lax.all_gather(tokens, 'tp', axis=0, tiled=True)  44.5 us
    all_gather x1, waiting for transfers between devices, local(): mlp_in = lax.all_gather(normed_own, 'tp', axis=0, tiled=True)  41.4 us
    ppermute x6, starting transfers between devices, shifted(): lax.ppermute(value, axis, [(source, source + steps) for source in range(c...  14.5 us
    ppermute x6, waiting for transfers between devices, shifted(): lax.ppermute(value, axis, [(source, source + steps) for source in range(c...  11.2 us
    dot_general x1, matrix products, local(): jnp.dot(piece, w_down, preferred_element_type=jnp.float32)  10.3 us
    dot_general x1, matrix products, local(): jnp.dot(piece, w_out_wide, preferred_element_type=jnp.float32) + extra  7.54 us
    unnamed x66, local copies, waits for them, and re-layouts  7.39 us
  transfers between devices with their start and end apart: 11, of which 8 were waited for; matrix products, arithmetic and copies ran while one was open for 3% of the time, Pallas kernels for 0%

profile of v8, /device:TPU:2, one launch (start us, length us, event | category | flops | bytes accessed | tf_op | source)
XLA Modules:
  0.0 340.3 jit_solution(9581432790951546564)
XLA Ops:
  10.9 44.5 %all-gather.3.cloned.1.call-done = bf16[1024,2560]{1,0:T(8,128)(2,1)} async-done(((bf16[64,2560]{1,0:T(8,128)(2,1)}), bf16[1024,2560]{1,0:T(8,128)(2,1)}) %all-gather.3.cloned.1.call-update) | async-done | bytes 5242896 | tf_op jit(solution)/shard_map/all_gather | solution.py:83
  55.3 3.7 %fusion = f32[1024]{0:T(1024)S(1)} fusion(bf16[1024,2560]{1,0:T(8,128)(2,1)} %all-gather.3.cloned.1.call-done), kind=kLoop, calls=%fused_computation.3 | loop fusion | flops 7863296 | bytes 5246976 | tf_op jit(solution)/shard_map/reduce_sum | solution.py:52
  59.4 1.3 fusion.2
  60.7 1.5 negate_multiply_fusion
  64.2 4.6 %convolution_convert_fusion.2 = bf16[1024,256]{0,1:T(8,128)(2,1)S(1)} fusion(bf16[1024,2560]{1,0:T(8,128)(2,1)} %copy-done.1, bf16[2560,256]{1,0:T(8,128)(2,1)} %param.21), kind=kOutput, calls=%fused_computation.47 | convolution fusion | flops 1342439424 | bytes 7077888 | tf_op jit(solution)/shard_map/dot_general | solution.py:85
  69.0 1.9 convolution_convert_fusion.1
  71.0 3.4 collective-permute-start
  75.4 5.6 %collective-permute-done = bf16[3,576]{0,1:T(8,128)(2,1)S(1)} collective-permute-done((bf16[3,576]{0,1:T(8,128)(2,1)S(1)}, bf16[3,576]{0,1:T(8,128)(2,1)S(1)}, u32[]{:S(2)}, u32[]{:S(2)}) %collective-permute-start) | collective-permute-done | bytes 3488 | tf_op jit(solution)/shard_map/ppermute | solution.py:18
  81.3 1.1 multiply_convert_fusion.2
  83.8 2.4 fusion.43
  86.2 1.9 reshape.106
  88.1 1.6 fusion.28
  91.4 2.5 collective-permute-start.3
  93.9 3.6 %collective-permute-start.2 = (f32[5,65,128]{2,1,0:T(8,128)}, f32[5,65,128]{2,1,0:T(8,128)}, u32[]{:S(2)}, u32[]{:S(2)}) collective-permute-start(f32[5,65,128]{2,1,0:T(8,128)} %pad_maximum_fusion), channel_id=1, source_target_pairs={{0,32},{16,48},{32,64},{48,80},{64,96},{80,112},{96,128},{112,144}... | collective-permute-start | bytes 499208 | tf_op jit(solution)/shard_map/ppermute | solution.py:23
  97.6 3.0 collective-permute-start.1
  100.9 4.4 %fusion.17 = f32[4,256,5,64]{1,3,2,0:T(8,128)} fusion(f32[4,256,5]{1,2,0:T(8,128)S(1)} %copy-done.10, f32[4,256,256]{2,1,0:T(8,128)S(1)} %fusion.47, pred[256,256]{1,0:T(8,128)(4,1)S(1)} %copy-done.11, f32[4,256,5,64]{1,0,3,2:T(4,128)S(1)} %reshape.106, f32[4,256,5]{1,2,0:T(8,128)S(1)} %bitcast.117), kind=kOutput, calls=%fused_computation.26 | convolution fusion | flops 508887040 | bytes 3776512 | tf_op jit(solution)/shard_map/btsh,bshp->bthp/dot_general | solution.py:114
  105.5 4.0 %collective-permute-done.1 = f32[5,65,128]{2,1,0:T(8,128)} collective-permute-done((f32[5,65,128]{2,1,0:T(8,128)}, f32[5,65,128]{2,1,0:T(8,128)}, u32[]{:S(2)}, u32[]{:S(2)}) %collective-permute-start.1) | collective-permute-done | bytes 166432 | tf_op jit(solution)/shard_map/ppermute | solution.py:23
  111.0 1.5 multiply_add_fusion
  112.6 2.8 collective-permute-start.5
  116.2 1.9 collective-permute-start.4
  118.4 6.9 %collective-permute-done.4 = f32[5,65,128]{2,1,0:T(8,128)S(1)} collective-permute-done((f32[5,65,128]{2,1,0:T(8,128)S(1)}, f32[5,65,128]{2,1,0:T(8,128)S(1)}, u32[]{:S(2)}, u32[]{:S(2)}) %collective-permute-start.4) | collective-permute-done | bytes 166432 | tf_op jit(solution)/shard_map/ppermute | solution.py:23
  128.6 3.2 multiply_reduce_fusion
  132.0 7.5 %add_convert_fusion = bf16[1024,2688]{1,0:T(8,128)(2,1)} fusion(bf16[1024,2]{1,0:T(8,128)(2,1)S(1)} %copy.81, bf16[320,2560]{1,0:T(8,128)(2,1)} %param.29, f32[320]{0:T(512)S(1)} %copy-done.23, f32[1024,320]{0,1:T(8,128)S(1)} %bitcast.113, f32[1024,320]{0,1:T(8,128)} %get-tuple-element.41), kind=kOutput, calls=%fused_computation.2 | convolution fusion | flops 1772158976 | bytes 9770240 | tf_op jit(solution)/shard_map/dot_general | solution.py:153
  140.8 60.6 %reduce-scatter.7.cloned.1.call-done = bf16[64,2688]{1,0:T(8,128)(2,1)} async-done(((bf16[1024,2688]{1,0:T(8,128)(2,1)}), bf16[64,2688]{1,0:T(8,128)(2,1)}) %reduce-scatter.7.cloned.1.call-update) | async-done | bytes 344080
  203.5 1.1 copy.102
  204.6 1.4 fusion.21
  207.7 41.4 %all-gather.5.cloned.1.call-done = bf16[1024,2560]{1,0:T(8,128)(2,1)} async-done(((bf16[64,2560]{1,0:T(8,128)(2,1)}), bf16[1024,2560]{1,0:T(8,128)(2,1)}) %all-gather.5.cloned.1.call-update) | async-done | bytes 5242896 | tf_op jit(solution)/shard_map/all_gather | solution.py:162
  249.2 5.9 %fusion.84 = f32[1024,320]{0,1:T(8,128)} fusion(bf16[1024,2560]{1,0:T(8,128)(2,1)} %all-gather.5.cloned.1.call-done, bf16[2560,320]{0,1:T(8,128)(2,1)} %param.31), kind=kOutput, calls=%fused_computation.155 | convolution fusion | flops 1677721600 | bytes 8192000 | tf_op jit(solution)/shard_map/dot_general | solution.py:163
  255.1 10.3 %convolution_convert_fusion = bf16[1024,2560]{1,0:T(8,128)(2,1)} fusion(bf16[320,2560]{1,0:T(8,128)(2,1)S(1)} %copy-done, bf16[1024,2560]{1,0:T(8,128)(2,1)} %all-gather.5.cloned.1.call-done, bf16[2560,320]{0,1:T(8,128)(2,1)} %param.32, f32[1024,320]{0,1:T(8,128)} %fusion.84), kind=kOutput, calls=%fused_computation.6 | convolution fusion | flops 3360030720 | bytes 15073280 | tf_op jit(solution)/shard_map/dot_general | solution.py:168
  265.5 64.0 %reduce-scatter.9.cloned.1.call-done = bf16[64,2560]{1,0:T(8,128)(2,1)} async-done(((bf16[1024,2560]{1,0:T(8,128)(2,1)}), bf16[64,2560]{1,0:T(8,128)(2,1)}) %reduce-scatter.9.cloned.1.call-update) | async-done | bytes 327696
  329.4 1.3 copy.96
  331.8 2.0 copy.85
  (126 shorter events, 23.8 us)
Async XLA Ops:
  6.5 248.6 %copy-start = (bf16[320,2560]{1,0:T(8,128)(2,1)S(1)}, bf16[320,2560]{1,0:T(8,128)(2,1)}, u32[]{:S(2)}) copy-start(bf16[320,2560]{1,0:T(8,128)(2,1)} %param.33) | copy-start | bytes 4915204
  6.5 48.8 %all-gather.3.cloned.1.call-start = ((), (), s32[]{:S(2)}) async-start(), calls=%async_computation.2 | async-start | bytes 5570560 | tf_op jit(solution)/shard_map/all_gather | solution.py:83
  7.3 194.2 %reduce-scatter.7.cloned.1.call-start = ((), (), s32[]{:S(2)}) async-start(), calls=%async_computation.4 | async-start | bytes 5849088
  10.9 48.2 %copy-start.13 = (f32[2560]{0:T(1024)S(1)}, f32[2560]{0:T(1024)}, u32[]{:S(2)}) copy-start(f32[2560]{0:T(1024)} %param.18) | copy-start | bytes 30724
  55.3 4.0 %copy-start.2 = (bf16[1024,2560]{1,0:T(8,128)(2,1)S(1)}, bf16[1024,2560]{1,0:T(8,128)(2,1)}, u32[]{:S(2)}) copy-start(bf16[1024,2560]{1,0:T(8,128)(2,1)} %all-gather.3.cloned.1.call-done) | copy-start | bytes 15728644
  60.7 2.3 copy-start.1
  63.0 5.9 %slice-start = ((s8[5242880]{0:T(1024)(128)(4,1)}), s8[1048576]{0:T(1024)(128)(4,1)S(1)}, s32[]{:S(2)}) async-start(s8[5242880]{0:T(1024)(128)(4,1)} %bitcast.105), calls=%async_computation.6 | async-start | bytes 2097152
  63.2 5.6 %copy-start.9 = (f32[4,256,5]{1,2,0:T(8,128)}, f32[4,256,5]{1,2,0:T(8,128)S(1)}, u32[]{:S(2)}) copy-start(f32[4,256,5]{1,2,0:T(8,128)S(1)} %convolution_bitcast_fusion) | copy-start | bytes 61444
  63.5 11.5 %copy-start.16 = (f32[5]{0:T(128)}, f32[5]{0:T(128)S(1)}, u32[]{:S(2)}) copy-start(f32[5]{0:T(128)S(1)} %get-tuple-element.5) | copy-start | bytes 64
  64.2 4.7 %slice-start.1 = ((s8[5242880]{0:T(1024)(128)(4,1)}), s8[4194304]{0:T(1024)(128)(4,1)S(1)}, s32[]{:S(2)}) async-start(s8[5242880]{0:T(1024)(128)(4,1)} %bitcast.105), calls=%async_computation.7 | async-start | bytes 8388608
  64.2 4.7 %copy-start.21 = (bf16[2560,320]{0,1:T(8,128)(2,1)S(1)}, bf16[2560,320]{0,1:T(8,128)(2,1)}, u32[]{:S(2)}) copy-start(bf16[2560,320]{0,1:T(8,128)(2,1)} %param.20) | copy-start | bytes 4915204
  70.9 10.4 %copy-start.7 = (bf16[1024,320]{0,1:T(8,128)(2,1)}, bf16[1024,320]{0,1:T(8,128)(2,1)S(1)}, u32[]{:S(2)}) copy-start(bf16[1024,320]{0,1:T(8,128)(2,1)S(1)} %convolution_convert_fusion.1) | copy-start | bytes 1966084
  71.0 10.0 %collective-permute-start = (bf16[3,576]{0,1:T(8,128)(2,1)S(1)}, bf16[3,576]{0,1:T(8,128)(2,1)S(1)}, u32[]{:S(2)}, u32[]{:S(2)}) collective-permute-start(bf16[3,576]{0,1:T(8,128)(2,1)S(1)} %pad_maximum_fusion.2), channel_id=1, source_target_pairs={{0,16},{16,32},{32,48},{48,64},{64,80},{80,96},{96,112},{112,128},... | collective-permute-start | bytes 10376 | tf_op jit(solution)/shard_map/ppermute | solution.py:18
  88.1 2.4 copy-start.15
  88.1 2.5 copy-start.17
  90.5 10.4 %copy-start.10 = (f32[4,256,5]{1,2,0:T(8,128)S(1)}, f32[4,256,5]{1,2,0:T(8,128)}, u32[]{:S(2)}) copy-start(f32[4,256,5]{1,2,0:T(8,128)} %copy-done.9) | copy-start | bytes 61444
  90.5 10.4 %copy-start.11 = (pred[256,256]{1,0:T(8,128)(4,1)S(1)}, pred[256,256]{1,0:T(8,128)(4,1)}, u32[]{:S(2)}) copy-start(pred[256,256]{1,0:T(8,128)(4,1)} %iota_compare_fusion) | copy-start | bytes 196612
  91.4 14.1 %collective-permute-start.3 = (f32[5,65,128]{2,1,0:T(8,128)}, f32[5,65,128]{2,1,0:T(8,128)}, u32[]{:S(2)}, u32[]{:S(2)}) collective-permute-start(f32[5,65,128]{2,1,0:T(8,128)} %pad_maximum_fusion), channel_id=1, source_target_pairs={{0,48},{16,64},{32,80},{48,96},{64,112},{80,128},{96,144},{112,160... | collective-permute-start | bytes 499208 | tf_op jit(solution)/shard_map/ppermute | solution.py:23
  93.9 11.6 %collective-permute-start.2 = (f32[5,65,128]{2,1,0:T(8,128)}, f32[5,65,128]{2,1,0:T(8,128)}, u32[]{:S(2)}, u32[]{:S(2)}) collective-permute-start(f32[5,65,128]{2,1,0:T(8,128)} %pad_maximum_fusion), channel_id=1, source_target_pairs={{0,32},{16,48},{32,64},{48,80},{64,96},{80,112},{96,128},{112,144}... | collective-permute-start | bytes 499208 | tf_op jit(solution)/shard_map/ppermute | solution.py:23
  97.6 12.0 %collective-permute-start.1 = (f32[5,65,128]{2,1,0:T(8,128)}, f32[5,65,128]{2,1,0:T(8,128)}, u32[]{:S(2)}, u32[]{:S(2)}) collective-permute-start(f32[5,65,128]{2,1,0:T(8,128)} %pad_maximum_fusion), channel_id=1, source_target_pairs={{0,16},{16,32},{32,48},{48,64},{64,80},{80,96},{96,112},{112,128},... | collective-permute-start | bytes 499208 | tf_op jit(solution)/shard_map/ppermute | solution.py:23
  105.5 9.9 %copy-start.4 = (f32[4,5,64,128]{3,2,1,0:T(8,128)S(1)}, f32[4,5,64,128]{3,2,1,0:T(8,128)}, u32[]{:S(2)}) copy-start(f32[4,5,64,128]{3,2,1,0:T(8,128)} %copy-done.3) | copy-start | bytes 1966084
  112.5 12.9 %copy-start.6 = (f32[4,256,5,64]{1,3,2,0:T(8,128)S(1)}, f32[4,256,5,64]{1,3,2,0:T(8,128)}, u32[]{:S(2)}) copy-start(f32[4,256,5,64]{1,3,2,0:T(8,128)} %fusion.17) | copy-start | bytes 3932164
  112.5 12.9 %copy-start.19 = (f32[5]{0:T(128)S(1)}, f32[5]{0:T(128)}, u32[]{:S(2)}) copy-start(f32[5]{0:T(128)} %param.27) | copy-start | bytes 64
  112.5 12.9 %copy-start.20 = (f32[4]{0:T(128)S(1)}, f32[4]{0:T(128)}, u32[]{:S(2)}) copy-start(f32[4]{0:T(128)} %pad.20.clone) | copy-start | bytes 52
  112.6 5.9 %collective-permute-start.5 = (f32[5,65,128]{2,1,0:T(8,128)S(1)}, f32[5,65,128]{2,1,0:T(8,128)S(1)}, u32[]{:S(2)}, u32[]{:S(2)}) collective-permute-start(f32[5,65,128]{2,1,0:T(8,128)S(1)} %pad_maximum_fusion.1), channel_id=1, source_target_pairs={{0,128},{16,144},{32,160},{48,176},{64,192},{80,208},{96,224},{112... | collective-permute-start | bytes 499208 | tf_op jit(solution)/shard_map/ppermute | solution.py:23
  115.5 9.8 %collective-permute-start.6 = (f32[5,65,128]{2,1,0:T(8,128)S(1)}, f32[5,65,128]{2,1,0:T(8,128)S(1)}, u32[]{:S(2)}, u32[]{:S(2)}) collective-permute-start(f32[5,65,128]{2,1,0:T(8,128)S(1)} %pad_maximum_fusion.1), channel_id=1, source_target_pairs={{0,192},{16,208},{32,224},{48,240},{1,193},{17,209},{33,225},{49,2... | collective-permute-start | bytes 499208 | tf_op jit(solution)/shard_map/ppermute | solution.py:23
  116.2 9.1 %collective-permute-start.4 = (f32[5,65,128]{2,1,0:T(8,128)S(1)}, f32[5,65,128]{2,1,0:T(8,128)S(1)}, u32[]{:S(2)}, u32[]{:S(2)}) collective-permute-start(f32[5,65,128]{2,1,0:T(8,128)S(1)} %pad_maximum_fusion.1), channel_id=1, source_target_pairs={{0,64},{16,80},{32,96},{48,112},{64,128},{80,144},{96,160},{112,17... | collective-permute-start | bytes 499208 | tf_op jit(solution)/shard_map/ppermute | solution.py:23
  125.4 2.4 slice-start.3
  128.6 3.4 %copy-start.23 = (f32[320]{0:T(512)S(1)}, f32[320]{0:T(512)}, u32[]{:S(2)}) copy-start(f32[320]{0:T(512)} %param.28) | copy-start | bytes 3844
  139.6 109.6 %all-gather.5.cloned.1.call-start = ((), (), s32[]{:S(2)}) async-start(), calls=%async_computation.3 | async-start | bytes 5570560 | tf_op jit(solution)/shard_map/all_gather | solution.py:162
  203.5 2.6 copy-start.14
  207.4 122.0 %reduce-scatter.9.cloned.1.call-start = ((), (), s32[]{:S(2)}) async-start(), calls=%async_computation.5 | async-start | bytes 5570560
  (7 other events, 9.1 us)
Sparse Core Ops, SparseCore 0:
  9.2 46.1 all-gather.2
  139.7 61.6 reduce-scatter.6
  207.6 41.5 all-gather.4
  265.6 63.8 reduce-scatter.8

commit v9 on v8

--- a/solution.py
+++ b/solution.py
@@ -33,18 +33,12 @@
 
 def exclusive_prefix(packed, axis):
     count = lax.axis_size(axis)
-    before = jnp.zeros_like(packed)
-    upto = packed
+    upto = shifted(packed, axis, 1)
     stride = 1
     while stride < count:
-        parts = [shifted(upto, axis, k * stride) for k in (3, 2, 1) if k * stride < count]
-        older = parts[0]
-        for part in parts[1:]:
-            older = join_packed(older, part)
-        before = join_packed(older, before)
-        upto = join_packed(older, upto)
-        stride *= 4
-    return before
+        upto = join_packed(shifted(upto, axis, stride), upto)
+        stride *= 2
+    return upto
 
 
 def rms_rows(values, gain):

time: 341 us -> 356 us (1.044)
  waiting for transfers between devices: 228 us -> 246 us
    ppermute x6 -> x5, waiting for transfers between devices: 11.2 us -> 24.3 us  [shifted(): lax.ppermute(value, axis, [(source, source + steps) for source in range(c...]
    ppermute x6 -> x5, starting transfers between devices: 14.5 us -> 12 us  [shifted(): lax.ppermute(value, axis, [(source, source + steps) for source in range(c...]
    unnamed x66 -> x62, local copies, waits for them, and re-layouts: 7.39 us -> 6.56 us
  transfers between devices with their start and end apart: 11 -> 10, of which waited for: 8 -> 9; matrix products, arithmetic and copies ran while one was open for 3% -> 3% of each run, Pallas kernels for 0% -> 0%
where the time goes in v9:
time: 356 us; the launch traced here: 355 us
  waiting for transfers between devices  246 us (69%)
  matrix products  42.4 us (12%)
  local copies, waits for them, and re-layouts  19.3 us (5%)
  other arithmetic  18.1 us (5%)
  starting transfers between devices  15.7 us (4%)
  between operations  13.7 us (4%)
    unnamed x6, waiting for transfers between devices  128 us
    all_gather x1, waiting for transfers between devices, local(): gathered = lax.all_gather(tokens, 'tp', axis=0, tiled=True)  45.6 us
    all_gather x1, waiting for transfers between devices, local(): mlp_in = lax.all_gather(normed_own, 'tp', axis=0, tiled=True)  41.6 us
    ppermute x5, waiting for transfers between devices, shifted(): lax.ppermute(value, axis, [(source, source + steps) for source in range(c...  24.3 us
    ppermute x5, starting transfers between devices, shifted(): lax.ppermute(value, axis, [(source, source + steps) for source in range(c...  12 us
    dot_general x1, matrix products, local(): jnp.dot(piece, w_down, preferred_element_type=jnp.float32)  10.3 us
    dot_general x1, matrix products, local(): jnp.dot(piece, w_out_wide, preferred_element_type=jnp.float32) + extra  7.52 us
  transfers between devices with their start and end apart: 10, of which 9 were waited for; matrix products, arithmetic and copies ran while one was open for 3% of the time, Pallas kernels for 0%

profile of v9, /device:TPU:2, one launch (start us, length us, event | category | flops | bytes accessed | tf_op | source)
XLA Modules:
  0.0 355.1 jit_solution(3543200404778481870)
XLA Ops:
  9.7 45.6 %all-gather.3.cloned.1.call-done = bf16[1024,2560]{1,0:T(8,128)(2,1)} async-done(((bf16[64,2560]{1,0:T(8,128)(2,1)}), bf16[1024,2560]{1,0:T(8,128)(2,1)}) %all-gather.3.cloned.1.call-update) | async-done | bytes 5242896 | tf_op jit(solution)/shard_map/all_gather | solution.py:77
  55.3 3.7 %fusion = f32[1024]{0:T(1024)S(1)} fusion(bf16[1024,2560]{1,0:T(8,128)(2,1)} %all-gather.3.cloned.1.call-done), kind=kLoop, calls=%fused_computation.3 | loop fusion | flops 7863296 | bytes 5246976 | tf_op jit(solution)/shard_map/reduce_sum | solution.py:46
  59.4 1.3 fusion.2
  60.7 1.5 negate_multiply_fusion
  64.8 4.6 %convolution_convert_fusion.2 = bf16[1024,256]{0,1:T(8,128)(2,1)S(1)} fusion(bf16[1024,2560]{1,0:T(8,128)(2,1)} %copy-done.1, bf16[2560,256]{1,0:T(8,128)(2,1)} %param.21), kind=kOutput, calls=%fused_computation.47 | convolution fusion | flops 1342439424 | bytes 7077888 | tf_op jit(solution)/shard_map/dot_general | solution.py:79
  69.5 1.9 convolution_convert_fusion.1
  71.6 3.4 collective-permute-start
  75.5 6.0 %collective-permute-done = bf16[3,576]{0,1:T(8,128)(2,1)S(1)} collective-permute-done((bf16[3,576]{0,1:T(8,128)(2,1)S(1)}, bf16[3,576]{0,1:T(8,128)(2,1)S(1)}, u32[]{:S(2)}, u32[]{:S(2)}) %collective-permute-start) | collective-permute-done | bytes 3488 | tf_op jit(solution)/shard_map/ppermute | solution.py:18
  84.3 2.4 fusion.43
  86.8 1.9 reshape.102
  88.7 1.6 fusion.28
  90.5 1.9 collective-permute-start.1
  92.4 8.0 %collective-permute-done.1 = f32[5,65,128]{2,1,0:T(8,128)S(1)} collective-permute-done((f32[5,65,128]{2,1,0:T(8,128)S(1)}, f32[5,65,128]{2,1,0:T(8,128)S(1)}, u32[]{:S(2)}, u32[]{:S(2)}) %collective-permute-start.1) | collective-permute-done | bytes 166432 | tf_op jit(solution)/shard_map/ppermute | solution.py:23
  100.4 1.9 collective-permute-start.2
  102.8 7.1 %collective-permute-done.2 = f32[5,65,128]{2,1,0:T(8,128)S(1)} collective-permute-done((f32[5,65,128]{2,1,0:T(8,128)S(1)}, f32[5,65,128]{2,1,0:T(8,128)S(1)}, u32[]{:S(2)}, u32[]{:S(2)}) %collective-permute-start.2) | collective-permute-done | bytes 166432 | tf_op jit(solution)/shard_map/ppermute | solution.py:23
  110.0 1.9 collective-permute-start.3
  112.3 7.5 %collective-permute-done.3 = f32[5,65,128]{2,1,0:T(8,128)S(1)} collective-permute-done((f32[5,65,128]{2,1,0:T(8,128)S(1)}, f32[5,65,128]{2,1,0:T(8,128)S(1)}, u32[]{:S(2)}, u32[]{:S(2)}) %collective-permute-start.3) | collective-permute-done | bytes 166432 | tf_op jit(solution)/shard_map/ppermute | solution.py:23
  120.6 3.5 collective-permute-start.4
  124.1 4.4 %fusion.17 = f32[4,256,5,64]{1,3,2,0:T(8,128)} fusion(f32[4,256,5]{1,2,0:T(8,128)S(1)} %copy-done.10, f32[4,256,256]{2,1,0:T(8,128)S(1)} %fusion.47, pred[256,256]{1,0:T(8,128)(4,1)S(1)} %iota_compare_fusion, f32[4,256,5,64]{1,0,3,2:T(4,128)S(1)} %reshape.102, f32[4,256,5]{1,2,0:T(8,128)S(1)} %bitcast.108), kind=kOutput, calls=%fused_computation.26 | convolution fusion | flops 508887040 | bytes 3776512 | tf_op jit(solution)/shard_map/btsh,bshp->bthp/dot_general | solution.py:108
  131.3 2.7 collective-permute-start.5
  134.0 1.3 multiply_add_fusion
  135.4 1.7 collective-permute-done.5
  140.2 3.2 multiply_reduce_fusion
  143.7 7.5 %add_convert_fusion = bf16[1024,2688]{1,0:T(8,128)(2,1)} fusion(bf16[1024,2]{1,0:T(8,128)(2,1)S(1)} %copy.81, bf16[320,2560]{1,0:T(8,128)(2,1)} %param.29, f32[320]{0:T(512)S(1)} %copy-done.21, f32[1024,320]{0,1:T(8,128)S(1)} %bitcast.104, f32[1024,320]{0,1:T(8,128)} %get-tuple-element.42), kind=kOutput, calls=%fused_computation.2 | convolution fusion | flops 1772158976 | bytes 9770240 | tf_op jit(solution)/shard_map/dot_general | solution.py:147
  152.5 63.5 %reduce-scatter.7.cloned.1.call-done = bf16[64,2688]{1,0:T(8,128)(2,1)} async-done(((bf16[1024,2688]{1,0:T(8,128)(2,1)}), bf16[64,2688]{1,0:T(8,128)(2,1)}) %reduce-scatter.7.cloned.1.call-update) | async-done | bytes 344080
  219.2 1.4 fusion.21
  222.3 41.6 %all-gather.5.cloned.1.call-done = bf16[1024,2560]{1,0:T(8,128)(2,1)} async-done(((bf16[64,2560]{1,0:T(8,128)(2,1)}), bf16[1024,2560]{1,0:T(8,128)(2,1)}) %all-gather.5.cloned.1.call-update) | async-done | bytes 5242896 | tf_op jit(solution)/shard_map/all_gather | solution.py:156
  263.9 5.9 %fusion.79 = f32[1024,320]{0,1:T(8,128)} fusion(bf16[1024,2560]{1,0:T(8,128)(2,1)} %all-gather.5.cloned.1.call-done, bf16[2560,320]{0,1:T(8,128)(2,1)} %param.31), kind=kOutput, calls=%fused_computation.152 | convolution fusion | flops 1677721600 | bytes 8192000 | tf_op jit(solution)/shard_map/dot_general | solution.py:157
  269.8 10.3 %convolution_convert_fusion = bf16[1024,2560]{1,0:T(8,128)(2,1)} fusion(bf16[320,2560]{1,0:T(8,128)(2,1)S(1)} %copy-done, bf16[1024,2560]{1,0:T(8,128)(2,1)} %all-gather.5.cloned.1.call-done, bf16[2560,320]{0,1:T(8,128)(2,1)} %param.32, f32[1024,320]{0,1:T(8,128)} %fusion.79), kind=kOutput, calls=%fused_computation.6 | convolution fusion | flops 3360030720 | bytes 15073280 | tf_op jit(solution)/shard_map/dot_general | solution.py:162
  280.2 64.0 %reduce-scatter.9.cloned.1.call-done = bf16[64,2560]{1,0:T(8,128)(2,1)} async-done(((bf16[1024,2560]{1,0:T(8,128)(2,1)}), bf16[64,2560]{1,0:T(8,128)(2,1)}) %reduce-scatter.9.cloned.1.call-update) | async-done | bytes 327696
  344.2 1.3 copy.96
  346.5 2.0 copy.85
  (122 shorter events, 24.6 us)
Async XLA Ops:
  6.5 263.3 %copy-start = (bf16[320,2560]{1,0:T(8,128)(2,1)S(1)}, bf16[320,2560]{1,0:T(8,128)(2,1)}, u32[]{:S(2)}) copy-start(bf16[320,2560]{1,0:T(8,128)(2,1)} %param.33) | copy-start | bytes 4915204
  6.5 48.8 %all-gather.3.cloned.1.call-start = ((), (), s32[]{:S(2)}) async-start(), calls=%async_computation.2 | async-start | bytes 5570560 | tf_op jit(solution)/shard_map/all_gather | solution.py:77
  7.3 208.8 %reduce-scatter.7.cloned.1.call-start = ((), (), s32[]{:S(2)}) async-start(), calls=%async_computation.4 | async-start | bytes 5849088
  9.7 49.4 %copy-start.12 = (f32[2560]{0:T(1024)S(1)}, f32[2560]{0:T(1024)}, u32[]{:S(2)}) copy-start(f32[2560]{0:T(1024)} %param.18) | copy-start | bytes 30724
  55.3 4.0 %copy-start.2 = (bf16[1024,2560]{1,0:T(8,128)(2,1)S(1)}, bf16[1024,2560]{1,0:T(8,128)(2,1)}, u32[]{:S(2)}) copy-start(bf16[1024,2560]{1,0:T(8,128)(2,1)} %all-gather.3.cloned.1.call-done) | copy-start | bytes 15728644
  60.7 2.3 copy-start.1
  63.0 6.5 %slice-start = ((s8[5242880]{0:T(1024)(128)(4,1)}), s8[1048576]{0:T(1024)(128)(4,1)S(1)}, s32[]{:S(2)}) async-start(s8[5242880]{0:T(1024)(128)(4,1)} %bitcast.96), calls=%async_computation.6 | async-start | bytes 2097152
  63.3 6.1 %copy-start.9 = (f32[4,256,5]{1,2,0:T(8,128)}, f32[4,256,5]{1,2,0:T(8,128)S(1)}, u32[]{:S(2)}) copy-start(f32[4,256,5]{1,2,0:T(8,128)S(1)} %convolution_bitcast_fusion) | copy-start | bytes 61444
  64.7 4.7 %slice-start.1 = ((s8[5242880]{0:T(1024)(128)(4,1)}), s8[4194304]{0:T(1024)(128)(4,1)S(1)}, s32[]{:S(2)}) async-start(s8[5242880]{0:T(1024)(128)(4,1)} %bitcast.96), calls=%async_computation.7 | async-start | bytes 8388608
  64.8 4.7 %copy-start.19 = (bf16[2560,320]{0,1:T(8,128)(2,1)S(1)}, bf16[2560,320]{0,1:T(8,128)(2,1)}, u32[]{:S(2)}) copy-start(bf16[2560,320]{0,1:T(8,128)(2,1)} %param.20) | copy-start | bytes 4915204
  71.4 10.4 %copy-start.7 = (bf16[1024,320]{0,1:T(8,128)(2,1)}, bf16[1024,320]{0,1:T(8,128)(2,1)S(1)}, u32[]{:S(2)}) copy-start(bf16[1024,320]{0,1:T(8,128)(2,1)S(1)} %convolution_convert_fusion.1) | copy-start | bytes 1966084
  71.6 10.0 %collective-permute-start = (bf16[3,576]{0,1:T(8,128)(2,1)S(1)}, bf16[3,576]{0,1:T(8,128)(2,1)S(1)}, u32[]{:S(2)}, u32[]{:S(2)}) collective-permute-start(bf16[3,576]{0,1:T(8,128)(2,1)S(1)} %pad_maximum_fusion.4), channel_id=1, source_target_pairs={{0,16},{16,32},{32,48},{48,64},{64,80},{80,96},{96,112},{112,128},... | collective-permute-start | bytes 10376 | tf_op jit(solution)/shard_map/ppermute | solution.py:18
  88.6 1.6 copy-start.15
  88.6 1.7 copy-start.16
  90.2 22.1 %copy-start.3 = (f32[4,5,64,128]{3,2,1,0:T(8,128)}, f32[4,5,64,128]{3,2,1,0:T(8,128)S(1)}, u32[]{:S(2)}) copy-start(f32[4,5,64,128]{3,2,1,0:T(8,128)S(1)} %fusion.28) | copy-start | bytes 1966084
  90.5 9.9 %collective-permute-start.1 = (f32[5,65,128]{2,1,0:T(8,128)S(1)}, f32[5,65,128]{2,1,0:T(8,128)S(1)}, u32[]{:S(2)}, u32[]{:S(2)}) collective-permute-start(f32[5,65,128]{2,1,0:T(8,128)S(1)} %pad_maximum_fusion), channel_id=1, source_target_pairs={{0,16},{16,32},{32,48},{48,64},{64,80},{80,96},{96,112},{112,128},... | collective-permute-start | bytes 499208 | tf_op jit(solution)/shard_map/ppermute | solution.py:23
  100.4 9.5 %collective-permute-start.2 = (f32[5,65,128]{2,1,0:T(8,128)S(1)}, f32[5,65,128]{2,1,0:T(8,128)S(1)}, u32[]{:S(2)}, u32[]{:S(2)}) collective-permute-start(f32[5,65,128]{2,1,0:T(8,128)S(1)} %collective-permute-done.1), channel_id=1, source_target_pairs={{0,16},{16,32},{32,48},{48,64},{64,80},{80,96},{96,112},{112,128},... | collective-permute-start | bytes 499208 | tf_op jit(solution)/shard_map/ppermute | solution.py:23
  110.0 14.1 %copy-start.10 = (f32[4,256,5]{1,2,0:T(8,128)S(1)}, f32[4,256,5]{1,2,0:T(8,128)}, u32[]{:S(2)}) copy-start(f32[4,256,5]{1,2,0:T(8,128)} %copy-done.9) | copy-start | bytes 61444
  110.0 9.8 %collective-permute-start.3 = (f32[5,65,128]{2,1,0:T(8,128)S(1)}, f32[5,65,128]{2,1,0:T(8,128)S(1)}, u32[]{:S(2)}, u32[]{:S(2)}) collective-permute-start(f32[5,65,128]{2,1,0:T(8,128)S(1)} %pad_maximum_fusion.1), channel_id=1, source_target_pairs={{0,32},{16,48},{32,64},{48,80},{64,96},{80,112},{96,128},{112,144}... | collective-permute-start | bytes 499208 | tf_op jit(solution)/shard_map/ppermute | solution.py:23
  120.6 8.9 %collective-permute-start.4 = (f32[5,65,128]{2,1,0:T(8,128)}, f32[5,65,128]{2,1,0:T(8,128)}, u32[]{:S(2)}, u32[]{:S(2)}) collective-permute-start(f32[5,65,128]{2,1,0:T(8,128)} %pad_maximum_fusion.2), channel_id=1, source_target_pairs={{0,64},{16,80},{32,96},{48,112},{64,128},{80,144},{96,160},{112,17... | collective-permute-start | bytes 499208 | tf_op jit(solution)/shard_map/ppermute | solution.py:23
  129.4 7.6 %copy-start.5 = (f32[4,256,5,64]{1,3,2,0:T(8,128)S(1)}, f32[4,256,5,64]{1,3,2,0:T(8,128)}, u32[]{:S(2)}) copy-start(f32[4,256,5,64]{1,3,2,0:T(8,128)} %fusion.17) | copy-start | bytes 3932164
  129.4 7.6 %copy-start.6 = (bf16[4,256,128]{1,0,2:T(4,128)(2,1)S(1)}, bf16[4,256,128]{1,0,2:T(4,128)(2,1)}, u32[]{:S(2)}) copy-start(bf16[4,256,128]{1,0,2:T(4,128)(2,1)} %reshape.97) | copy-start | bytes 786436
  129.4 7.6 %copy-start.17 = (f32[5]{0:T(128)S(1)}, f32[5]{0:T(128)}, u32[]{:S(2)}) copy-start(f32[5]{0:T(128)} %param.27) | copy-start | bytes 64
  129.4 7.6 %copy-start.18 = (f32[4]{0:T(128)S(1)}, f32[4]{0:T(128)}, u32[]{:S(2)}) copy-start(f32[4]{0:T(128)} %pad.24.clone) | copy-start | bytes 52
  131.3 5.7 %collective-permute-start.5 = (f32[5,65,128]{2,1,0:T(8,128)S(1)}, f32[5,65,128]{2,1,0:T(8,128)S(1)}, u32[]{:S(2)}, u32[]{:S(2)}) collective-permute-start(f32[5,65,128]{2,1,0:T(8,128)S(1)} %pad_maximum_fusion.3), channel_id=1, source_target_pairs={{0,128},{16,144},{32,160},{48,176},{64,192},{80,208},{96,224},{112... | collective-permute-start | bytes 499208 | tf_op jit(solution)/shard_map/ppermute | solution.py:23
  134.0 5.1 %slice-start.2 = ((s8[5242880]{0:T(1024)(128)(4,1)}), s8[4194304]{0:T(1024)(128)(4,1)S(1)}, s32[]{:S(2)}) async-start(s8[5242880]{0:T(1024)(128)(4,1)} %bitcast.98), calls=%async_computation.8 | async-start | bytes 8388608
  137.1 2.0 slice-start.3
  138.8 1.4 copy-start.20
  140.2 3.4 copy-start.21
  151.2 112.7 %all-gather.5.cloned.1.call-start = ((), (), s32[]{:S(2)}) async-start(), calls=%async_computation.3 | async-start | bytes 5570560 | tf_op jit(solution)/shard_map/all_gather | solution.py:156
  218.1 2.6 copy-start.13
  222.0 122.1 %reduce-scatter.9.cloned.1.call-start = ((), (), s32[]{:S(2)}) async-start(), calls=%async_computation.5 | async-start | bytes 5570560
  (4 other events, 4.6 us)
Sparse Core Ops, SparseCore 0:
  9.2 46.1 all-gather.2
  151.3 64.6 reduce-scatter.6
  222.2 41.6 all-gather.4
  280.3 63.8 reduce-scatter.8

commit v10 on v8

--- a/solution.py
+++ b/solution.py
@@ -145,19 +145,28 @@
     width = w_out.shape[1]
     pad_cols = 128
     extra = jnp.concatenate(
-        [squares_hi[:, None], squares_lo[:, None]], axis=1
-    ).astype(jnp.float32)
-    extra = jnp.pad(extra, ((0, 0), (width, pad_cols - 2)))
-    piece = (gated * ssm_gain).astype(jnp.bfloat16)
-    w_out_wide = jnp.pad(w_out, ((0, 0), (0, pad_cols)))
-    product = (jnp.dot(piece, w_out_wide, preferred_element_type=jnp.float32) + extra).astype(
-        jnp.bfloat16
-    )
+        [squares_hi[:, None], squares_lo[:, None], jnp.zeros((group_len, pad_cols - 2), jnp.bfloat16)],
+        axis=1,
+    )
+    piece = jnp.concatenate([(gated * ssm_gain).astype(jnp.bfloat16), extra], axis=1)
+    lane = lax.broadcasted_iota(jnp.int32, (pad_cols, pad_cols), 1)
+    sub = lax.broadcasted_iota(jnp.int32, (pad_cols, pad_cols), 0)
+    pick = ((lane == sub) & (sub < 2)).astype(jnp.bfloat16)
+    w_out_wide = jnp.concatenate(
+        [
+            jnp.pad(w_out, ((0, 0), (0, pad_cols))),
+            jnp.concatenate([jnp.zeros((pad_cols, width), jnp.bfloat16), pick], axis=1),
+        ],
+        axis=0,
+    )
+    product = jnp.dot(piece, w_out_wide, preferred_element_type=jnp.float32).astype(jnp.bfloat16)
     reduced = lax.psum_scatter(product, "tp", scatter_dimension=0, tiled=True)
     squares_own = reduced[:, width].astype(jnp.float32) + reduced[:, width + 1].astype(jnp.float32)
     scale = lax.rsqrt(squares_own / (HEADS * HEAD_DIM) + EPS)
     mixer_own = reduced[:, :width].astype(jnp.float32) * scale[:, None]
-    resid = (tokens.astype(jnp.float32) + mixer_own).astype(jnp.bfloat16)
+    own_rows = tokens.shape[0]
+    own_tokens = lax.dynamic_slice_in_dim(gathered, lax.axis_index("tp") * own_rows, own_rows, 0)
+    resid = (own_tokens.astype(jnp.float32) + mixer_own).astype(jnp.bfloat16)
     normed_own = rms_rows(resid, norm2_gain).astype(jnp.bfloat16)
     mlp_in = lax.all_gather(normed_own, "tp", axis=0, tiled=True)
     mlp_gate = jnp.dot(mlp_in, w_gate, preferred_element_type=jnp.float32)

time: 341 us -> 333 us (0.977)
  local copies, waits for them, and re-layouts: 19.9 us -> 13.8 us
  matrix products: 42.4 us -> 38.4 us
    reduce_scatter x0 -> x2, waiting for transfers between devices: none -> 130 us  [the longest x1 65.8 us: local(): reduced = lax.psum_scatter(product, 'tp', scatter_dimension=0, tiled=True)]
    unnamed x6 -> x4, waiting for transfers between devices: 125 us -> 0.76 us
    ppermute x6, waiting for transfers between devices: 11.2 us -> 6.23 us  [shifted(): lax.ppermute(value, axis, [(source, source + steps) for source in range(c...]
    unnamed x66 -> x83, local copies, waits for them, and re-layouts: 7.39 us -> 3.99 us
  transfers between devices with their start and end apart: 11 -> 11, of which waited for: 8 -> 7; matrix products, arithmetic and copies ran while one was open for 3% -> 4% of each run, Pallas kernels for 0% -> 0%
where the time goes in v10:
time: 333 us
  waiting for transfers between devices  226 us (68%)
  matrix products  38.4 us (12%)
  other arithmetic  20.5 us (6%)
  starting transfers between devices  20 us (6%)
  local copies, waits for them, and re-layouts  13.8 us (4%)
  between operations  13.8 us (4%)
    reduce_scatter x1, waiting for transfers between devices, local(): reduced = lax.psum_scatter(product, 'tp', scatter_dimension=0, tiled=True)  65.8 us
    reduce_scatter x1, waiting for transfers between devices, local(): lax.psum_scatter(jnp.dot(piece, w_down, preferred_element_type=jnp.float3...  64 us
    all_gather x1, waiting for transfers between devices, local(): gathered = lax.all_gather(tokens, 'tp', axis=0, tiled=True)  42.2 us
    all_gather x1, waiting for transfers between devices, local(): mlp_in = lax.all_gather(normed_own, 'tp', axis=0, tiled=True)  41.8 us
    ppermute x6, starting transfers between devices, shifted(): lax.ppermute(value, axis, [(source, source + steps) for source in range(c...  16.2 us
    dot_general x1, matrix products, local(): jnp.dot(piece, w_down, preferred_element_type=jnp.float32)  10 us
  transfers between devices with their start and end apart: 11, of which 7 were waited for; matrix products, arithmetic and copies ran while one was open for 4% of the time, Pallas kernels for 0%

profile of v10, /device:TPU:2, one launch (start us, length us, event | category | flops | bytes accessed | tf_op | source)
XLA Modules:
  0.0 332.5 jit_solution(778714249428914149)
XLA Ops:
  10.7 1.4 fusion.98
  12.2 0.9 pad_convert_fusion
  13.2 42.2 %all-gather.3.cloned.1.call-done = bf16[1024,2560]{1,0:T(8,128)(2,1)} async-done(((bf16[64,2560]{1,0:T(8,128)(2,1)}), bf16[1024,2560]{1,0:T(8,128)(2,1)}) %all-gather.3.cloned.1.call-update) | async-done | bytes 5242896 | tf_op jit(solution)/shard_map/all_gather | solution.py:83
  55.3 3.7 %fusion = f32[1024]{0:T(1024)S(1)} fusion(bf16[1024,2560]{1,0:T(8,128)(2,1)} %all-gather.3.cloned.1.call-done), kind=kLoop, calls=%fused_computation.2 | loop fusion | flops 7863296 | bytes 5246976 | tf_op jit(solution)/shard_map/reduce_sum | solution.py:52
  59.4 1.3 fusion.2
  60.7 2.3 negate_multiply_fusion
  64.6 5.0 %convolution_convert_fusion.2 = bf16[1024,320]{0,1:T(8,128)(2,1)S(1)} fusion(bf16[1024,2560]{1,0:T(8,128)(2,1)} %copy-done.1, bf16[2560,320]{0,1:T(8,128)(2,1)} %param.20), kind=kOutput, calls=%fused_computation.31 | convolution fusion | flops 1678049280 | bytes 7536640 | tf_op jit(solution)/shard_map/dot_general | solution.py:90
  69.8 1.6 convolution_convert_fusion.3
  71.5 3.4 %collective-permute-start = (bf16[3,576]{0,1:T(8,128)(2,1)S(1)}, bf16[3,576]{0,1:T(8,128)(2,1)S(1)}, u32[]{:S(2)}, u32[]{:S(2)}) collective-permute-start(bf16[3,576]{0,1:T(8,128)(2,1)S(1)} %pad_maximum_fusion.2), channel_id=1, source_target_pairs={{0,16},{16,32},{32,48},{48,64},{64,80},{80,96},{96,112},{112,128},... | collective-permute-start | bytes 10376 | tf_op jit(solution)/shard_map/ppermute | solution.py:18
  76.0 5.4 %collective-permute-done = bf16[3,576]{0,1:T(8,128)(2,1)S(1)} collective-permute-done((bf16[3,576]{0,1:T(8,128)(2,1)S(1)}, bf16[3,576]{0,1:T(8,128)(2,1)S(1)}, u32[]{:S(2)}, u32[]{:S(2)}) %collective-permute-start) | collective-permute-done | bytes 3488 | tf_op jit(solution)/shard_map/ppermute | solution.py:18
  82.1 2.4 fusion.54
  84.6 1.9 reshape.106
  87.2 1.1 multiply_convert_fusion.2
  88.4 0.9 reshape.102
  89.2 1.5 fusion.29
  93.2 1.9 collective-permute-start.1
  95.1 4.0 %collective-permute-start.2 = (f32[5,65,128]{2,1,0:T(8,128)}, f32[5,65,128]{2,1,0:T(8,128)}, u32[]{:S(2)}, u32[]{:S(2)}) collective-permute-start(f32[5,65,128]{2,1,0:T(8,128)} %pad_maximum_fusion), channel_id=1, source_target_pairs={{0,32},{16,48},{32,64},{48,80},{64,96},{80,112},{96,128},{112,144}... | collective-permute-start | bytes 499208 | tf_op jit(solution)/shard_map/ppermute | solution.py:23
  99.1 4.4 %collective-permute-start.3 = (f32[5,65,128]{2,1,0:T(8,128)}, f32[5,65,128]{2,1,0:T(8,128)}, u32[]{:S(2)}, u32[]{:S(2)}) collective-permute-start(f32[5,65,128]{2,1,0:T(8,128)} %pad_maximum_fusion), channel_id=1, source_target_pairs={{0,48},{16,64},{32,80},{48,96},{64,112},{80,128},{96,144},{112,160... | collective-permute-start | bytes 499208 | tf_op jit(solution)/shard_map/ppermute | solution.py:23
  103.9 4.4 %fusion.22 = f32[4,256,5,64]{1,3,2,0:T(8,128)} fusion(f32[4,256,5]{1,2,0:T(8,128)S(1)} %copy-done.12, f32[4,256,256]{2,1,0:T(8,128)S(1)} %fusion.59, pred[256,256]{1,0:T(8,128)(4,1)S(1)} %copy-done.13, f32[4,256,5,64]{1,0,3,2:T(4,128)S(1)} %reshape.106, f32[4,256,5]{1,2,0:T(8,128)S(1)} %bitcast.116), kind=kOutput, calls=%fused_computation.28 | convolution fusion | flops 508887040 | bytes 3776512 | tf_op jit(solution)/shard_map/btsh,bshp->bthp/dot_general | solution.py:114
  109.5 1.5 multiply_add_fusion
  111.1 3.3 collective-permute-start.5
  114.5 1.9 collective-permute-start.4
  117.4 5.9 %collective-permute-done.4 = f32[5,65,128]{2,1,0:T(8,128)S(1)} collective-permute-done((f32[5,65,128]{2,1,0:T(8,128)S(1)}, f32[5,65,128]{2,1,0:T(8,128)S(1)}, u32[]{:S(2)}, u32[]{:S(2)}) %collective-permute-start.4) | collective-permute-done | bytes 166432 | tf_op jit(solution)/shard_map/ppermute | solution.py:23
  126.6 2.1 multiply_convert_fusion
  128.9 5.2 %convolution_convert_fusion.1 = bf16[1024,2688]{1,0:T(8,128)(2,1)} fusion(bf16[320,2560]{1,0:T(8,128)(2,1)S(1)} %copy-done.31, bf16[128,2688]{1,0:T(8,128)(2,1)S(1)} %copy-done.6, bf16[1024,1]{0,1:T(2,128)(2,1)S(1)} %subtract_convert_fusion, bf16[1024,1]{0,1:T(2,128)(2,1)S(1)} %convert_element_type.116, bf16[1024,320]{0,1:T(8,128)(2,1)S(1)} %get-tuple-element.13, ...), kind=kOutput, calls=%fused_computation.6 | convolution fusion | flops 2479898624 | bytes 8491904 | tf_op jit(solution)/shard_map/dot_general | solution.py:162
  134.1 65.8 %reduce-scatter.7.cloned.1.call-done = bf16[64,2688]{1,0:T(8,128)(2,1)} async-done(((bf16[1024,2688]{1,0:T(8,128)(2,1)}), bf16[64,2688]{1,0:T(8,128)(2,1)}) %reduce-scatter.7.cloned.1.call-update) | async-done | bytes 344080 | tf_op jit(solution)/shard_map/reduce_scatter | solution.py:163
  201.0 1.4 fusion.41
  203.6 41.8 %all-gather.5.cloned.1.call-done = bf16[1024,2560]{1,0:T(8,128)(2,1)} async-done(((bf16[64,2560]{1,0:T(8,128)(2,1)}), bf16[1024,2560]{1,0:T(8,128)(2,1)}) %all-gather.5.cloned.1.call-update) | async-done | bytes 5242896 | tf_op jit(solution)/shard_map/all_gather | solution.py:171
  245.3 4.9 %fusion.99 = f32[1024,320]{0,1:T(8,128)S(1)} fusion(bf16[1024,2560]{1,0:T(8,128)(2,1)} %all-gather.5.cloned.1.call-done, bf16[2560,320]{0,1:T(8,128)(2,1)} %param.31), kind=kOutput, calls=%fused_computation.172 | convolution fusion | flops 1677721600 | bytes 8192000 | tf_op jit(solution)/shard_map/dot_general | solution.py:172
  250.2 10.0 %convolution_convert_fusion = bf16[1024,2560]{1,0:T(8,128)(2,1)} fusion(bf16[320,2560]{1,0:T(8,128)(2,1)S(1)} %copy-done, bf16[1024,2560]{1,0:T(8,128)(2,1)} %all-gather.5.cloned.1.call-done, bf16[2560,320]{0,1:T(8,128)(2,1)} %param.32, f32[1024,320]{0,1:T(8,128)S(1)} %fusion.99), kind=kOutput, calls=%fused_computation.5 | convolution fusion | flops 3360030720 | bytes 15073280 | tf_op jit(solution)/shard_map/dot_general | solution.py:177
  260.3 64.0 %reduce-scatter.9.cloned.1.call-done = bf16[64,2560]{1,0:T(8,128)(2,1)} async-done(((bf16[1024,2560]{1,0:T(8,128)(2,1)}), bf16[64,2560]{1,0:T(8,128)(2,1)}) %reduce-scatter.9.cloned.1.call-update) | async-done | bytes 327696 | tf_op jit(solution)/shard_map/reduce_scatter | solution.py:176
  324.2 1.8 fusion.44
  (145 shorter events, 19.4 us)
Async XLA Ops:
  6.5 243.7 %copy-start = (bf16[320,2560]{1,0:T(8,128)(2,1)S(1)}, bf16[320,2560]{1,0:T(8,128)(2,1)}, u32[]{:S(2)}) copy-start(bf16[320,2560]{1,0:T(8,128)(2,1)} %param.33) | copy-start | bytes 4915204
  6.5 48.8 %all-gather.3.cloned.1.call-start = ((), (), s32[]{:S(2)}) async-start(), calls=%async_computation.2 | async-start | bytes 5570560 | tf_op jit(solution)/shard_map/all_gather | solution.py:83
  7.3 192.7 %reduce-scatter.7.cloned.1.call-start = ((), (), s32[]{:S(2)}) async-start(), calls=%async_computation.4 | async-start | bytes 5849088 | tf_op jit(solution)/shard_map/reduce_scatter | solution.py:163
  13.2 45.9 %copy-start.15 = (f32[2560]{0:T(1024)S(1)}, f32[2560]{0:T(1024)}, u32[]{:S(2)}) copy-start(f32[2560]{0:T(1024)} %param.18) | copy-start | bytes 30724
  55.3 4.0 %copy-start.2 = (bf16[1024,2560]{1,0:T(8,128)(2,1)S(1)}, bf16[1024,2560]{1,0:T(8,128)(2,1)}, u32[]{:S(2)}) copy-start(bf16[1024,2560]{1,0:T(8,128)(2,1)} %all-gather.3.cloned.1.call-done) | copy-start | bytes 15728644
  60.7 2.3 copy-start.1
  63.0 6.7 %slice-start = ((s8[5242880]{0:T(1024)(128)(4,1)}), s8[1048576]{0:T(1024)(128)(4,1)S(1)}, s32[]{:S(2)}) async-start(s8[5242880]{0:T(1024)(128)(4,1)} %bitcast.105), calls=%async_computation.6 | async-start | bytes 2097152
  63.5 12.0 %copy-start.18 = (f32[5]{0:T(128)}, f32[5]{0:T(128)S(1)}, u32[]{:S(2)}) copy-start(f32[5]{0:T(128)S(1)} %get-tuple-element.5) | copy-start | bytes 64
  64.6 5.1 %slice-start.1 = ((s8[5242880]{0:T(1024)(128)(4,1)}), s8[4194304]{0:T(1024)(128)(4,1)S(1)}, s32[]{:S(2)}) async-start(s8[5242880]{0:T(1024)(128)(4,1)} %bitcast.105), calls=%async_computation.7 | async-start | bytes 8388608
  64.6 5.2 %copy-start.32 = (bf16[2560,256]{1,0:T(8,128)(2,1)S(1)}, bf16[2560,256]{1,0:T(8,128)(2,1)}, u32[]{:S(2)}) copy-start(bf16[2560,256]{1,0:T(8,128)(2,1)} %param.21) | copy-start | bytes 3932164
  71.5 10.0 %collective-permute-start = (bf16[3,576]{0,1:T(8,128)(2,1)S(1)}, bf16[3,576]{0,1:T(8,128)(2,1)S(1)}, u32[]{:S(2)}, u32[]{:S(2)}) collective-permute-start(bf16[3,576]{0,1:T(8,128)(2,1)S(1)} %pad_maximum_fusion.2), channel_id=1, source_target_pairs={{0,16},{16,32},{32,48},{48,64},{64,80},{80,96},{96,112},{112,128},... | collective-permute-start | bytes 10376 | tf_op jit(solution)/shard_map/ppermute | solution.py:18
  89.2 3.1 copy-start.19
  90.8 13.1 %copy-start.12 = (f32[4,256,5]{1,2,0:T(8,128)S(1)}, f32[4,256,5]{1,2,0:T(8,128)}, u32[]{:S(2)}) copy-start(f32[4,256,5]{1,2,0:T(8,128)} %copy-done.11) | copy-start | bytes 61444
  90.8 13.1 %copy-start.13 = (pred[256,256]{1,0:T(8,128)(4,1)S(1)}, pred[256,256]{1,0:T(8,128)(4,1)}, u32[]{:S(2)}) copy-start(pred[256,256]{1,0:T(8,128)(4,1)} %iota_compare_fusion.1) | copy-start | bytes 196612
  93.2 15.4 %collective-permute-start.1 = (f32[5,65,128]{2,1,0:T(8,128)}, f32[5,65,128]{2,1,0:T(8,128)}, u32[]{:S(2)}, u32[]{:S(2)}) collective-permute-start(f32[5,65,128]{2,1,0:T(8,128)} %pad_maximum_fusion), channel_id=1, source_target_pairs={{0,16},{16,32},{32,48},{48,64},{64,80},{80,96},{96,112},{112,128},... | collective-permute-start | bytes 499208 | tf_op jit(solution)/shard_map/ppermute | solution.py:23
  95.1 13.5 %collective-permute-start.2 = (f32[5,65,128]{2,1,0:T(8,128)}, f32[5,65,128]{2,1,0:T(8,128)}, u32[]{:S(2)}, u32[]{:S(2)}) collective-permute-start(f32[5,65,128]{2,1,0:T(8,128)} %pad_maximum_fusion), channel_id=1, source_target_pairs={{0,32},{16,48},{32,64},{48,80},{64,96},{80,112},{96,128},{112,144}... | collective-permute-start | bytes 499208 | tf_op jit(solution)/shard_map/ppermute | solution.py:23
  99.1 9.5 %collective-permute-start.3 = (f32[5,65,128]{2,1,0:T(8,128)}, f32[5,65,128]{2,1,0:T(8,128)}, u32[]{:S(2)}, u32[]{:S(2)}) collective-permute-start(f32[5,65,128]{2,1,0:T(8,128)} %pad_maximum_fusion), channel_id=1, source_target_pairs={{0,48},{16,64},{32,80},{48,96},{64,112},{80,128},{96,144},{112,160... | collective-permute-start | bytes 499208 | tf_op jit(solution)/shard_map/ppermute | solution.py:23
  103.9 5.5 %copy-start.20 = (f32[5]{0:T(128)S(1)}, f32[5]{0:T(128)}, u32[]{:S(2)}) copy-start(f32[5]{0:T(128)} %copy-done.18) | copy-start | bytes 64
  103.9 5.6 %copy-start.17 = (f32[5]{0:T(128)S(1)}, f32[5]{0:T(128)}, u32[]{:S(2)}) copy-start(f32[5]{0:T(128)} %get-tuple-element.36) | copy-start | bytes 64
  103.9 5.6 %copy-start.29 = (f32[5]{0:T(128)S(1)}, f32[5]{0:T(128)}, u32[]{:S(2)}) copy-start(f32[5]{0:T(128)} %exp.74) | copy-start | bytes 64
  108.5 5.8 %copy-start.4 = (f32[4,5,64,128]{3,2,1,0:T(8,128)S(1)}, f32[4,5,64,128]{3,2,1,0:T(8,128)}, u32[]{:S(2)}) copy-start(f32[4,5,64,128]{3,2,1,0:T(8,128)} %copy-done.3) | copy-start | bytes 1966084
  111.0 12.5 %copy-start.5 = (f32[4,256,5,64]{1,3,2,0:T(8,128)S(1)}, f32[4,256,5,64]{1,3,2,0:T(8,128)}, u32[]{:S(2)}) copy-start(f32[4,256,5,64]{1,3,2,0:T(8,128)} %fusion.22) | copy-start | bytes 3932164
  111.0 12.5 %copy-start.9 = (f32[4,256,5]{1,2,0:T(8,128)S(1)}, f32[4,256,5]{1,2,0:T(8,128)}, u32[]{:S(2)}) copy-start(f32[4,256,5]{1,2,0:T(8,128)} %get-tuple-element.28) | copy-start | bytes 61444
  111.0 12.5 %copy-start.27 = (f32[5]{0:T(128)S(1)}, f32[5]{0:T(128)}, u32[]{:S(2)}) copy-start(f32[5]{0:T(128)} %param.27) | copy-start | bytes 64
  111.0 12.5 %copy-start.28 = (f32[4]{0:T(128)S(1)}, f32[4]{0:T(128)}, u32[]{:S(2)}) copy-start(f32[4]{0:T(128)} %pad.17.clone) | copy-start | bytes 52
  111.1 6.3 %collective-permute-start.5 = (f32[5,65,128]{2,1,0:T(8,128)S(1)}, f32[5,65,128]{2,1,0:T(8,128)S(1)}, u32[]{:S(2)}, u32[]{:S(2)}) collective-permute-start(f32[5,65,128]{2,1,0:T(8,128)S(1)} %pad_maximum_fusion.1), channel_id=1, source_target_pairs={{0,128},{16,144},{32,160},{48,176},{64,192},{80,208},{96,224},{112... | collective-permute-start | bytes 499208 | tf_op jit(solution)/shard_map/ppermute | solution.py:23
  114.5 8.8 %collective-permute-start.4 = (f32[5,65,128]{2,1,0:T(8,128)S(1)}, f32[5,65,128]{2,1,0:T(8,128)S(1)}, u32[]{:S(2)}, u32[]{:S(2)}) collective-permute-start(f32[5,65,128]{2,1,0:T(8,128)S(1)} %pad_maximum_fusion.1), channel_id=1, source_target_pairs={{0,64},{16,80},{32,96},{48,112},{64,128},{80,144},{96,160},{112,17... | collective-permute-start | bytes 499208 | tf_op jit(solution)/shard_map/ppermute | solution.py:23
  116.4 6.9 %collective-permute-start.6 = (f32[5,65,128]{2,1,0:T(8,128)S(1)}, f32[5,65,128]{2,1,0:T(8,128)S(1)}, u32[]{:S(2)}, u32[]{:S(2)}) collective-permute-start(f32[5,65,128]{2,1,0:T(8,128)S(1)} %pad_maximum_fusion.1), channel_id=1, source_target_pairs={{0,192},{16,208},{32,224},{48,240},{1,193},{17,209},{33,225},{49,2... | collective-permute-start | bytes 499208 | tf_op jit(solution)/shard_map/ppermute | solution.py:23
  123.5 2.4 slice-start.3
  134.1 68.3 %copy-start.16 = (f32[2560]{0:T(1024)S(1)}, f32[2560]{0:T(1024)}, u32[]{:S(2)}) copy-start(f32[2560]{0:T(1024)} %param.30) | copy-start | bytes 30724
  134.1 111.2 %all-gather.5.cloned.1.call-start = ((), (), s32[]{:S(2)}) async-start(), calls=%async_computation.3 | async-start | bytes 5570560 | tf_op jit(solution)/shard_map/all_gather | solution.py:171
  203.3 120.9 %reduce-scatter.9.cloned.1.call-start = ((), (), s32[]{:S(2)}) async-start(), calls=%async_computation.5 | async-start | bytes 5570560 | tf_op jit(solution)/shard_map/reduce_scatter | solution.py:176
  (18 other events, 22.9 us)
Sparse Core Ops, SparseCore 0:
  9.2 46.1 all-gather.2
  134.2 65.6 reduce-scatter.6
  203.4 41.8 all-gather.4
  260.4 63.7 reduce-scatter.8

commit v11 on v10

--- a/solution.py
+++ b/solution.py
@@ -80,8 +80,22 @@
     w_up,
     w_down,
 ):
-    gathered = lax.all_gather(tokens, "tp", axis=0, tiled=True)
-    normed = rms_rows(gathered, norm1_gain).astype(jnp.bfloat16)
+    wide = tokens.astype(jnp.float32)
+    own_scale = lax.rsqrt(jnp.mean(wide * wide, axis=-1) + EPS)
+    scale_top = lax.reduce_precision(own_scale, exponent_bits=8, mantissa_bits=7)
+    scale_hi = scale_top.astype(jnp.bfloat16)
+    scale_lo = (own_scale - scale_top).astype(jnp.bfloat16)
+    width_in = tokens.shape[1]
+    payload = jnp.concatenate(
+        [tokens, scale_hi[:, None], scale_lo[:, None], jnp.zeros((tokens.shape[0], 126), jnp.bfloat16)],
+        axis=1,
+    )
+    gathered_all = lax.all_gather(payload, "tp", axis=0, tiled=True)
+    gathered = gathered_all[:, :width_in]
+    row_scale = gathered_all[:, width_in].astype(jnp.float32) + gathered_all[:, width_in + 1].astype(
+        jnp.float32
+    )
+    normed = (gathered.astype(jnp.float32) * row_scale[:, None] * norm1_gain).astype(jnp.bfloat16)
     bc_rows = jnp.dot(normed, w_bc, preferred_element_type=jnp.float32).astype(jnp.bfloat16)
     group_len = gathered.shape[0]
     head_count = w_dt.shape[1]
@@ -165,7 +179,8 @@
     scale = lax.rsqrt(squares_own / (HEADS * HEAD_DIM) + EPS)
     mixer_own = reduced[:, :width].astype(jnp.float32) * scale[:, None]
     own_rows = tokens.shape[0]
-    own_tokens = lax.dynamic_slice_in_dim(gathered, lax.axis_index("tp") * own_rows, own_rows, 0)
+    own_tokens = lax.dynamic_slice_in_dim(gathered_all, lax.axis_index("tp") * own_rows, own_rows, 0)
+    own_tokens = own_tokens[:, :width_in]
     resid = (own_tokens.astype(jnp.float32) + mixer_own).astype(jnp.bfloat16)
     normed_own = rms_rows(resid, norm2_gain).astype(jnp.bfloat16)
     mlp_in = lax.all_gather(normed_own, "tp", axis=0, tiled=True)

time: 333 us -> 335 us (level)
    reduce_sum x2 -> x1, other arithmetic: 5.12 us -> 1.4 us  [rms_rows(): jnp.mean(wide * wide, axis=-1, keepdims=True) + EPS]
  transfers between devices with their start and end apart: 11 -> 11, of which waited for: 7 -> 7; matrix products, arithmetic and copies ran while one was open for 4% -> 3% of each run, Pallas kernels for 0% -> 0%
where the time goes in v11:
time: 335 us; the launch traced here: 334 us
  waiting for transfers between devices  225 us (67%)
  matrix products  38.5 us (11%)
  other arithmetic  21.9 us (7%)
  starting transfers between devices  20 us (6%)
  local copies, waits for them, and re-layouts  14.6 us (4%)
  between operations  13.9 us (4%)
    reduce_scatter x1, waiting for transfers between devices, local(): reduced = lax.psum_scatter(product, 'tp', scatter_dimension=0, tiled=True)  66 us
    reduce_scatter x1, waiting for transfers between devices, local(): lax.psum_scatter(jnp.dot(piece, w_down, preferred_element_type=jnp.float3...  64 us
    all_gather x1, waiting for transfers between devices, local(): mlp_in = lax.all_gather(normed_own, 'tp', axis=0, tiled=True)  41.8 us
    all_gather x1, waiting for transfers between devices, local(): gathered_all = lax.all_gather(payload, 'tp', axis=0, tiled=True)  41.7 us
    ppermute x6, starting transfers between devices, shifted(): lax.ppermute(value, axis, [(source, source + steps) for source in range(c...  16.2 us
    dot_general x1, matrix products, local(): jnp.dot(piece, w_down, preferred_element_type=jnp.float32)  10 us
  transfers between devices with their start and end apart: 11, of which 7 were waited for; matrix products, arithmetic and copies ran while one was open for 3% of the time, Pallas kernels for 0%

profile of v11, /device:TPU:2, one launch (start us, length us, event | category | flops | bytes accessed | tf_op | source)
XLA Modules:
  0.0 334.1 jit_solution(8875514941468628145)
XLA Ops:
  6.5 1.3 multiply_reduce_fusion.1
  8.1 1.8 concatenate.29
  14.0 0.9 pad_convert_fusion
  14.9 41.7 %all-gather.3.cloned.1.call-done = bf16[1024,2688]{1,0:T(8,128)(2,1)} async-done(((bf16[64,2688]{1,0:T(8,128)(2,1)}), bf16[1024,2688]{1,0:T(8,128)(2,1)}) %all-gather.3.cloned.1.call-update) | async-done | bytes 5505040 | tf_op jit(solution)/shard_map/all_gather | solution.py:93
  56.7 1.4 add_reduce_fusion
  58.1 3.7 %multiply_convert_fusion = bf16[1024,2560]{1,0:T(8,128)(2,1)S(1)} fusion(bf16[1024,2688]{1,0:T(8,128)(2,1)} %all-gather.3.cloned.1.call-done, f32[2560]{0:T(1024)S(1)} %copy-done.14, f32[1024]{0:T(1024)S(1)} %add_reduce_fusion), kind=kLoop, calls=%fused_computation | loop fusion | flops 10485760 | bytes 10500096 | tf_op jit(solution)/shard_map/convert_element_type | solution.py:98
  61.9 2.3 negate_multiply_fusion
  65.8 5.0 %convolution_convert_fusion.2 = bf16[1024,320]{0,1:T(8,128)(2,1)S(1)} fusion(bf16[1024,2560]{1,0:T(8,128)(2,1)} %copy-done.1, bf16[2560,320]{0,1:T(8,128)(2,1)} %param.20), kind=kOutput, calls=%fused_computation.27 | convolution fusion | flops 1678049280 | bytes 7536640 | tf_op jit(solution)/shard_map/dot_general | solution.py:104
  71.0 1.6 convolution_convert_fusion.3
  72.7 3.4 %collective-permute-start = (bf16[3,576]{0,1:T(8,128)(2,1)S(1)}, bf16[3,576]{0,1:T(8,128)(2,1)S(1)}, u32[]{:S(2)}, u32[]{:S(2)}) collective-permute-start(bf16[3,576]{0,1:T(8,128)(2,1)S(1)} %pad_maximum_fusion.2), channel_id=1, source_target_pairs={{0,16},{16,32},{32,48},{48,64},{64,80},{80,96},{96,112},{112,128},... | collective-permute-start | bytes 10376 | tf_op jit(solution)/shard_map/ppermute | solution.py:18
  77.2 5.5 %collective-permute-done = bf16[3,576]{0,1:T(8,128)(2,1)S(1)} collective-permute-done((bf16[3,576]{0,1:T(8,128)(2,1)S(1)}, bf16[3,576]{0,1:T(8,128)(2,1)S(1)}, u32[]{:S(2)}, u32[]{:S(2)}) %collective-permute-start) | collective-permute-done | bytes 3488 | tf_op jit(solution)/shard_map/ppermute | solution.py:18
  83.4 2.4 fusion.51
  85.8 1.9 reshape.132
  88.4 1.1 multiply_convert_fusion.3
  90.5 1.5 fusion.26
  94.4 1.9 collective-permute-start.1
  96.3 4.0 %collective-permute-start.2 = (f32[5,65,128]{2,1,0:T(8,128)}, f32[5,65,128]{2,1,0:T(8,128)}, u32[]{:S(2)}, u32[]{:S(2)}) collective-permute-start(f32[5,65,128]{2,1,0:T(8,128)} %pad_maximum_fusion), channel_id=1, source_target_pairs={{0,32},{16,48},{32,64},{48,80},{64,96},{80,112},{96,128},{112,144}... | collective-permute-start | bytes 499208 | tf_op jit(solution)/shard_map/ppermute | solution.py:23
  100.4 4.4 %collective-permute-start.3 = (f32[5,65,128]{2,1,0:T(8,128)}, f32[5,65,128]{2,1,0:T(8,128)}, u32[]{:S(2)}, u32[]{:S(2)}) collective-permute-start(f32[5,65,128]{2,1,0:T(8,128)} %pad_maximum_fusion), channel_id=1, source_target_pairs={{0,48},{16,64},{32,80},{48,96},{64,112},{80,128},{96,144},{112,160... | collective-permute-start | bytes 499208 | tf_op jit(solution)/shard_map/ppermute | solution.py:23
  105.2 4.4 %fusion.19 = f32[4,256,5,64]{1,3,2,0:T(8,128)} fusion(f32[4,256,5]{1,2,0:T(8,128)S(1)} %copy-done.11, f32[4,256,256]{2,1,0:T(8,128)S(1)} %fusion.56, pred[256,256]{1,0:T(8,128)(4,1)S(1)} %copy-done.12, f32[4,256,5,64]{1,0,3,2:T(4,128)S(1)} %reshape.132, f32[4,256,5]{1,2,0:T(8,128)S(1)} %bitcast.119), kind=kOutput, calls=%fused_computation.24 | convolution fusion | flops 508887040 | bytes 3776512 | tf_op jit(solution)/shard_map/btsh,bshp->bthp/dot_general | solution.py:128
  110.8 1.5 multiply_add_fusion
  112.3 3.3 collective-permute-start.5
  115.7 1.9 collective-permute-start.4
  118.7 5.9 %collective-permute-done.4 = f32[5,65,128]{2,1,0:T(8,128)S(1)} collective-permute-done((f32[5,65,128]{2,1,0:T(8,128)S(1)}, f32[5,65,128]{2,1,0:T(8,128)S(1)}, u32[]{:S(2)}, u32[]{:S(2)}) %collective-permute-start.4) | collective-permute-done | bytes 166432 | tf_op jit(solution)/shard_map/ppermute | solution.py:23
  127.9 2.1 multiply_convert_fusion.1
  130.2 5.2 %convolution_convert_fusion.1 = bf16[1024,2688]{1,0:T(8,128)(2,1)} fusion(bf16[320,2560]{1,0:T(8,128)(2,1)S(1)} %copy-done.31, bf16[128,2688]{1,0:T(8,128)(2,1)S(1)} %copy-done.5, bf16[1024,1]{0,1:T(2,128)(2,1)S(1)} %subtract_convert_fusion, bf16[1024,1]{0,1:T(2,128)(2,1)S(1)} %convert_element_type.152, bf16[1024,320]{0,1:T(8,128)(2,1)S(1)} %get-tuple-element.13, ...), kind=kOutput, calls=%fused_computation.2 | convolution fusion | flops 2479898624 | bytes 8491904 | tf_op jit(solution)/shard_map/dot_general | solution.py:176
  135.5 66.0 %reduce-scatter.7.cloned.1.call-done = bf16[64,2688]{1,0:T(8,128)(2,1)} async-done(((bf16[1024,2688]{1,0:T(8,128)(2,1)}), bf16[64,2688]{1,0:T(8,128)(2,1)}) %reduce-scatter.7.cloned.1.call-update) | async-done | bytes 344080 | tf_op jit(solution)/shard_map/reduce_scatter | solution.py:177
  202.5 1.4 fusion.38
  205.1 41.8 %all-gather.5.cloned.1.call-done = bf16[1024,2560]{1,0:T(8,128)(2,1)} async-done(((bf16[64,2560]{1,0:T(8,128)(2,1)}), bf16[1024,2560]{1,0:T(8,128)(2,1)}) %all-gather.5.cloned.1.call-update) | async-done | bytes 5242896 | tf_op jit(solution)/shard_map/all_gather | solution.py:186
  246.9 4.9 %fusion.97 = f32[1024,320]{0,1:T(8,128)S(1)} fusion(bf16[1024,2560]{1,0:T(8,128)(2,1)} %all-gather.5.cloned.1.call-done, bf16[2560,320]{0,1:T(8,128)(2,1)} %param.31), kind=kOutput, calls=%fused_computation.173 | convolution fusion | flops 1677721600 | bytes 8192000 | tf_op jit(solution)/shard_map/dot_general | solution.py:187
  251.8 10.0 %convolution_convert_fusion = bf16[1024,2560]{1,0:T(8,128)(2,1)} fusion(bf16[320,2560]{1,0:T(8,128)(2,1)S(1)} %copy-done, bf16[1024,2560]{1,0:T(8,128)(2,1)} %all-gather.5.cloned.1.call-done, bf16[2560,320]{0,1:T(8,128)(2,1)} %param.32, f32[1024,320]{0,1:T(8,128)S(1)} %fusion.97), kind=kOutput, calls=%fused_computation.1 | convolution fusion | flops 3360030720 | bytes 15073280 | tf_op jit(solution)/shard_map/dot_general | solution.py:192
  261.8 64.0 %reduce-scatter.9.cloned.1.call-done = bf16[64,2560]{1,0:T(8,128)(2,1)} async-done(((bf16[1024,2560]{1,0:T(8,128)(2,1)}), bf16[64,2560]{1,0:T(8,128)(2,1)}) %reduce-scatter.9.cloned.1.call-update) | async-done | bytes 327696 | tf_op jit(solution)/shard_map/reduce_scatter | solution.py:191
  325.8 1.8 fusion.41
  (150 shorter events, 20.1 us)
Async XLA Ops:
  6.5 245.2 %copy-start = (bf16[320,2560]{1,0:T(8,128)(2,1)S(1)}, bf16[320,2560]{1,0:T(8,128)(2,1)}, u32[]{:S(2)}) copy-start(bf16[320,2560]{1,0:T(8,128)(2,1)} %param.33) | copy-start | bytes 4915204
  6.5 6.8 %copy-start.20 = (f32[4,256]{1,0:T(4,128)S(1)}, f32[4,256]{1,0:T(4,128)}, u32[]{:S(2)}) copy-start(f32[4,256]{1,0:T(4,128)} %param.26) | copy-start | bytes 12292
  6.5 51.5 %copy-start.14 = (f32[2560]{0:T(1024)S(1)}, f32[2560]{0:T(1024)}, u32[]{:S(2)}) copy-start(f32[2560]{0:T(1024)} %param.18) | copy-start | bytes 30724
  6.5 50.1 %all-gather.3.cloned.1.call-start = ((), (), s32[]{:S(2)}) async-start(), calls=%async_computation.2 | async-start | bytes 5849088 | tf_op jit(solution)/shard_map/all_gather | solution.py:93
  9.9 191.6 %reduce-scatter.7.cloned.1.call-start = ((), (), s32[]{:S(2)}) async-start(), calls=%async_computation.4 | async-start | bytes 5849088 | tf_op jit(solution)/shard_map/reduce_scatter | solution.py:177
  58.0 3.8 %copy-start.13 = (bf16[2560,5]{0,1:T(8,128)(2,1)S(1)}, bf16[2560,5]{0,1:T(8,128)(2,1)}, u32[]{:S(2)}) copy-start(bf16[2560,5]{0,1:T(8,128)(2,1)} %param.22) | copy-start | bytes 76804
  58.1 3.8 %copy-start.25 = (f32[5]{0:T(128)S(1)}, f32[5]{0:T(128)}, u32[]{:S(2)}) copy-start(f32[5]{0:T(128)} %param.23) | copy-start | bytes 64
  64.2 6.7 %slice-start = ((s8[5242880]{0:T(1024)(128)(4,1)}), s8[1048576]{0:T(1024)(128)(4,1)S(1)}, s32[]{:S(2)}) async-start(s8[5242880]{0:T(1024)(128)(4,1)} %bitcast.108), calls=%async_computation.6 | async-start | bytes 2097152
  64.7 12.0 %copy-start.17 = (f32[5]{0:T(128)}, f32[5]{0:T(128)S(1)}, u32[]{:S(2)}) copy-start(f32[5]{0:T(128)S(1)} %get-tuple-element.5) | copy-start | bytes 64
  65.8 5.1 %slice-start.1 = ((s8[5242880]{0:T(1024)(128)(4,1)}), s8[4194304]{0:T(1024)(128)(4,1)S(1)}, s32[]{:S(2)}) async-start(s8[5242880]{0:T(1024)(128)(4,1)} %bitcast.108), calls=%async_computation.7 | async-start | bytes 8388608
  65.8 5.2 %copy-start.32 = (bf16[2560,256]{1,0:T(8,128)(2,1)S(1)}, bf16[2560,256]{1,0:T(8,128)(2,1)}, u32[]{:S(2)}) copy-start(bf16[2560,256]{1,0:T(8,128)(2,1)} %param.21) | copy-start | bytes 3932164
  72.7 10.0 %collective-permute-start = (bf16[3,576]{0,1:T(8,128)(2,1)S(1)}, bf16[3,576]{0,1:T(8,128)(2,1)S(1)}, u32[]{:S(2)}, u32[]{:S(2)}) collective-permute-start(bf16[3,576]{0,1:T(8,128)(2,1)S(1)} %pad_maximum_fusion.2), channel_id=1, source_target_pairs={{0,16},{16,32},{32,48},{48,64},{64,80},{80,96},{96,112},{112,128},... | collective-permute-start | bytes 10376 | tf_op jit(solution)/shard_map/ppermute | solution.py:18
  90.5 3.2 copy-start.18
  92.0 13.1 %copy-start.11 = (f32[4,256,5]{1,2,0:T(8,128)S(1)}, f32[4,256,5]{1,2,0:T(8,128)}, u32[]{:S(2)}) copy-start(f32[4,256,5]{1,2,0:T(8,128)} %copy-done.10) | copy-start | bytes 61444
  92.0 13.1 %copy-start.12 = (pred[256,256]{1,0:T(8,128)(4,1)S(1)}, pred[256,256]{1,0:T(8,128)(4,1)}, u32[]{:S(2)}) copy-start(pred[256,256]{1,0:T(8,128)(4,1)} %iota_compare_fusion.1) | copy-start | bytes 196612
  94.4 15.4 %collective-permute-start.1 = (f32[5,65,128]{2,1,0:T(8,128)}, f32[5,65,128]{2,1,0:T(8,128)}, u32[]{:S(2)}, u32[]{:S(2)}) collective-permute-start(f32[5,65,128]{2,1,0:T(8,128)} %pad_maximum_fusion), channel_id=1, source_target_pairs={{0,16},{16,32},{32,48},{48,64},{64,80},{80,96},{96,112},{112,128},... | collective-permute-start | bytes 499208 | tf_op jit(solution)/shard_map/ppermute | solution.py:23
  96.3 13.5 %collective-permute-start.2 = (f32[5,65,128]{2,1,0:T(8,128)}, f32[5,65,128]{2,1,0:T(8,128)}, u32[]{:S(2)}, u32[]{:S(2)}) collective-permute-start(f32[5,65,128]{2,1,0:T(8,128)} %pad_maximum_fusion), channel_id=1, source_target_pairs={{0,32},{16,48},{32,64},{48,80},{64,96},{80,112},{96,128},{112,144}... | collective-permute-start | bytes 499208 | tf_op jit(solution)/shard_map/ppermute | solution.py:23
  100.4 9.5 %collective-permute-start.3 = (f32[5,65,128]{2,1,0:T(8,128)}, f32[5,65,128]{2,1,0:T(8,128)}, u32[]{:S(2)}, u32[]{:S(2)}) collective-permute-start(f32[5,65,128]{2,1,0:T(8,128)} %pad_maximum_fusion), channel_id=1, source_target_pairs={{0,48},{16,64},{32,80},{48,96},{64,112},{80,128},{96,144},{112,160... | collective-permute-start | bytes 499208 | tf_op jit(solution)/shard_map/ppermute | solution.py:23
  105.2 5.5 %copy-start.19 = (f32[5]{0:T(128)S(1)}, f32[5]{0:T(128)}, u32[]{:S(2)}) copy-start(f32[5]{0:T(128)} %copy-done.17) | copy-start | bytes 64
  105.2 5.6 %copy-start.16 = (f32[5]{0:T(128)S(1)}, f32[5]{0:T(128)}, u32[]{:S(2)}) copy-start(f32[5]{0:T(128)} %get-tuple-element.36) | copy-start | bytes 64
  105.2 5.6 %copy-start.29 = (f32[5]{0:T(128)S(1)}, f32[5]{0:T(128)}, u32[]{:S(2)}) copy-start(f32[5]{0:T(128)} %exp.74) | copy-start | bytes 64
  109.8 5.8 %copy-start.3 = (f32[4,5,64,128]{3,2,1,0:T(8,128)S(1)}, f32[4,5,64,128]{3,2,1,0:T(8,128)}, u32[]{:S(2)}) copy-start(f32[4,5,64,128]{3,2,1,0:T(8,128)} %copy-done.2) | copy-start | bytes 1966084
  112.3 12.5 %copy-start.4 = (f32[4,256,5,64]{1,3,2,0:T(8,128)S(1)}, f32[4,256,5,64]{1,3,2,0:T(8,128)}, u32[]{:S(2)}) copy-start(f32[4,256,5,64]{1,3,2,0:T(8,128)} %fusion.19) | copy-start | bytes 3932164
  112.3 12.5 %copy-start.8 = (f32[4,256,5]{1,2,0:T(8,128)S(1)}, f32[4,256,5]{1,2,0:T(8,128)}, u32[]{:S(2)}) copy-start(f32[4,256,5]{1,2,0:T(8,128)} %get-tuple-element.28) | copy-start | bytes 61444
  112.3 12.5 %copy-start.27 = (f32[5]{0:T(128)S(1)}, f32[5]{0:T(128)}, u32[]{:S(2)}) copy-start(f32[5]{0:T(128)} %param.27) | copy-start | bytes 64
  112.3 12.5 %copy-start.28 = (f32[4]{0:T(128)S(1)}, f32[4]{0:T(128)}, u32[]{:S(2)}) copy-start(f32[4]{0:T(128)} %pad.17.clone) | copy-start | bytes 52
  112.3 6.3 %collective-permute-start.5 = (f32[5,65,128]{2,1,0:T(8,128)S(1)}, f32[5,65,128]{2,1,0:T(8,128)S(1)}, u32[]{:S(2)}, u32[]{:S(2)}) collective-permute-start(f32[5,65,128]{2,1,0:T(8,128)S(1)} %pad_maximum_fusion.1), channel_id=1, source_target_pairs={{0,128},{16,144},{32,160},{48,176},{64,192},{80,208},{96,224},{112... | collective-permute-start | bytes 499208 | tf_op jit(solution)/shard_map/ppermute | solution.py:23
  115.7 8.9 %collective-permute-start.4 = (f32[5,65,128]{2,1,0:T(8,128)S(1)}, f32[5,65,128]{2,1,0:T(8,128)S(1)}, u32[]{:S(2)}, u32[]{:S(2)}) collective-permute-start(f32[5,65,128]{2,1,0:T(8,128)S(1)} %pad_maximum_fusion.1), channel_id=1, source_target_pairs={{0,64},{16,80},{32,96},{48,112},{64,128},{80,144},{96,160},{112,17... | collective-permute-start | bytes 499208 | tf_op jit(solution)/shard_map/ppermute | solution.py:23
  117.7 7.0 %collective-permute-start.6 = (f32[5,65,128]{2,1,0:T(8,128)S(1)}, f32[5,65,128]{2,1,0:T(8,128)S(1)}, u32[]{:S(2)}, u32[]{:S(2)}) collective-permute-start(f32[5,65,128]{2,1,0:T(8,128)S(1)} %pad_maximum_fusion.1), channel_id=1, source_target_pairs={{0,192},{16,208},{32,224},{48,240},{1,193},{17,209},{33,225},{49,2... | collective-permute-start | bytes 499208 | tf_op jit(solution)/shard_map/ppermute | solution.py:23
  135.4 68.5 %copy-start.15 = (f32[2560]{0:T(1024)S(1)}, f32[2560]{0:T(1024)}, u32[]{:S(2)}) copy-start(f32[2560]{0:T(1024)} %param.30) | copy-start | bytes 30724
  135.4 111.5 %all-gather.5.cloned.1.call-start = ((), (), s32[]{:S(2)}) async-start(), calls=%async_computation.3 | async-start | bytes 5570560 | tf_op jit(solution)/shard_map/all_gather | solution.py:186
  204.8 121.0 %reduce-scatter.9.cloned.1.call-start = ((), (), s32[]{:S(2)}) async-start(), calls=%async_computation.5 | async-start | bytes 5570560 | tf_op jit(solution)/shard_map/reduce_scatter | solution.py:191
  (18 other events, 25.2 us)
Sparse Core Ops, SparseCore 0:
  10.0 46.6 all-gather.2
  135.5 65.8 reduce-scatter.6
  204.9 41.9 all-gather.4
  261.9 63.8 reduce-scatter.8
